TPU v7x, 512 devices: a whole 4x4x16 slice. The times are simulated.
512 devices in a mesh: dom: 16 (over x_hi, y, core), band: 32 (over z, x_lo).
Axes of the slice: x: 4 (x_hi: 2, x_lo: 2; x = x_hi * 2 + x_lo), y: 4, z: 16, core: 2. Of those that a mesh axis runs over, the one named last changes fastest.
Arguments:
- psi: float32 [1024, 192, 2, 384], P('band', 'dom'), may hold values from -6 to 6
- potential: float32 [192, 2, 384], P('dom'), may hold values from -3 to 3
- rotation: bfloat16 [1024, 1024], replicated, may hold values from -0.1875 to 0.1875
Outputs:
- rotated: bfloat16 [1024, 192, 2, 384], P('band', 'dom')
All inputs are finite; a program needn't handle non-finite values.
Results may differ from a plain program's by a relative error of at most 0.005.
Values may be sent and summed in bfloat16 or wider, within the bound.
No kernel may reach another device: no remote copies, remote signals or barrier semaphores. Data moves between devices by JAX's collectives and lax.ppermute only.
A program may use at most 128 MiB of HBM per device.

v0:
```python
import jax
import jax.numpy as jnp
from jax import lax
from jax.experimental import pallas as pl
from jax.experimental.pallas import tpu as pltpu
from jax.sharding import PartitionSpec as P

coeffs = (
    -5369.0 / 1800.0,
    12.0 / 7.0,
    -15.0 / 56.0,
    10.0 / 189.0,
    -1.0 / 112.0,
    2.0 / 1925.0,
    -1.0 / 16632.0,
)
center_shift = 32.5
half_width = 27.5
reach = 6
state_block = 8


def rim_rows(rows):
    count = lax.axis_size("dom")
    halo = 2 * reach
    head = rows[:, :halo]
    tail = rows[:, rows.shape[1] - halo :]
    left = lax.ppermute(tail, "dom", [(i, (i + 1) % count) for i in range(count)])
    right = lax.ppermute(head, "dom", [((i + 1) % count, i) for i in range(count)])
    return jnp.concatenate([left, rows, right], axis=1)


def ham_rows(ext_ref, pot, s, rows, ny):
    halo = 2 * reach
    mid = ext_ref[s, pl.ds(halo, rows), :]
    lap = (3.0 * coeffs[0]) * mid
    for k in range(1, 7):
        lap = lap + coeffs[k] * (
            ext_ref[s, pl.ds(halo + 2 * k, rows), :] + ext_ref[s, pl.ds(halo - 2 * k, rows), :]
        )
    for k in range(1, 7):
        lap = lap + coeffs[k] * (pltpu.roll(mid, k, 1) + pltpu.roll(mid, ny - k, 1))
    up = ext_ref[s, pl.ds(halo + 1, rows), :]
    down = ext_ref[s, pl.ds(halo - 1, rows), :]
    even = lax.broadcasted_iota(jnp.int32, (rows, ny), 0) % 2 == 0
    lap = lap + coeffs[1] * jnp.where(even, up, down)
    return -2.0 * lap + pot * mid, mid


def first_kernel(ext_ref, pot_ref, out_ref):
    rows, ny = out_ref.shape[1], out_ref.shape[2]
    pot = pot_ref[...]

    def body(s, carry):
        h, mid = ham_rows(ext_ref, pot, s, rows, ny)
        out_ref[s] = (h - center_shift * mid) / half_width
        return carry

    lax.fori_loop(0, out_ref.shape[0], body, 0)


def second_kernel(ext_ref, psi_ref, pot_ref, out_ref):
    rows, ny = out_ref.shape[1], out_ref.shape[2]
    pot = pot_ref[...]

    def body(s, carry):
        h, mid = ham_rows(ext_ref, pot, s, rows, ny)
        second = 2.0 / half_width * (h - center_shift * mid) - psi_ref[s]
        out_ref[s] = second.astype(out_ref.dtype)
        return carry

    lax.fori_loop(0, out_ref.shape[0], body, 0)


def run_first(ext, pot):
    states, ext_rows, ny = ext.shape
    rows = pot.shape[0]
    sb = state_block
    return pl.pallas_call(
        first_kernel,
        grid=(states // sb,),
        in_specs=[
            pl.BlockSpec((sb, ext_rows, ny), lambda i: (i, 0, 0)),
            pl.BlockSpec((rows, ny), lambda i: (0, 0)),
        ],
        out_specs=pl.BlockSpec((sb, rows, ny), lambda i: (i, 0, 0)),
        out_shape=jax.ShapeDtypeStruct((states, rows, ny), jnp.float32),
    )(ext, pot)


def run_second(ext, psi, pot):
    states, ext_rows, ny = ext.shape
    rows = pot.shape[0]
    sb = state_block
    return pl.pallas_call(
        second_kernel,
        grid=(states // sb,),
        in_specs=[
            pl.BlockSpec((sb, ext_rows, ny), lambda i: (i, 0, 0)),
            pl.BlockSpec((sb, rows, ny), lambda i: (i, 0, 0)),
            pl.BlockSpec((rows, ny), lambda i: (0, 0)),
        ],
        out_specs=pl.BlockSpec((sb, rows, ny), lambda i: (i, 0, 0)),
        out_shape=jax.ShapeDtypeStruct((states, rows, ny), jnp.bfloat16),
    )(ext, psi, pot)


def per_device(psi, potential, rotation):
    own_states, planes, depth, ny = psi.shape
    rows = planes * depth
    psi_rows = psi.reshape(own_states, rows, ny)
    pot_rows = potential.reshape(rows, ny)
    first = run_first(rim_rows(psi_rows), pot_rows)
    filtered = run_second(rim_rows(first), psi_rows, pot_rows)
    count = lax.axis_size("band")
    points = rows * ny
    chunk = points // count
    blocks = filtered.reshape(own_states, count, chunk).transpose(1, 0, 2)
    gathered = lax.all_to_all(blocks, "band", 0, 0, tiled=True)
    mixed = lax.dot_general(
        rotation,
        gathered.reshape(own_states * count, chunk),
        (((0,), (0,)), ((), ())),
        preferred_element_type=jnp.float32,
    ).astype(jnp.bfloat16)
    back = lax.all_to_all(mixed.reshape(count, own_states, chunk), "band", 0, 0, tiled=True)
    result = back.reshape(count, own_states, chunk).transpose(1, 0, 2)
    return result.reshape(psi.shape)


def solution(mesh):
    in_specs = (P("band", "dom", None, None), P("dom", None, None), P())
    out_specs = P("band", "dom", None, None)
    return jax.shard_map(
        per_device, mesh=mesh, in_specs=in_specs, out_specs=out_specs, check_vma=False
    )
```

profile of v0, /device:TPU:25, one launch (start us, length us, event | category | flops | bytes accessed | tf_op | source)
XLA Modules:
  0.0 170.8 jit_solution(627922949318799787)
XLA Ops:
  0.0 0.0 copy-start
  0.0 2.2 %reshape.18.psi_ref = f32[32,24,384]{2,1,0:T(8,128)S(1)} reshape(f32[32,12,2,384]{3,2,1,0:T(2,128)} %param.3) | data formatting | bytes 2359296 | tf_op jit(solution)/shard_map/reshape | solution.py:111
  2.2 0.0 copy-start.1
  2.3 0.0 copy-start.3
  2.3 0.1 fusion.2
  2.4 1.1 copy.11
  3.5 2.6 %collective-permute-start.1 = (f32[32,12,384]{2,0,1:T(8,128)}, f32[32,12,384]{2,0,1:T(8,128)}, u32[]{:S(2)}, u32[]{:S(2)}) collective-permute-start(f32[32,12,384]{2,0,1:T(8,128)} %copy.11), channel_id=1, source_target_pairs={{32,0},{64,32},{96,64},{128,96},{160,128},{192,160},{224,192},{256... | collective-permute-start | bytes 1769480 | tf_op jit(solution)/shard_map/ppermute | solution.py:29
  6.0 1.0 copy.10
  7.0 6.6 %collective-permute-start = (f32[32,12,384]{2,0,1:T(8,128)}, f32[32,12,384]{2,0,1:T(8,128)}, u32[]{:S(2)}, u32[]{:S(2)}) collective-permute-start(f32[32,12,384]{2,0,1:T(8,128)} %copy.10), channel_id=1, source_target_pairs={{0,32},{32,64},{64,96},{96,128},{128,160},{160,192},{192,224},{224... | collective-permute-start | bytes 1769480 | tf_op jit(solution)/shard_map/ppermute | solution.py:28
  13.6 0.0 copy-done.3
  13.6 0.6 reshape.19.pot_ref
  14.3 4.3 %collective-permute-done.1 = f32[32,12,384]{2,0,1:T(8,128)} collective-permute-done((f32[32,12,384]{2,0,1:T(8,128)}, f32[32,12,384]{2,0,1:T(8,128)}, u32[]{:S(2)}, u32[]{:S(2)}) %collective-permute-start.1) | collective-permute-done | bytes 589856 | tf_op jit(solution)/shard_map/ppermute | solution.py:29
  18.6 1.4 copy.13
  20.0 0.8 collective-permute-done
  20.8 1.4 copy.12
  22.2 0.0 copy-done.1
  22.2 1.7 pad_maximum_fusion.ext_ref
  23.8 8.5 %shard_map.37 = f32[32,24,384]{2,1,0:T(8,128)} custom-call(f32[32,48,384]{2,1,0:T(8,128)} %pad_maximum_fusion.ext_ref, f32[24,384]{1,0:T(8,128)} %reshape.19.pot_ref), custom_call_target="tpu_custom_call" | custom-call | tf_op jit(solution)/shard_map/pallas_call | solution.py:79
  32.3 1.5 fusion.1
  33.8 0.2 copy.15
  34.0 0.0 copy-start.2
  34.0 2.1 %collective-permute-start.3 = (f32[32,12,384]{2,0,1:T(8,128)S(1)}, f32[32,12,384]{2,0,1:T(8,128)S(1)}, u32[]{:S(2)}, u32[]{:S(2)}) collective-permute-start(f32[32,12,384]{2,0,1:T(8,128)S(1)} %copy.15), channel_id=1, source_target_pairs={{32,0},{64,32},{96,64},{128,96},{160,128},{192,160},{224,192},{256... | collective-permute-start | bytes 1769480 | tf_op jit(solution)/shard_map/ppermute | solution.py:29
  36.1 0.2 copy.14
  36.3 8.0 %collective-permute-start.2 = (f32[32,12,384]{2,0,1:T(8,128)S(1)}, f32[32,12,384]{2,0,1:T(8,128)S(1)}, u32[]{:S(2)}, u32[]{:S(2)}) collective-permute-start(f32[32,12,384]{2,0,1:T(8,128)S(1)} %copy.14), channel_id=1, source_target_pairs={{0,32},{32,64},{64,96},{96,128},{128,160},{160,192},{192,224},{224... | collective-permute-start | bytes 1769480 | tf_op jit(solution)/shard_map/ppermute | solution.py:28
  44.3 5.4 %collective-permute-done.3 = f32[32,12,384]{2,0,1:T(8,128)S(1)} collective-permute-done((f32[32,12,384]{2,0,1:T(8,128)S(1)}, f32[32,12,384]{2,0,1:T(8,128)S(1)}, u32[]{:S(2)}, u32[]{:S(2)}) %collective-permute-start.3) | collective-permute-done | bytes 589856 | tf_op jit(solution)/shard_map/ppermute | solution.py:29
  49.7 0.4 copy.17
  50.1 1.0 collective-permute-done.2
  51.1 0.4 copy.16
  51.5 0.0 copy-done.2
  51.5 1.6 pad_maximum_fusion.1.ext_ref
  53.1 8.7 %shard_map.38 = bf16[32,24,384]{2,1,0:T(8,128)(2,1)} custom-call(f32[32,48,384]{2,1,0:T(8,128)} %pad_maximum_fusion.1.ext_ref, f32[32,24,384]{2,1,0:T(8,128)} %copy-done.1, f32[24,384]{1,0:T(8,128)} %reshape.19.pot_ref), custom_call_target="tpu_custom_call" | custom-call | tf_op jit(solution)/shard_map/pallas_call | solution.py:95
  61.8 2.2 %reshape.20 = bf16[32,32,288]{2,1,0:T(8,128)(2,1)S(1)} reshape(bf16[32,24,384]{2,1,0:T(8,128)(2,1)} %shard_map.38) | data formatting | bytes 1179648 | tf_op jit(solution)/shard_map/reshape | solution.py:118
  64.1 0.3 copy.22
  64.3 55.5 %all_to_all.10 = bf16[32,32,288]{2,1,0:T(8,128)(2,1)S(1)} all-to-all(bf16[32,32,288]{2,1,0:T(8,128)(2,1)S(1)} %bitcast.11), channel_id=1, replica_groups=mesh['dom'=16,'band'=32] {'band'}, dimensions={0} | all-to-all | bytes 1179648 | tf_op jit(solution)/shard_map/all_to_all | solution.py:119
  119.8 0.0 copy-done
  119.8 0.8 fusion
  120.6 0.4 copy.19
  121.0 47.4 %all_to_all.11 = bf16[32,32,288]{2,1,0:T(8,128)(2,1)S(1)} all-to-all(bf16[32,32,288]{2,1,0:T(8,128)(2,1)S(1)} %bitcast.13), channel_id=1, replica_groups=mesh['dom'=16,'band'=32] {'band'}, dimensions={0} | all-to-all | bytes 1179648 | tf_op jit(solution)/shard_map/all_to_all | solution.py:126
  168.4 0.3 copy.20
  168.7 2.2 %reshape.23 = bf16[32,12,2,384]{3,2,1,0:T(2,128)(2,1)} reshape(bf16[32,32,288]{2,1,0:T(8,128)(2,1)S(1)} %copy.20) | data formatting | bytes 1179648 | tf_op jit(solution)/shard_map/reshape | solution.py:128
Async XLA Ops:
  0.0 119.8 %copy-start = (bf16[1024,1024]{1,0:T(8,128)(2,1)S(1)}, bf16[1024,1024]{1,0:T(8,128)(2,1)}, u32[]{:S(2)}) copy-start(bf16[1024,1024]{1,0:T(8,128)(2,1)} %param.5) | copy-start | bytes 6291460
  2.2 19.9 %copy-start.1 = (f32[32,24,384]{2,1,0:T(8,128)}, f32[32,24,384]{2,1,0:T(8,128)S(1)}, u32[]{:S(2)}) copy-start(f32[32,24,384]{2,1,0:T(8,128)S(1)} %reshape.18.psi_ref) | copy-start | bytes 3538948
  2.3 11.4 %copy-start.3 = (f32[12,2,384]{2,1,0:T(2,128)S(1)}, f32[12,2,384]{2,1,0:T(2,128)}, u32[]{:S(2)}) copy-start(f32[12,2,384]{2,1,0:T(2,128)} %param.4) | copy-start | bytes 110596
  3.5 15.1 %collective-permute-start.1 = (f32[32,12,384]{2,0,1:T(8,128)}, f32[32,12,384]{2,0,1:T(8,128)}, u32[]{:S(2)}, u32[]{:S(2)}) collective-permute-start(f32[32,12,384]{2,0,1:T(8,128)} %copy.11), channel_id=1, source_target_pairs={{32,0},{64,32},{96,64},{128,96},{160,128},{192,160},{224,192},{256... | collective-permute-start | bytes 1769480 | tf_op jit(solution)/shard_map/ppermute | solution.py:29
  7.0 13.7 %collective-permute-start = (f32[32,12,384]{2,0,1:T(8,128)}, f32[32,12,384]{2,0,1:T(8,128)}, u32[]{:S(2)}, u32[]{:S(2)}) collective-permute-start(f32[32,12,384]{2,0,1:T(8,128)} %copy.10), channel_id=1, source_target_pairs={{0,32},{32,64},{64,96},{96,128},{128,160},{160,192},{192,224},{224... | collective-permute-start | bytes 1769480 | tf_op jit(solution)/shard_map/ppermute | solution.py:28
  34.0 17.4 %copy-start.2 = (f32[32,24,384]{2,1,0:T(8,128)S(1)}, f32[32,24,384]{2,1,0:T(8,128)}, u32[]{:S(2)}) copy-start(f32[32,24,384]{2,1,0:T(8,128)} %shard_map.37) | copy-start | bytes 3538948
  34.0 15.7 %collective-permute-start.3 = (f32[32,12,384]{2,0,1:T(8,128)S(1)}, f32[32,12,384]{2,0,1:T(8,128)S(1)}, u32[]{:S(2)}, u32[]{:S(2)}) collective-permute-start(f32[32,12,384]{2,0,1:T(8,128)S(1)} %copy.15), channel_id=1, source_target_pairs={{32,0},{64,32},{96,64},{128,96},{160,128},{192,160},{224,192},{256... | collective-permute-start | bytes 1769480 | tf_op jit(solution)/shard_map/ppermute | solution.py:29
  36.3 14.8 %collective-permute-start.2 = (f32[32,12,384]{2,0,1:T(8,128)S(1)}, f32[32,12,384]{2,0,1:T(8,128)S(1)}, u32[]{:S(2)}, u32[]{:S(2)}) collective-permute-start(f32[32,12,384]{2,0,1:T(8,128)S(1)} %copy.14), channel_id=1, source_target_pairs={{0,32},{32,64},{64,96},{96,128},{128,160},{160,192},{192,224},{224... | collective-permute-start | bytes 1769480 | tf_op jit(solution)/shard_map/ppermute | solution.py:28
where the time goes:
time: 172 us; the launch traced here: 171 us
  blocking collectives  103 us (60%)
  starting transfers between devices  19.2 us (11%)
  Pallas kernels  17.2 us (10%)
  local copies, waits for them, and re-layouts  15.8 us (9%)
  waiting for transfers between devices  11.5 us (7%)
  other arithmetic  3.29 us (2%)
    all_to_all x1, blocking collectives, per_device(): gathered = lax.all_to_all(blocks, 'band', 0, 0, tiled=True)  55.5 us
    all_to_all x1, blocking collectives, per_device(): lax.all_to_all(mixed.reshape(count, own_states, chunk), 'band', 0, 0, til...  47.4 us
    ppermute x2, starting transfers between devices, rim_rows(): lax.ppermute(tail, 'dom', [(i, (i + 1) % count) for i in range(count)])  14.6 us
    ppermute x2, waiting for transfers between devices, rim_rows(): lax.ppermute(head, 'dom', [((i + 1) % count, i) for i in range(count)])  9.72 us
    pallas_call x1, Pallas kernels, run_second(): pl.pallas_call(second_kernel, grid=(states // sb,), in_specs=[pl.BlockSpe...  8.72 us
    pallas_call x1, Pallas kernels, run_first(): pl.pallas_call(first_kernel, grid=(states // sb,), in_specs=[pl.BlockSpec...  8.48 us
    ppermute x2, starting transfers between devices, rim_rows(): lax.ppermute(head, 'dom', [((i + 1) % count, i) for i in range(count)])  4.63 us
  transfers between devices with their start and end apart: 4, of which 4 were waited for; matrix products, arithmetic and copies ran while one was open for 2% of the time, Pallas kernels for 0%

commit v1 on v0

v1 whole, which is shorter than its diff:
```python
import jax
import jax.numpy as jnp
from jax import lax
from jax.experimental import pallas as pl
from jax.experimental.pallas import tpu as pltpu
from jax.sharding import PartitionSpec as P

coeffs = (
    -5369.0 / 1800.0,
    12.0 / 7.0,
    -15.0 / 56.0,
    10.0 / 189.0,
    -1.0 / 112.0,
    2.0 / 1925.0,
    -1.0 / 16632.0,
)
center_shift = 32.5
half_width = 27.5
reach = 6
state_block = 8


def swap_rims(head, tail):
    count = lax.axis_size("dom")
    left = lax.ppermute(tail, "dom", [(i, (i + 1) % count) for i in range(count)])
    right = lax.ppermute(head, "dom", [((i + 1) % count, i) for i in range(count)])
    return left, right


def ham_rows(left_ref, mid_ref, right_ref, ext_ref, pot, p, t, rows, ny):
    halo = 2 * reach
    s = 2 * p + t
    ext_ref[pl.ds(0, halo), :] = left_ref[p, pl.ds(t * halo, halo), :]
    ext_ref[pl.ds(halo, rows), :] = mid_ref[s]
    ext_ref[pl.ds(halo + rows, halo), :] = right_ref[p, pl.ds(t * halo, halo), :]
    mid = ext_ref[pl.ds(halo, rows), :]
    lap = (3.0 * coeffs[0]) * mid
    for k in range(1, 7):
        lap = lap + coeffs[k] * (
            ext_ref[pl.ds(halo + 2 * k, rows), :] + ext_ref[pl.ds(halo - 2 * k, rows), :]
        )
    for k in range(1, 7):
        lap = lap + coeffs[k] * (pltpu.roll(mid, k, 1) + pltpu.roll(mid, ny - k, 1))
    up = ext_ref[pl.ds(halo + 1, rows), :]
    down = ext_ref[pl.ds(halo - 1, rows), :]
    even = lax.broadcasted_iota(jnp.int32, (rows, ny), 0) % 2 == 0
    lap = lap + coeffs[1] * jnp.where(even, up, down)
    return -2.0 * lap + pot * mid, mid


def first_kernel(left_ref, mid_ref, right_ref, pot_ref, out_ref, head_ref, tail_ref, ext_ref):
    rows, ny = out_ref.shape[1], out_ref.shape[2]
    halo = 2 * reach
    pot = pot_ref[...]

    def body(p, carry):
        for t in range(2):
            s = 2 * p + t
            h, mid = ham_rows(left_ref, mid_ref, right_ref, ext_ref, pot, p, t, rows, ny)
            out_ref[s] = (h - center_shift * mid) / half_width
            head_ref[p, pl.ds(t * halo, halo), :] = out_ref[s, pl.ds(0, halo), :]
            tail_ref[p, pl.ds(t * halo, halo), :] = out_ref[s, pl.ds(rows - halo, halo), :]
        return carry

    lax.fori_loop(0, out_ref.shape[0] // 2, body, 0)


def second_kernel(left_ref, mid_ref, right_ref, psi_ref, pot_ref, out_ref, ext_ref):
    rows, ny = out_ref.shape[1], out_ref.shape[2]
    pot = pot_ref[...]

    def body(p, carry):
        for t in range(2):
            s = 2 * p + t
            h, mid = ham_rows(left_ref, mid_ref, right_ref, ext_ref, pot, p, t, rows, ny)
            second = 2.0 / half_width * (h - center_shift * mid) - psi_ref[s]
            out_ref[s] = second.astype(out_ref.dtype)
        return carry

    lax.fori_loop(0, out_ref.shape[0] // 2, body, 0)


def run_first(left, mid, right, pot):
    states, rows, ny = mid.shape
    pair_rows = left.shape[1]
    sb = state_block
    rim = pl.BlockSpec((sb // 2, pair_rows, ny), lambda i: (i, 0, 0))
    body = pl.BlockSpec((sb, rows, ny), lambda i: (i, 0, 0))
    return pl.pallas_call(
        first_kernel,
        grid=(states // sb,),
        in_specs=[rim, body, rim, pl.BlockSpec((rows, ny), lambda i: (0, 0))],
        out_specs=[body, rim, rim],
        out_shape=[
            jax.ShapeDtypeStruct((states, rows, ny), jnp.float32),
            jax.ShapeDtypeStruct(left.shape, jnp.float32),
            jax.ShapeDtypeStruct(left.shape, jnp.float32),
        ],
        scratch_shapes=[pltpu.VMEM((rows + 4 * reach, ny), jnp.float32)],
    )(left, mid, right, pot)


def run_second(left, mid, right, psi, pot):
    states, rows, ny = mid.shape
    pair_rows = left.shape[1]
    sb = state_block
    rim = pl.BlockSpec((sb // 2, pair_rows, ny), lambda i: (i, 0, 0))
    body = pl.BlockSpec((sb, rows, ny), lambda i: (i, 0, 0))
    return pl.pallas_call(
        second_kernel,
        grid=(states // sb,),
        in_specs=[rim, body, rim, body, pl.BlockSpec((rows, ny), lambda i: (0, 0))],
        out_specs=body,
        out_shape=jax.ShapeDtypeStruct((states, rows, ny), jnp.bfloat16),
        scratch_shapes=[pltpu.VMEM((rows + 4 * reach, ny), jnp.float32)],
    )(left, mid, right, psi, pot)


def per_device(psi, potential, rotation):
    own_states, planes, depth, ny = psi.shape
    rows = planes * depth
    halo = 2 * reach
    psi_rows = psi.reshape(own_states, rows, ny)
    pot_rows = potential.reshape(rows, ny)
    pairs = (own_states // 2, 2 * halo, ny)
    left, right = swap_rims(
        psi_rows[:, :halo].reshape(pairs), psi_rows[:, rows - halo :].reshape(pairs)
    )
    first, head, tail = run_first(left, psi_rows, right, pot_rows)
    left, right = swap_rims(head, tail)
    filtered = run_second(left, first, right, psi_rows, pot_rows)
    count = lax.axis_size("band")
    chunk = rows * ny // count
    blocks = filtered.reshape(own_states, count, chunk).transpose(1, 0, 2)
    wire = (count, own_states * chunk // ny, ny)
    gathered = lax.all_to_all(blocks.reshape(wire), "band", 0, 0, tiled=True)
    mixed = lax.dot_general(
        rotation,
        gathered.reshape(own_states * count, chunk),
        (((0,), (0,)), ((), ())),
        preferred_element_type=jnp.float32,
    ).astype(jnp.bfloat16)
    back = lax.all_to_all(mixed.reshape(wire), "band", 0, 0, tiled=True)
    result = back.reshape(count, own_states, chunk).transpose(1, 0, 2)
    return result.reshape(psi.shape)


def solution(mesh):
    in_specs = (P("band", "dom", None, None), P("dom", None, None), P())
    out_specs = P("band", "dom", None, None)
    return jax.shard_map(
        per_device, mesh=mesh, in_specs=in_specs, out_specs=out_specs, check_vma=False
    )
```

time: 172 us -> 163 us (0.948)
  blocking collectives: 103 us -> 85.9 us
  waiting for transfers between devices: 11.5 us -> 25.1 us
  local copies, waits for them, and re-layouts: 15.8 us -> 24.8 us
  starting transfers between devices: 19.2 us -> 11.1 us
  other arithmetic: 3.29 us -> 0 us
  Pallas kernels: 17.2 us -> 15.2 us
    all_to_all x2, blocking collectives: 103 us -> 85.9 us  [the longest x1 47.1 us: per_device(): gathered = lax.all_to_all(blocks.reshape(wire), 'band', 0, 0, tiled=True)]
    ppermute x4, waiting for transfers between devices: 11.5 us -> 25.1 us  [the longest x2 16.7 us: swap_rims(): lax.ppermute(head, 'dom', [((i + 1) % count, i) for i in range(count)])]
    reshape x0 -> x6, local copies, waits for them, and re-layouts: none -> 10.3 us  [the longest x1 2.58 us: per_device(): gathered = lax.all_to_all(blocks.reshape(wire), 'band', 0, 0, tiled=True)]
    ppermute x4, starting transfers between devices: 19.2 us -> 11.1 us  [the longest x2 6.77 us: swap_rims(): lax.ppermute(tail, 'dom', [(i, (i + 1) % count) for i in range(count)])]
    ppermute x4 -> x0, local copies, waits for them, and re-layouts: 3.55 us -> none  [the longest x2 1.77 us: rim_rows(): lax.ppermute(head, 'dom', [((i + 1) % count, i) for i in range(count)])]
    concatenate x2 -> x0, other arithmetic: 3.29 us -> none  [rim_rows(): return jnp.concatenate([left, rows, right], axis=1)]
    slice x6 -> x1, local copies, waits for them, and re-layouts: 4.05 us -> 1.32 us  [per_device(): psi_rows[:, :halo].reshape(pairs)]
    pallas_call x2, Pallas kernels: 17.2 us -> 15.2 us  [the longest x1 7.68 us: run_first(): pl.pallas_call(first_kernel, grid=(states // sb,), in_specs=[rim, body, r...]
  transfers between devices with their start and end apart: 4 -> 4, of which waited for: 4 -> 4; matrix products, arithmetic and copies ran while one was open for 2% -> 1% of each run, Pallas kernels for 0% -> 0%
where the time goes in v1:
time: 163 us
  blocking collectives  85.9 us (53%)
  waiting for transfers between devices  25.1 us (15%)
  local copies, waits for them, and re-layouts  24.8 us (15%)
  Pallas kernels  15.2 us (9%)
  starting transfers between devices  11.1 us (7%)
    all_to_all x1, blocking collectives, per_device(): gathered = lax.all_to_all(blocks.reshape(wire), 'band', 0, 0, tiled=True)  47.1 us
    all_to_all x1, blocking collectives, per_device(): back = lax.all_to_all(mixed.reshape(wire), 'band', 0, 0, tiled=True)  38.8 us
    ppermute x2, waiting for transfers between devices, swap_rims(): lax.ppermute(head, 'dom', [((i + 1) % count, i) for i in range(count)])  16.7 us
    ppermute x2, waiting for transfers between devices, swap_rims(): lax.ppermute(tail, 'dom', [(i, (i + 1) % count) for i in range(count)])  8.36 us
    pallas_call x1, Pallas kernels, run_first(): pl.pallas_call(first_kernel, grid=(states // sb,), in_specs=[rim, body, r...  7.68 us
    pallas_call x1, Pallas kernels, run_second(): pl.pallas_call(second_kernel, grid=(states // sb,), in_specs=[rim, body,...  7.5 us
    ppermute x2, starting transfers between devices, swap_rims(): lax.ppermute(tail, 'dom', [(i, (i + 1) % count) for i in range(count)])  6.77 us
    ppermute x2, starting transfers between devices, swap_rims(): lax.ppermute(head, 'dom', [((i + 1) % count, i) for i in range(count)])  4.31 us
  transfers between devices with their start and end apart: 4, of which 4 were waited for; matrix products, arithmetic and copies ran while one was open for 1% of the time, Pallas kernels for 0%

profile of v1, /device:TPU:25, one launch (start us, length us, event | category | flops | bytes accessed | tf_op | source)
XLA Modules:
  0.0 162.9 jit_solution(741939583992583944)
XLA Ops:
  0.0 0.0 copy-start
  0.0 2.2 %reshape.30.mid_ref.psi_ref = f32[32,24,384]{2,1,0:T(8,128)S(1)} reshape(f32[32,12,2,384]{3,2,1,0:T(2,128)} %param.3) | data formatting | bytes 2359296 | tf_op jit(solution)/shard_map/reshape | solution.py:123
  2.2 0.0 copy-start.1
  2.3 1.3 fusion.1
  3.6 0.2 copy-done.1
  3.8 0.0 copy-start.2
  3.8 0.0 copy-start.7
  3.8 2.1 %reshape.31 = f32[16,24,384]{2,1,0:T(8,128)} reshape(f32[32,12,384]{2,1,0:T(8,128)} %get-tuple-element.12) | data formatting | bytes 1179648 | tf_op jit(solution)/shard_map/reshape | solution.py:127
  5.9 4.9 %collective-permute-start = (f32[16,24,384]{2,1,0:T(8,128)}, f32[16,24,384]{2,1,0:T(8,128)S(1)}, u32[]{:S(2)}, u32[]{:S(2)}) collective-permute-start(f32[16,24,384]{2,1,0:T(8,128)} %reshape.31), channel_id=1, source_target_pairs={{0,32},{32,64},{64,96},{96,128},{128,160},{160,192},{192,224},{224... | collective-permute-start | bytes 1769480 | tf_op jit(solution)/shard_map/ppermute | solution.py:25
  10.7 0.0 copy-done.2
  10.8 0.9 reshape.32
  11.7 1.9 %collective-permute-start.1 = (f32[16,24,384]{2,1,0:T(8,128)}, f32[16,24,384]{2,1,0:T(8,128)S(1)}, u32[]{:S(2)}, u32[]{:S(2)}) collective-permute-start(f32[16,24,384]{2,1,0:T(8,128)} %reshape.32), channel_id=1, source_target_pairs={{32,0},{64,32},{96,64},{128,96},{160,128},{192,160},{224,192},{256... | collective-permute-start | bytes 1769480 | tf_op jit(solution)/shard_map/ppermute | solution.py:26
  13.6 0.0 copy-done.7
  13.6 0.6 reshape.33.pot_ref
  14.2 3.7 %collective-permute-done.left_ref = f32[16,24,384]{2,1,0:T(8,128)S(1)} collective-permute-done((f32[16,24,384]{2,1,0:T(8,128)}, f32[16,24,384]{2,1,0:T(8,128)S(1)}, u32[]{:S(2)}, u32[]{:S(2)}) %collective-permute-start) | collective-permute-done | bytes 589856 | tf_op jit(solution)/shard_map/ppermute | solution.py:25
  17.9 0.0 copy-start.5
  17.9 8.8 %collective-permute-done.1.right_ref = f32[16,24,384]{2,1,0:T(8,128)S(1)} collective-permute-done((f32[16,24,384]{2,1,0:T(8,128)}, f32[16,24,384]{2,1,0:T(8,128)S(1)}, u32[]{:S(2)}, u32[]{:S(2)}) %collective-permute-start.1) | collective-permute-done | bytes 589856 | tf_op jit(solution)/shard_map/ppermute | solution.py:26
  26.7 0.0 copy-done.5
  26.7 0.0 copy-start.6
  26.7 0.8 copy-done.6
  27.5 7.7 %shard_map.37 = (f32[32,24,384]{2,1,0:T(8,128)}, f32[16,24,384]{2,1,0:T(8,128)}, f32[16,24,384]{2,1,0:T(8,128)}) custom-call(f32[16,24,384]{2,1,0:T(8,128)} %copy-done.5, f32[32,24,384]{2,1,0:T(8,128)} %copy-done.1, f32[16,24,384]{2,1,0:T(8,128)} %copy-done.6, f32[24,384]{1,0:T(8,128)} %reshape.33.pot_ref), custom_call_target="tpu_custom_call" | custom-call | tf_op jit(solution)/shard_map/pallas_call | solution.py:89
  35.2 1.9 %collective-permute-start.2 = (f32[16,24,384]{2,1,0:T(8,128)}, f32[16,24,384]{2,1,0:T(8,128)S(1)}, u32[]{:S(2)}, u32[]{:S(2)}) collective-permute-start(f32[16,24,384]{2,1,0:T(8,128)} %get-tuple-element.8), channel_id=1, source_target_pairs={{0,32},{32,64},{64,96},{96,128},{128,160},{160,192},{192,224},{224... | collective-permute-start | bytes 1769480 | tf_op jit(solution)/shard_map/ppermute | solution.py:25
  37.1 2.4 %collective-permute-start.3 = (f32[16,24,384]{2,1,0:T(8,128)}, f32[16,24,384]{2,1,0:T(8,128)S(1)}, u32[]{:S(2)}, u32[]{:S(2)}) collective-permute-start(f32[16,24,384]{2,1,0:T(8,128)} %get-tuple-element.10), channel_id=1, source_target_pairs={{32,0},{64,32},{96,64},{128,96},{160,128},{192,160},{224,192},{256... | collective-permute-start | bytes 1769480 | tf_op jit(solution)/shard_map/ppermute | solution.py:26
  39.5 4.7 %collective-permute-done.2.left_ref = f32[16,24,384]{2,1,0:T(8,128)S(1)} collective-permute-done((f32[16,24,384]{2,1,0:T(8,128)}, f32[16,24,384]{2,1,0:T(8,128)S(1)}, u32[]{:S(2)}, u32[]{:S(2)}) %collective-permute-start.2) | collective-permute-done | bytes 589856 | tf_op jit(solution)/shard_map/ppermute | solution.py:25
  44.2 0.0 copy-start.3
  44.2 7.9 %collective-permute-done.3.right_ref = f32[16,24,384]{2,1,0:T(8,128)S(1)} collective-permute-done((f32[16,24,384]{2,1,0:T(8,128)}, f32[16,24,384]{2,1,0:T(8,128)S(1)}, u32[]{:S(2)}, u32[]{:S(2)}) %collective-permute-start.3) | collective-permute-done | bytes 589856 | tf_op jit(solution)/shard_map/ppermute | solution.py:26
  52.1 0.0 copy-start.4
  52.1 0.0 copy-done.3
  52.1 0.8 copy-done.4
  52.9 7.5 %shard_map.38 = bf16[32,24,384]{2,1,0:T(8,128)(2,1)} custom-call(f32[16,24,384]{2,1,0:T(8,128)} %copy-done.3, f32[32,24,384]{2,1,0:T(8,128)} %get-tuple-element.9.mid_ref, f32[16,24,384]{2,1,0:T(8,128)} %copy-done.4, f32[32,24,384]{2,1,0:T(8,128)} %copy-done.1, f32[24,384]{1,0:T(8,128)} %reshape.33.pot_ref), custom_call_target="tpu_custom_call" | custom-call | tf_op jit(solution)/shard_map/pallas_call | solution.py:109
  60.4 2.2 %reshape.34 = bf16[32,32,288]{2,1,0:T(8,128)(2,1)S(1)} reshape(bf16[32,24,384]{2,1,0:T(8,128)(2,1)} %shard_map.38) | data formatting | bytes 1179648 | tf_op jit(solution)/shard_map/reshape | solution.py:134
  62.7 1.2 copy.10
  63.8 2.6 %reshape.35 = bf16[32,24,384]{2,1,0:T(8,128)(2,1)S(1)} reshape(bf16[32,32,288]{2,1,0:T(8,128)(2,1)} %bitcast.8) | data formatting | bytes 1179648 | tf_op jit(solution)/shard_map/reshape | solution.py:136
  66.4 47.1 %all_to_all.10 = bf16[32,24,384]{2,1,0:T(8,128)(2,1)S(1)} all-to-all(bf16[32,24,384]{2,1,0:T(8,128)(2,1)S(1)} %reshape.35), channel_id=1, replica_groups=mesh['dom'=16,'band'=32] {'band'}, dimensions={0} | all-to-all | bytes 1179648 | tf_op jit(solution)/shard_map/all_to_all | solution.py:136
  113.6 1.1 reshape.36
  114.7 0.0 copy-done
  114.7 0.8 fusion
  115.5 0.4 copy.7
  115.9 1.4 reshape.37
  117.2 38.8 %all_to_all.11 = bf16[32,24,384]{2,1,0:T(8,128)(2,1)} all-to-all(bf16[32,24,384]{2,1,0:T(8,128)(2,1)S(1)} %reshape.37), channel_id=1, replica_groups=mesh['dom'=16,'band'=32] {'band'}, dimensions={0} | all-to-all | bytes 1179648 | tf_op jit(solution)/shard_map/all_to_all | solution.py:143
  156.0 2.2 %reshape.38 = bf16[32,32,288]{2,1,0:T(8,128)(2,1)S(1)} reshape(bf16[32,24,384]{2,1,0:T(8,128)(2,1)} %all_to_all.11) | data formatting | bytes 1179648 | tf_op jit(solution)/shard_map/reshape | solution.py:144
  158.2 1.2 copy.8
  159.4 3.5 %reshape.39 = bf16[32,12,2,384]{3,2,1,0:T(2,128)(2,1)} reshape(bf16[32,32,288]{2,1,0:T(8,128)(2,1)} %copy.8) | data formatting | bytes 1179648 | tf_op jit(solution)/shard_map/reshape | solution.py:145
Async XLA Ops:
  0.0 114.7 %copy-start = (bf16[1024,1024]{1,0:T(8,128)(2,1)S(1)}, bf16[1024,1024]{1,0:T(8,128)(2,1)}, u32[]{:S(2)}) copy-start(bf16[1024,1024]{1,0:T(8,128)(2,1)} %param.5) | copy-start | bytes 6291460
  2.2 1.5 copy-start.1
  3.8 7.0 %copy-start.2 = (f32[32,12,384]{2,1,0:T(8,128)S(1)}, f32[32,12,384]{2,1,0:T(8,128)}, u32[]{:S(2)}) copy-start(f32[32,12,384]{2,1,0:T(8,128)} %get-tuple-element.11) | copy-start | bytes 1769476
  3.8 9.8 %copy-start.7 = (f32[12,2,384]{2,1,0:T(2,128)S(1)}, f32[12,2,384]{2,1,0:T(2,128)}, u32[]{:S(2)}) copy-start(f32[12,2,384]{2,1,0:T(2,128)} %param.4) | copy-start | bytes 110596
  5.9 12.0 %collective-permute-start = (f32[16,24,384]{2,1,0:T(8,128)}, f32[16,24,384]{2,1,0:T(8,128)S(1)}, u32[]{:S(2)}, u32[]{:S(2)}) collective-permute-start(f32[16,24,384]{2,1,0:T(8,128)} %reshape.31), channel_id=1, source_target_pairs={{0,32},{32,64},{64,96},{96,128},{128,160},{160,192},{192,224},{224... | collective-permute-start | bytes 1769480 | tf_op jit(solution)/shard_map/ppermute | solution.py:25
  11.7 15.0 %collective-permute-start.1 = (f32[16,24,384]{2,1,0:T(8,128)}, f32[16,24,384]{2,1,0:T(8,128)S(1)}, u32[]{:S(2)}, u32[]{:S(2)}) collective-permute-start(f32[16,24,384]{2,1,0:T(8,128)} %reshape.32), channel_id=1, source_target_pairs={{32,0},{64,32},{96,64},{128,96},{160,128},{192,160},{224,192},{256... | collective-permute-start | bytes 1769480 | tf_op jit(solution)/shard_map/ppermute | solution.py:26
  17.9 8.8 %copy-start.5 = (f32[16,24,384]{2,1,0:T(8,128)}, f32[16,24,384]{2,1,0:T(8,128)S(1)}, u32[]{:S(2)}) copy-start(f32[16,24,384]{2,1,0:T(8,128)S(1)} %collective-permute-done.left_ref) | copy-start | bytes 1769476
  26.7 0.8 copy-start.6
  35.2 9.0 %collective-permute-start.2 = (f32[16,24,384]{2,1,0:T(8,128)}, f32[16,24,384]{2,1,0:T(8,128)S(1)}, u32[]{:S(2)}, u32[]{:S(2)}) collective-permute-start(f32[16,24,384]{2,1,0:T(8,128)} %get-tuple-element.8), channel_id=1, source_target_pairs={{0,32},{32,64},{64,96},{96,128},{128,160},{160,192},{192,224},{224... | collective-permute-start | bytes 1769480 | tf_op jit(solution)/shard_map/ppermute | solution.py:25
  37.1 15.0 %collective-permute-start.3 = (f32[16,24,384]{2,1,0:T(8,128)}, f32[16,24,384]{2,1,0:T(8,128)S(1)}, u32[]{:S(2)}, u32[]{:S(2)}) collective-permute-start(f32[16,24,384]{2,1,0:T(8,128)} %get-tuple-element.10), channel_id=1, source_target_pairs={{32,0},{64,32},{96,64},{128,96},{160,128},{192,160},{224,192},{256... | collective-permute-start | bytes 1769480 | tf_op jit(solution)/shard_map/ppermute | solution.py:26
  44.2 7.9 %copy-start.3 = (f32[16,24,384]{2,1,0:T(8,128)}, f32[16,24,384]{2,1,0:T(8,128)S(1)}, u32[]{:S(2)}) copy-start(f32[16,24,384]{2,1,0:T(8,128)S(1)} %collective-permute-done.2.left_ref) | copy-start | bytes 1769476
  52.1 0.8 copy-start.4

commit v2 on v1

--- a/solution.py
+++ b/solution.py
@@ -120,12 +120,12 @@
     own_states, planes, depth, ny = psi.shape
     rows = planes * depth
     halo = 2 * reach
+    pairs = (own_states // 2, 2 * halo, ny)
+    left, right = swap_rims(
+        psi[:, :reach].reshape(pairs), psi[:, planes - reach :].reshape(pairs)
+    )
     psi_rows = psi.reshape(own_states, rows, ny)
     pot_rows = potential.reshape(rows, ny)
-    pairs = (own_states // 2, 2 * halo, ny)
-    left, right = swap_rims(
-        psi_rows[:, :halo].reshape(pairs), psi_rows[:, rows - halo :].reshape(pairs)
-    )
     first, head, tail = run_first(left, psi_rows, right, pot_rows)
     left, right = swap_rims(head, tail)
     filtered = run_second(left, first, right, psi_rows, pot_rows)

time: 163 us -> 163 us (level)
  waiting for transfers between devices: 25.1 us -> 23.3 us
    ppermute x2, waiting for transfers between devices: 8.36 us -> 5.01 us  [swap_rims(): lax.ppermute(tail, 'dom', [(i, (i + 1) % count) for i in range(count)])]
    reshape x2, local copies, waits for them, and re-layouts: 2.98 us -> 4.68 us  [the longest x1 2.4 us: per_device(): psi[:, planes - reach:].reshape(pairs)]
  transfers between devices with their start and end apart: 4 -> 4, of which waited for: 4 -> 4; matrix products, arithmetic and copies ran while one was open for 1% -> 3% of each run, Pallas kernels for 0% -> 0%
where the time goes in v2:
time: 163 us
  blocking collectives  85.9 us (53%)
  local copies, waits for them, and re-layouts  26.4 us (16%)
  waiting for transfers between devices  23.3 us (14%)
  Pallas kernels  15.1 us (9%)
  starting transfers between devices  11.2 us (7%)
    all_to_all x1, blocking collectives, per_device(): gathered = lax.all_to_all(blocks.reshape(wire), 'band', 0, 0, tiled=True)  47.1 us
    all_to_all x1, blocking collectives, per_device(): back = lax.all_to_all(mixed.reshape(wire), 'band', 0, 0, tiled=True)  38.8 us
    ppermute x2, waiting for transfers between devices, swap_rims(): lax.ppermute(head, 'dom', [((i + 1) % count, i) for i in range(count)])  18.3 us
    pallas_call x1, Pallas kernels, run_first(): pl.pallas_call(first_kernel, grid=(states // sb,), in_specs=[rim, body, r...  7.64 us
    pallas_call x1, Pallas kernels, run_second(): pl.pallas_call(second_kernel, grid=(states // sb,), in_specs=[rim, body,...  7.5 us
    ppermute x2, starting transfers between devices, swap_rims(): lax.ppermute(tail, 'dom', [(i, (i + 1) % count) for i in range(count)])  6.77 us
    ppermute x2, waiting for transfers between devices, swap_rims(): lax.ppermute(tail, 'dom', [(i, (i + 1) % count) for i in range(count)])  5.01 us
    ppermute x2, starting transfers between devices, swap_rims(): lax.ppermute(head, 'dom', [((i + 1) % count, i) for i in range(count)])  4.45 us
  transfers between devices with their start and end apart: 4, of which 4 were waited for; matrix products, arithmetic and copies ran while one was open for 3% of the time, Pallas kernels for 0%

profile of v2, /device:TPU:25, one launch (start us, length us, event | category | flops | bytes accessed | tf_op | source)
XLA Modules:
  0.0 162.9 jit_solution(6186312334997822131)
XLA Ops:
  0.0 0.0 copy-start
  0.0 2.8 %fusion.1 = (f32[32,6,2,384]{3,2,1,0:T(2,128)}, f32[32,6,2,384]{3,2,1,0:T(2,128)}) fusion(f32[32,12,2,384]{3,2,1,0:T(2,128)} %param.3), kind=kLoop, calls=%fused_computation.3 | loop fusion | bytes 2359296 | tf_op jit(solution)/shard_map/slice | solution.py:125
  2.8 0.0 copy-start.1
  2.8 2.4 %reshape.30 = f32[16,24,384]{2,1,0:T(8,128)} reshape(f32[32,6,2,384]{3,2,1,0:T(2,128)} %get-tuple-element.12) | data formatting | bytes 1179648 | tf_op jit(solution)/shard_map/reshape | solution.py:125
  5.2 4.9 %collective-permute-start = (f32[16,24,384]{2,1,0:T(8,128)}, f32[16,24,384]{2,1,0:T(8,128)}, u32[]{:S(2)}, u32[]{:S(2)}) collective-permute-start(f32[16,24,384]{2,1,0:T(8,128)} %reshape.30), channel_id=1, source_target_pairs={{0,32},{32,64},{64,96},{96,128},{128,160},{160,192},{192,224},{224... | collective-permute-start | bytes 1769480 | tf_op jit(solution)/shard_map/ppermute | solution.py:25
  10.1 2.3 %reshape.32 = f32[16,24,384]{2,1,0:T(8,128)} reshape(f32[32,6,2,384]{3,2,1,0:T(2,128)} %get-tuple-element.11) | data formatting | bytes 1179648 | tf_op jit(solution)/shard_map/reshape | solution.py:125
  12.4 0.0 copy-start.4
  12.4 2.0 %collective-permute-start.1 = (f32[16,24,384]{2,1,0:T(8,128)}, f32[16,24,384]{2,1,0:T(8,128)}, u32[]{:S(2)}, u32[]{:S(2)}) collective-permute-start(f32[16,24,384]{2,1,0:T(8,128)} %reshape.32), channel_id=1, source_target_pairs={{32,0},{64,32},{96,64},{128,96},{160,128},{192,160},{224,192},{256... | collective-permute-start | bytes 1769480 | tf_op jit(solution)/shard_map/ppermute | solution.py:26
  14.4 0.0 copy-done.1
  14.4 1.8 %reshape.31.mid_ref.psi_ref = f32[32,24,384]{2,1,0:T(8,128)} reshape(f32[32,12,2,384]{3,2,1,0:T(2,128)S(1)} %copy-done.1) | data formatting | bytes 2359296 | tf_op jit(solution)/shard_map/reshape | solution.py:127
  16.3 0.0 copy-done.4
  16.3 0.6 reshape.33.pot_ref
  16.9 0.3 collective-permute-done.left_ref
  17.2 10.4 %collective-permute-done.1.right_ref = f32[16,24,384]{2,1,0:T(8,128)} collective-permute-done((f32[16,24,384]{2,1,0:T(8,128)}, f32[16,24,384]{2,1,0:T(8,128)}, u32[]{:S(2)}, u32[]{:S(2)}) %collective-permute-start.1) | collective-permute-done | bytes 589856 | tf_op jit(solution)/shard_map/ppermute | solution.py:26
  27.6 7.6 %shard_map.37 = (f32[32,24,384]{2,1,0:T(8,128)}, f32[16,24,384]{2,1,0:T(8,128)}, f32[16,24,384]{2,1,0:T(8,128)}) custom-call(f32[16,24,384]{2,1,0:T(8,128)} %collective-permute-done.left_ref, f32[32,24,384]{2,1,0:T(8,128)} %reshape.31.mid_ref.psi_ref, f32[16,24,384]{2,1,0:T(8,128)} %collective-permute-done.1.right_ref, f32[24,384]{1,0:T(8,128)} %reshape.33.pot_ref), custom_call_target="tpu_custom_call" | custom-call | tf_op jit(solution)/shard_map/pallas_call | solution.py:89
  35.3 1.9 %collective-permute-start.2 = (f32[16,24,384]{2,1,0:T(8,128)}, f32[16,24,384]{2,1,0:T(8,128)S(1)}, u32[]{:S(2)}, u32[]{:S(2)}) collective-permute-start(f32[16,24,384]{2,1,0:T(8,128)} %get-tuple-element.8), channel_id=1, source_target_pairs={{0,32},{32,64},{64,96},{96,128},{128,160},{160,192},{192,224},{224... | collective-permute-start | bytes 1769480 | tf_op jit(solution)/shard_map/ppermute | solution.py:25
  37.2 2.4 %collective-permute-start.3 = (f32[16,24,384]{2,1,0:T(8,128)}, f32[16,24,384]{2,1,0:T(8,128)S(1)}, u32[]{:S(2)}, u32[]{:S(2)}) collective-permute-start(f32[16,24,384]{2,1,0:T(8,128)} %get-tuple-element.10), channel_id=1, source_target_pairs={{32,0},{64,32},{96,64},{128,96},{160,128},{192,160},{224,192},{256... | collective-permute-start | bytes 1769480 | tf_op jit(solution)/shard_map/ppermute | solution.py:26
  39.6 4.7 %collective-permute-done.2.left_ref = f32[16,24,384]{2,1,0:T(8,128)S(1)} collective-permute-done((f32[16,24,384]{2,1,0:T(8,128)}, f32[16,24,384]{2,1,0:T(8,128)S(1)}, u32[]{:S(2)}, u32[]{:S(2)}) %collective-permute-start.2) | collective-permute-done | bytes 589856 | tf_op jit(solution)/shard_map/ppermute | solution.py:25
  44.3 0.0 copy-start.2
  44.3 7.9 %collective-permute-done.3.right_ref = f32[16,24,384]{2,1,0:T(8,128)S(1)} collective-permute-done((f32[16,24,384]{2,1,0:T(8,128)}, f32[16,24,384]{2,1,0:T(8,128)S(1)}, u32[]{:S(2)}, u32[]{:S(2)}) %collective-permute-start.3) | collective-permute-done | bytes 589856 | tf_op jit(solution)/shard_map/ppermute | solution.py:26
  52.2 0.0 copy-start.3
  52.2 0.0 copy-done.2
  52.2 0.8 copy-done.3
  53.0 7.5 %shard_map.38 = bf16[32,24,384]{2,1,0:T(8,128)(2,1)} custom-call(f32[16,24,384]{2,1,0:T(8,128)} %copy-done.2, f32[32,24,384]{2,1,0:T(8,128)} %get-tuple-element.9.mid_ref, f32[16,24,384]{2,1,0:T(8,128)} %copy-done.3, f32[32,24,384]{2,1,0:T(8,128)} %reshape.31.mid_ref.psi_ref, f32[24,384]{1,0:T(8,128)} %reshape.33.pot_ref), custom_call_target="tpu_custom_call" | custom-call | tf_op jit(solution)/shard_map/pallas_call | solution.py:109
  60.5 2.2 %reshape.34 = bf16[32,32,288]{2,1,0:T(8,128)(2,1)S(1)} reshape(bf16[32,24,384]{2,1,0:T(8,128)(2,1)} %shard_map.38) | data formatting | bytes 1179648 | tf_op jit(solution)/shard_map/reshape | solution.py:134
  62.8 1.1 copy.10
  63.9 2.6 %reshape.35 = bf16[32,24,384]{2,1,0:T(8,128)(2,1)S(1)} reshape(bf16[32,32,288]{2,1,0:T(8,128)(2,1)} %bitcast.8) | data formatting | bytes 1179648 | tf_op jit(solution)/shard_map/reshape | solution.py:136
  66.5 47.1 %all_to_all.10 = bf16[32,24,384]{2,1,0:T(8,128)(2,1)S(1)} all-to-all(bf16[32,24,384]{2,1,0:T(8,128)(2,1)S(1)} %reshape.35), channel_id=1, replica_groups=mesh['dom'=16,'band'=32] {'band'}, dimensions={0} | all-to-all | bytes 1179648 | tf_op jit(solution)/shard_map/all_to_all | solution.py:136
  113.6 1.1 reshape.36
  114.7 0.0 copy-done
  114.7 0.8 fusion
  115.6 0.4 copy.7
  115.9 1.4 reshape.37
  117.3 38.8 %all_to_all.11 = bf16[32,24,384]{2,1,0:T(8,128)(2,1)} all-to-all(bf16[32,24,384]{2,1,0:T(8,128)(2,1)S(1)} %reshape.37), channel_id=1, replica_groups=mesh['dom'=16,'band'=32] {'band'}, dimensions={0} | all-to-all | bytes 1179648 | tf_op jit(solution)/shard_map/all_to_all | solution.py:143
  156.0 2.2 %reshape.38 = bf16[32,32,288]{2,1,0:T(8,128)(2,1)S(1)} reshape(bf16[32,24,384]{2,1,0:T(8,128)(2,1)} %all_to_all.11) | data formatting | bytes 1179648 | tf_op jit(solution)/shard_map/reshape | solution.py:144
  158.3 1.1 copy.8
  159.4 3.5 %reshape.39 = bf16[32,12,2,384]{3,2,1,0:T(2,128)(2,1)} reshape(bf16[32,32,288]{2,1,0:T(8,128)(2,1)} %copy.8) | data formatting | bytes 1179648 | tf_op jit(solution)/shard_map/reshape | solution.py:145
Async XLA Ops:
  0.0 114.7 %copy-start = (bf16[1024,1024]{1,0:T(8,128)(2,1)S(1)}, bf16[1024,1024]{1,0:T(8,128)(2,1)}, u32[]{:S(2)}) copy-start(bf16[1024,1024]{1,0:T(8,128)(2,1)} %param.5) | copy-start | bytes 6291460
  2.8 11.6 %copy-start.1 = (f32[32,12,2,384]{3,2,1,0:T(2,128)S(1)}, f32[32,12,2,384]{3,2,1,0:T(2,128)}, u32[]{:S(2)}) copy-start(f32[32,12,2,384]{3,2,1,0:T(2,128)} %param.3) | copy-start | bytes 3538948
  5.2 12.0 %collective-permute-start = (f32[16,24,384]{2,1,0:T(8,128)}, f32[16,24,384]{2,1,0:T(8,128)}, u32[]{:S(2)}, u32[]{:S(2)}) collective-permute-start(f32[16,24,384]{2,1,0:T(8,128)} %reshape.30), channel_id=1, source_target_pairs={{0,32},{32,64},{64,96},{96,128},{128,160},{160,192},{192,224},{224... | collective-permute-start | bytes 1769480 | tf_op jit(solution)/shard_map/ppermute | solution.py:25
  12.4 3.9 %copy-start.4 = (f32[12,2,384]{2,1,0:T(2,128)S(1)}, f32[12,2,384]{2,1,0:T(2,128)}, u32[]{:S(2)}) copy-start(f32[12,2,384]{2,1,0:T(2,128)} %param.4) | copy-start | bytes 110596
  12.4 15.3 %collective-permute-start.1 = (f32[16,24,384]{2,1,0:T(8,128)}, f32[16,24,384]{2,1,0:T(8,128)}, u32[]{:S(2)}, u32[]{:S(2)}) collective-permute-start(f32[16,24,384]{2,1,0:T(8,128)} %reshape.32), channel_id=1, source_target_pairs={{32,0},{64,32},{96,64},{128,96},{160,128},{192,160},{224,192},{256... | collective-permute-start | bytes 1769480 | tf_op jit(solution)/shard_map/ppermute | solution.py:26
  35.3 9.0 %collective-permute-start.2 = (f32[16,24,384]{2,1,0:T(8,128)}, f32[16,24,384]{2,1,0:T(8,128)S(1)}, u32[]{:S(2)}, u32[]{:S(2)}) collective-permute-start(f32[16,24,384]{2,1,0:T(8,128)} %get-tuple-element.8), channel_id=1, source_target_pairs={{0,32},{32,64},{64,96},{96,128},{128,160},{160,192},{192,224},{224... | collective-permute-start | bytes 1769480 | tf_op jit(solution)/shard_map/ppermute | solution.py:25
  37.2 15.0 %collective-permute-start.3 = (f32[16,24,384]{2,1,0:T(8,128)}, f32[16,24,384]{2,1,0:T(8,128)S(1)}, u32[]{:S(2)}, u32[]{:S(2)}) collective-permute-start(f32[16,24,384]{2,1,0:T(8,128)} %get-tuple-element.10), channel_id=1, source_target_pairs={{32,0},{64,32},{96,64},{128,96},{160,128},{192,160},{224,192},{256... | collective-permute-start | bytes 1769480 | tf_op jit(solution)/shard_map/ppermute | solution.py:26
  44.3 7.9 %copy-start.2 = (f32[16,24,384]{2,1,0:T(8,128)}, f32[16,24,384]{2,1,0:T(8,128)S(1)}, u32[]{:S(2)}) copy-start(f32[16,24,384]{2,1,0:T(8,128)S(1)} %collective-permute-done.2.left_ref) | copy-start | bytes 1769476
  52.2 0.8 copy-start.3

commit v3 on v1

--- a/solution.py
+++ b/solution.py
@@ -22,8 +22,17 @@
 
 def swap_rims(head, tail):
     count = lax.axis_size("dom")
-    left = lax.ppermute(tail, "dom", [(i, (i + 1) % count) for i in range(count)])
-    right = lax.ppermute(head, "dom", [((i + 1) % count, i) for i in range(count)])
+    if count % 2:
+        left = lax.ppermute(tail, "dom", [(i, (i + 1) % count) for i in range(count)])
+        right = lax.ppermute(head, "dom", [((i + 1) % count, i) for i in range(count)])
+        return left, right
+    even = lax.axis_index("dom") % 2 == 0
+    inner = [(i, i + 1) if i % 2 == 0 else (i, i - 1) for i in range(count)]
+    outer = [(i, (i - 1) % count) if i % 2 == 0 else (i, (i + 1) % count) for i in range(count)]
+    got_inner = lax.ppermute(jnp.where(even, tail, head), "dom", inner)
+    got_outer = lax.ppermute(jnp.where(even, head, tail), "dom", outer)
+    left = jnp.where(even, got_outer, got_inner)
+    right = jnp.where(even, got_inner, got_outer)
     return left, right
 
 

time: 163 us -> 163 us (level)
  waiting for transfers between devices: 25.1 us -> 16.6 us
  other arithmetic: 0 us -> 4.89 us
  blocking collectives: 85.9 us -> 90 us
  local copies, waits for them, and re-layouts: 24.8 us -> 21.7 us
  starting transfers between devices: 11.1 us -> 13.6 us
    ppermute x4, waiting for transfers between devices: 25.1 us -> 16.6 us  [the longest x2 16.6 us: swap_rims(): got_outer = lax.ppermute(jnp.where(even, head, tail), 'dom', outer)]
    select_n x0 -> x4, other arithmetic: none -> 4.89 us  [the longest x2 2.68 us: swap_rims(): got_inner = lax.ppermute(jnp.where(even, tail, head), 'dom', inner)]
    reshape x2 -> x0, local copies, waits for them, and re-layouts: 2.98 us -> none  [the longest x1 2.08 us: per_device(): psi_rows[:, rows - halo:].reshape(pairs)]
    select_n x0 -> x2, local copies, waits for them, and re-layouts: none -> 2.97 us  [the longest x1 2.09 us: swap_rims(): got_outer = lax.ppermute(jnp.where(even, head, tail), 'dom', outer)]
    all_to_all x1, blocking collectives: 47.1 us -> 49.8 us  [per_device(): gathered = lax.all_to_all(blocks.reshape(wire), 'band', 0, 0, tiled=True)]
    ppermute x4, starting transfers between devices: 11.1 us -> 13.6 us  [the longest x2 9.73 us: swap_rims(): got_outer = lax.ppermute(jnp.where(even, head, tail), 'dom', outer)]
    unnamed x16 -> x8, local copies, waits for them, and re-layouts: 1.88 us -> 0.17 us
  transfers between devices with their start and end apart: 4 -> 4, of which waited for: 4 -> 2; matrix products, arithmetic and copies ran while one was open for 1% -> 1% of each run, Pallas kernels for 0% -> 0%
where the time goes in v3:
time: 163 us
  blocking collectives  90 us (55%)
  local copies, waits for them, and re-layouts  21.7 us (13%)
  waiting for transfers between devices  16.6 us (10%)
  Pallas kernels  15.2 us (9%)
  starting transfers between devices  13.6 us (8%)
  other arithmetic  4.89 us (3%)
    all_to_all x1, blocking collectives, per_device(): gathered = lax.all_to_all(blocks.reshape(wire), 'band', 0, 0, tiled=True)  49.8 us
    all_to_all x1, blocking collectives, per_device(): back = lax.all_to_all(mixed.reshape(wire), 'band', 0, 0, tiled=True)  40.2 us
    ppermute x2, waiting for transfers between devices, swap_rims(): got_outer = lax.ppermute(jnp.where(even, head, tail), 'dom', outer)  16.6 us
    ppermute x2, starting transfers between devices, swap_rims(): got_outer = lax.ppermute(jnp.where(even, head, tail), 'dom', outer)  9.73 us
    pallas_call x1, Pallas kernels, run_first(): pl.pallas_call(first_kernel, grid=(states // sb,), in_specs=[rim, body, r...  7.68 us
    pallas_call x1, Pallas kernels, run_second(): pl.pallas_call(second_kernel, grid=(states // sb,), in_specs=[rim, body,...  7.5 us
    ppermute x2, starting transfers between devices, swap_rims(): got_inner = lax.ppermute(jnp.where(even, tail, head), 'dom', inner)  3.83 us
    reshape x1, local copies, waits for them, and re-layouts, per_device(): return result.reshape(psi.shape)  3.52 us
  transfers between devices with their start and end apart: 4, of which 2 were waited for; matrix products, arithmetic and copies ran while one was open for 1% of the time, Pallas kernels for 0%

profile of v3, /device:TPU:25, one launch (start us, length us, event | category | flops | bytes accessed | tf_op | source)
XLA Modules:
  0.0 162.9 jit_solution(7674715360779367544)
XLA Ops:
  0.0 0.0 copy-start
  0.0 2.2 %reshape.30.mid_ref.psi_ref = f32[32,24,384]{2,1,0:T(8,128)S(1)} reshape(f32[32,12,2,384]{3,2,1,0:T(2,128)} %param.3) | data formatting | bytes 2359296 | tf_op jit(solution)/shard_map/reshape | solution.py:132
  2.2 0.0 copy-start.1
  2.3 1.4 slice_select_fusion
  3.6 0.2 copy-done.1
  3.8 0.0 copy-start.2
  3.8 0.0 copy-start.3
  3.8 2.1 %select_n.57 = f32[16,24,384]{2,1,0:T(8,128)} reshape(f32[32,12,384]{2,1,0:T(8,128)} %get-tuple-element.18) | data formatting | bytes 1179648 | tf_op jit(solution)/shard_map/jit(_where)/select_n | solution.py:33
  5.9 4.9 %collective-permute-start = (f32[16,24,384]{2,1,0:T(8,128)}, f32[16,24,384]{2,1,0:T(8,128)S(1)}, u32[]{:S(2)}, u32[]{:S(2)}) collective-permute-start(f32[16,24,384]{2,1,0:T(8,128)} %select_n.57), channel_id=1, source_target_pairs={{0,480},{32,64},{64,32},{96,128},{128,96},{160,192},{192,160},{224... | collective-permute-start | bytes 1769480 | tf_op jit(solution)/shard_map/ppermute | solution.py:33
  10.7 0.0 copy-done.2
  10.7 0.9 select_n.59
  11.6 1.9 %collective-permute-start.1 = (f32[16,24,384]{2,1,0:T(8,128)}, f32[16,24,384]{2,1,0:T(8,128)S(1)}, u32[]{:S(2)}, u32[]{:S(2)}) collective-permute-start(f32[16,24,384]{2,1,0:T(8,128)} %select_n.59), channel_id=1, source_target_pairs={{0,32},{32,0},{64,96},{96,64},{128,160},{160,128},{192,224},{224,1... | collective-permute-start | bytes 1769480 | tf_op jit(solution)/shard_map/ppermute | solution.py:32
  13.5 0.0 copy-done.3
  13.6 0.6 reshape.31.pot_ref
  14.2 6.7 %collective-permute-done = f32[16,24,384]{2,1,0:T(8,128)S(1)} collective-permute-done((f32[16,24,384]{2,1,0:T(8,128)}, f32[16,24,384]{2,1,0:T(8,128)S(1)}, u32[]{:S(2)}, u32[]{:S(2)}) %collective-permute-start) | collective-permute-done | bytes 589856 | tf_op jit(solution)/shard_map/ppermute | solution.py:33
  20.9 0.0 collective-permute-done.1
  20.9 1.1 broadcast_select_fusion.4
  22.0 7.7 %shard_map.37 = (f32[32,24,384]{2,1,0:T(8,128)}, f32[16,24,384]{2,1,0:T(8,128)}, f32[16,24,384]{2,1,0:T(8,128)}) custom-call(f32[16,24,384]{2,1,0:T(8,128)} %get-tuple-element.16.left_ref, f32[32,24,384]{2,1,0:T(8,128)} %copy-done.1, f32[16,24,384]{2,1,0:T(8,128)} %get-tuple-element.15.right_ref, f32[24,384]{1,0:T(8,128)} %reshape.31.pot_ref), custom_call_target="tpu_custom_call" | custom-call | tf_op jit(solution)/shard_map/pallas_call | solution.py:98
  29.7 1.3 broadcast_select_fusion.2
  31.0 1.9 %collective-permute-start.3 = (f32[16,24,384]{2,1,0:T(8,128)S(1)}, f32[16,24,384]{2,1,0:T(8,128)S(1)}, u32[]{:S(2)}, u32[]{:S(2)}) collective-permute-start(f32[16,24,384]{2,1,0:T(8,128)S(1)} %get-tuple-element.13), channel_id=1, source_target_pairs={{0,32},{32,0},{64,96},{96,64},{128,160},{160,128},{192,224},{224,1... | collective-permute-start | bytes 1769480 | tf_op jit(solution)/shard_map/ppermute | solution.py:32
  32.9 4.9 %collective-permute-start.2 = (f32[16,24,384]{2,1,0:T(8,128)S(1)}, f32[16,24,384]{2,1,0:T(8,128)S(1)}, u32[]{:S(2)}, u32[]{:S(2)}) collective-permute-start(f32[16,24,384]{2,1,0:T(8,128)S(1)} %get-tuple-element.14), channel_id=1, source_target_pairs={{0,480},{32,64},{64,32},{96,128},{128,96},{160,192},{192,160},{224... | collective-permute-start | bytes 1769480 | tf_op jit(solution)/shard_map/ppermute | solution.py:33
  37.8 0.0 collective-permute-done.3
  37.8 9.9 %collective-permute-done.2 = f32[16,24,384]{2,1,0:T(8,128)S(1)} collective-permute-done((f32[16,24,384]{2,1,0:T(8,128)S(1)}, f32[16,24,384]{2,1,0:T(8,128)S(1)}, u32[]{:S(2)}, u32[]{:S(2)}) %collective-permute-start.2) | collective-permute-done | bytes 589856 | tf_op jit(solution)/shard_map/ppermute | solution.py:33
  47.7 1.1 broadcast_select_fusion
  48.9 7.5 %shard_map.38 = bf16[32,24,384]{2,1,0:T(8,128)(2,1)} custom-call(f32[16,24,384]{2,1,0:T(8,128)} %get-tuple-element.12.left_ref, f32[32,24,384]{2,1,0:T(8,128)} %get-tuple-element.10.mid_ref, f32[16,24,384]{2,1,0:T(8,128)} %get-tuple-element.11.right_ref, f32[32,24,384]{2,1,0:T(8,128)} %copy-done.1, f32[24,384]{1,0:T(8,128)} %reshape.31.pot_ref), custom_call_target="tpu_custom_call" | custom-call | tf_op jit(solution)/shard_map/pallas_call | solution.py:118
  56.4 2.2 %reshape.32 = bf16[32,32,288]{2,1,0:T(8,128)(2,1)S(1)} reshape(bf16[32,24,384]{2,1,0:T(8,128)(2,1)} %shard_map.38) | data formatting | bytes 1179648 | tf_op jit(solution)/shard_map/reshape | solution.py:143
  58.6 1.1 copy.10
  59.7 2.6 %reshape.33 = bf16[32,24,384]{2,1,0:T(8,128)(2,1)S(1)} reshape(bf16[32,32,288]{2,1,0:T(8,128)(2,1)} %bitcast.8) | data formatting | bytes 1179648 | tf_op jit(solution)/shard_map/reshape | solution.py:145
  62.3 49.8 %all_to_all.10 = bf16[32,24,384]{2,1,0:T(8,128)(2,1)S(1)} all-to-all(bf16[32,24,384]{2,1,0:T(8,128)(2,1)S(1)} %reshape.33), channel_id=1, replica_groups=mesh['dom'=16,'band'=32] {'band'}, dimensions={0} | all-to-all | bytes 1179648 | tf_op jit(solution)/shard_map/all_to_all | solution.py:145
  112.1 1.1 reshape.34
  113.3 0.0 copy-done
  113.3 0.8 fusion
  114.1 0.4 copy.7
  114.4 1.4 reshape.35
  115.8 40.2 %all_to_all.11 = bf16[32,24,384]{2,1,0:T(8,128)(2,1)} all-to-all(bf16[32,24,384]{2,1,0:T(8,128)(2,1)S(1)} %reshape.35), channel_id=1, replica_groups=mesh['dom'=16,'band'=32] {'band'}, dimensions={0} | all-to-all | bytes 1179648 | tf_op jit(solution)/shard_map/all_to_all | solution.py:152
  156.0 2.2 %reshape.36 = bf16[32,32,288]{2,1,0:T(8,128)(2,1)S(1)} reshape(bf16[32,24,384]{2,1,0:T(8,128)(2,1)} %all_to_all.11) | data formatting | bytes 1179648 | tf_op jit(solution)/shard_map/reshape | solution.py:153
  158.2 1.1 copy.8
  159.4 3.5 %reshape.37 = bf16[32,12,2,384]{3,2,1,0:T(2,128)(2,1)} reshape(bf16[32,32,288]{2,1,0:T(8,128)(2,1)} %copy.8) | data formatting | bytes 1179648 | tf_op jit(solution)/shard_map/reshape | solution.py:154
Async XLA Ops:
  0.0 113.3 %copy-start = (bf16[1024,1024]{1,0:T(8,128)(2,1)S(1)}, bf16[1024,1024]{1,0:T(8,128)(2,1)}, u32[]{:S(2)}) copy-start(bf16[1024,1024]{1,0:T(8,128)(2,1)} %param.5) | copy-start | bytes 6291460
  2.2 1.5 copy-start.1
  3.8 7.0 %copy-start.2 = (f32[32,12,384]{2,1,0:T(8,128)S(1)}, f32[32,12,384]{2,1,0:T(8,128)}, u32[]{:S(2)}) copy-start(f32[32,12,384]{2,1,0:T(8,128)} %get-tuple-element.17) | copy-start | bytes 1769476
  3.8 9.8 %copy-start.3 = (f32[12,2,384]{2,1,0:T(2,128)S(1)}, f32[12,2,384]{2,1,0:T(2,128)}, u32[]{:S(2)}) copy-start(f32[12,2,384]{2,1,0:T(2,128)} %param.4) | copy-start | bytes 110596
  5.9 15.0 %collective-permute-start = (f32[16,24,384]{2,1,0:T(8,128)}, f32[16,24,384]{2,1,0:T(8,128)S(1)}, u32[]{:S(2)}, u32[]{:S(2)}) collective-permute-start(f32[16,24,384]{2,1,0:T(8,128)} %select_n.57), channel_id=1, source_target_pairs={{0,480},{32,64},{64,32},{96,128},{128,96},{160,192},{192,160},{224... | collective-permute-start | bytes 1769480 | tf_op jit(solution)/shard_map/ppermute | solution.py:33
  11.6 9.3 %collective-permute-start.1 = (f32[16,24,384]{2,1,0:T(8,128)}, f32[16,24,384]{2,1,0:T(8,128)S(1)}, u32[]{:S(2)}, u32[]{:S(2)}) collective-permute-start(f32[16,24,384]{2,1,0:T(8,128)} %select_n.59), channel_id=1, source_target_pairs={{0,32},{32,0},{64,96},{96,64},{128,160},{160,128},{192,224},{224,1... | collective-permute-start | bytes 1769480 | tf_op jit(solution)/shard_map/ppermute | solution.py:32
  31.0 6.8 %collective-permute-start.3 = (f32[16,24,384]{2,1,0:T(8,128)S(1)}, f32[16,24,384]{2,1,0:T(8,128)S(1)}, u32[]{:S(2)}, u32[]{:S(2)}) collective-permute-start(f32[16,24,384]{2,1,0:T(8,128)S(1)} %get-tuple-element.13), channel_id=1, source_target_pairs={{0,32},{32,0},{64,96},{96,64},{128,160},{160,128},{192,224},{224,1... | collective-permute-start | bytes 1769480 | tf_op jit(solution)/shard_map/ppermute | solution.py:32
  32.9 14.8 %collective-permute-start.2 = (f32[16,24,384]{2,1,0:T(8,128)S(1)}, f32[16,24,384]{2,1,0:T(8,128)S(1)}, u32[]{:S(2)}, u32[]{:S(2)}) collective-permute-start(f32[16,24,384]{2,1,0:T(8,128)S(1)} %get-tuple-element.14), channel_id=1, source_target_pairs={{0,480},{32,64},{64,32},{96,128},{128,96},{160,192},{192,160},{224... | collective-permute-start | bytes 1769480 | tf_op jit(solution)/shard_map/ppermute | solution.py:33

commit v4 on v3

--- a/solution.py
+++ b/solution.py
@@ -131,13 +131,24 @@
     halo = 2 * reach
     psi_rows = psi.reshape(own_states, rows, ny)
     pot_rows = potential.reshape(rows, ny)
-    pairs = (own_states // 2, 2 * halo, ny)
-    left, right = swap_rims(
-        psi_rows[:, :halo].reshape(pairs), psi_rows[:, rows - halo :].reshape(pairs)
+    groups = own_states // (2 * state_block) if own_states % (2 * state_block) == 0 else 1
+    size = own_states // groups
+    pieces = []
+    for g in range(groups):
+        part = psi_rows[g * size : (g + 1) * size]
+        pairs = (size // 2, 2 * halo, ny)
+        left, right = swap_rims(
+            part[:, :halo].reshape(pairs), part[:, rows - halo :].reshape(pairs)
+        )
+        pieces.append((part, left, right))
+    firsts = []
+    for part, left, right in pieces:
+        first, head, tail = run_first(left, part, right, pot_rows)
+        firsts.append((part, first, swap_rims(head, tail)))
+    filtered = jnp.concatenate(
+        [run_second(left, first, right, part, pot_rows) for part, first, (left, right) in firsts],
+        axis=0,
     )
-    first, head, tail = run_first(left, psi_rows, right, pot_rows)
-    left, right = swap_rims(head, tail)
-    filtered = run_second(left, first, right, psi_rows, pot_rows)
     count = lax.axis_size("band")
     chunk = rows * ny // count
     blocks = filtered.reshape(own_states, count, chunk).transpose(1, 0, 2)

time: 163 us -> 177 us (1.086)
  waiting for transfers between devices: 16.6 us -> 0.95 us
  starting transfers between devices: 13.6 us -> 26.6 us
  other arithmetic: 4.89 us -> 13.9 us
  Pallas kernels: 15.2 us -> 18.9 us
  local copies, waits for them, and re-layouts: 21.7 us -> 25 us
    ppermute x2 -> x4, waiting for transfers between devices: 16.6 us -> 0.94 us  [swap_rims(): got_outer = lax.ppermute(jnp.where(even, head, tail), 'dom', outer)]
    ppermute x2 -> x4, starting transfers between devices: 9.73 us -> 18.3 us  [swap_rims(): got_outer = lax.ppermute(jnp.where(even, head, tail), 'dom', outer)]
    select_n x2 -> x4, other arithmetic: 2.21 us -> 7.39 us  [swap_rims(): right = jnp.where(even, got_inner, got_outer)]
    slice x0 -> x3, local copies, waits for them, and re-layouts: none -> 4.49 us  [per_device(): part = psi_rows[g * size:(g + 1) * size]]
    ppermute x2 -> x4, starting transfers between devices: 3.83 us -> 8.25 us  [swap_rims(): got_inner = lax.ppermute(jnp.where(even, tail, head), 'dom', inner)]
    select_n x2 -> x4, other arithmetic: 2.68 us -> 5.51 us  [swap_rims(): got_inner = lax.ppermute(jnp.where(even, tail, head), 'dom', inner)]
    reshape x1 -> x0, local copies, waits for them, and re-layouts: 2.24 us -> none  [per_device(): psi_rows = psi.reshape(own_states, rows, ny)]
    pallas_call x1 -> x2, Pallas kernels: 7.68 us -> 9.54 us  [run_first(): pl.pallas_call(first_kernel, grid=(states // sb,), in_specs=[rim, body, r...]
  transfers between devices with their start and end apart: 4 -> 8, of which waited for: 2 -> 1; matrix products, arithmetic and copies ran while one was open for 1% -> 9% of each run, Pallas kernels for 0% -> 8%
where the time goes in v4:
time: 177 us; the launch traced here: 176 us
  blocking collectives  89.5 us (51%)
  starting transfers between devices  26.6 us (15%)
  local copies, waits for them, and re-layouts  25 us (14%)
  Pallas kernels  18.9 us (11%)
  other arithmetic  13.9 us (8%)
    all_to_all x1, blocking collectives, per_device(): gathered = lax.all_to_all(blocks.reshape(wire), 'band', 0, 0, tiled=True)  49.3 us
    all_to_all x1, blocking collectives, per_device(): back = lax.all_to_all(mixed.reshape(wire), 'band', 0, 0, tiled=True)  40.2 us
    ppermute x4, starting transfers between devices, swap_rims(): got_outer = lax.ppermute(jnp.where(even, head, tail), 'dom', outer)  18.3 us
    pallas_call x2, Pallas kernels, run_first(): pl.pallas_call(first_kernel, grid=(states // sb,), in_specs=[rim, body, r...  9.54 us
    pallas_call x2, Pallas kernels, run_second(): pl.pallas_call(second_kernel, grid=(states // sb,), in_specs=[rim, body,...  9.33 us
    ppermute x4, starting transfers between devices, swap_rims(): got_inner = lax.ppermute(jnp.where(even, tail, head), 'dom', inner)  8.25 us
    select_n x4, other arithmetic, swap_rims(): right = jnp.where(even, got_inner, got_outer)  7.39 us
    select_n x4, other arithmetic, swap_rims(): got_inner = lax.ppermute(jnp.where(even, tail, head), 'dom', inner)  5.51 us
  transfers between devices with their start and end apart: 8, of which 1 were waited for; matrix products, arithmetic and copies ran while one was open for 9% of the time, Pallas kernels for 8%

profile of v4, /device:TPU:25, one launch (start us, length us, event | category | flops | bytes accessed | tf_op | source)
XLA Modules:
  0.0 175.8 jit_solution(13998817495004941702)
XLA Ops:
  0.0 0.0 copy-start
  0.0 2.6 %fusion.1 = (f32[16,12,2,384]{3,2,1,0:T(2,128)}, f32[16,12,2,384]{3,2,1,0:T(2,128)S(1)}) fusion(f32[32,12,2,384]{3,2,1,0:T(2,128)} %param.3), kind=kLoop, calls=%fused_computation.20 | loop fusion | bytes 2359296 | tf_op jit(solution)/shard_map/slice | solution.py:138
  2.6 0.4 slice.29.mid_ref.psi_ref
  3.0 0.0 copy-start.2
  3.0 0.9 slice_select_fusion
  3.9 1.7 select_n.109
  5.7 4.9 %collective-permute-start.4 = (f32[8,24,384]{2,1,0:T(8,128)}, f32[8,24,384]{2,1,0:T(8,128)}, u32[]{:S(2)}, u32[]{:S(2)}) collective-permute-start(f32[8,24,384]{2,1,0:T(8,128)} %select_n.109), channel_id=1, source_target_pairs={{0,480},{32,64},{64,32},{96,128},{128,96},{160,192},{192,160},{224... | collective-permute-start | bytes 884744 | tf_op jit(solution)/shard_map/ppermute | solution.py:33
  10.5 0.8 select_n.111
  11.3 0.0 copy-start.4
  11.3 2.0 %collective-permute-start.5 = (f32[8,24,384]{2,1,0:T(8,128)}, f32[8,24,384]{2,1,0:T(8,128)}, u32[]{:S(2)}, u32[]{:S(2)}) collective-permute-start(f32[8,24,384]{2,1,0:T(8,128)} %select_n.111), channel_id=1, source_target_pairs={{0,32},{32,0},{64,96},{96,64},{128,160},{160,128},{192,224},{224,1... | collective-permute-start | bytes 884744 | tf_op jit(solution)/shard_map/ppermute | solution.py:32
  13.4 1.5 slice.25.mid_ref.psi_ref
  14.8 0.0 copy-start.1
  14.8 1.0 slice_select_fusion.2
  15.8 0.0 copy-done.2
  15.8 1.0 select_n.99
  16.9 4.3 %collective-permute-start = (f32[8,24,384]{2,1,0:T(8,128)S(1)}, f32[8,24,384]{2,1,0:T(8,128)S(1)}, u32[]{:S(2)}, u32[]{:S(2)}) collective-permute-start(f32[8,24,384]{2,1,0:T(8,128)S(1)} %select_n.99), channel_id=1, source_target_pairs={{0,480},{32,64},{64,32},{96,128},{128,96},{160,192},{192,160},{224... | collective-permute-start | bytes 884744 | tf_op jit(solution)/shard_map/ppermute | solution.py:33
  21.2 1.7 select_n.101
  22.9 1.9 %collective-permute-start.1 = (f32[8,24,384]{2,1,0:T(8,128)}, f32[8,24,384]{2,1,0:T(8,128)}, u32[]{:S(2)}, u32[]{:S(2)}) collective-permute-start(f32[8,24,384]{2,1,0:T(8,128)} %select_n.101), channel_id=1, source_target_pairs={{0,32},{32,0},{64,96},{96,64},{128,160},{160,128},{192,224},{224,1... | collective-permute-start | bytes 884744 | tf_op jit(solution)/shard_map/ppermute | solution.py:32
  24.8 0.0 copy-done.4
  24.9 0.6 reshape.36.pot_ref
  25.5 0.0 collective-permute-done.4
  25.5 0.0 collective-permute-done.5
  25.5 1.9 %broadcast_select_fusion.4 = (f32[8,24,384]{2,1,0:T(8,128)}, f32[8,24,384]{2,1,0:T(8,128)}) fusion(f32[8,24,384]{2,1,0:T(8,128)} %collective-permute-done.5, f32[8,24,384]{2,1,0:T(8,128)} %collective-permute-done.4, pred[]{:T(512)S(6)} %eq.11), kind=kLoop, calls=%fused_computation.12 | loop fusion | flops 147456 | bytes 1179649 | tf_op jit(solution)/shard_map/jit(_where)/select_n | solution.py:35
  27.4 0.0 copy-done.1
  27.4 4.8 %shard_map.39 = (f32[16,24,384]{2,1,0:T(8,128)}, f32[8,24,384]{2,1,0:T(8,128)}, f32[8,24,384]{2,1,0:T(8,128)}) custom-call(f32[8,24,384]{2,1,0:T(8,128)} %get-tuple-element.32.left_ref, f32[16,24,384]{2,1,0:T(8,128)} %copy-done.2, f32[8,24,384]{2,1,0:T(8,128)} %get-tuple-element.31.right_ref, f32[24,384]{1,0:T(8,128)} %reshape.36.pot_ref), custom_call_target="tpu_custom_call" | custom-call | tf_op jit(solution)/shard_map/pallas_call | solution.py:98
  32.2 1.8 %broadcast_select_fusion.2 = (f32[8,24,384]{2,1,0:T(8,128)}, f32[8,24,384]{2,1,0:T(8,128)S(1)}) fusion(f32[8,24,384]{2,1,0:T(8,128)} %get-tuple-element.15, f32[8,24,384]{2,1,0:T(8,128)} %get-tuple-element.14, pred[]{:T(512)S(6)} %eq.11), kind=kLoop, calls=%fused_computation.10 | loop fusion | flops 147456 | bytes 1179649 | tf_op jit(solution)/shard_map/jit(_where)/select_n | solution.py:32
  34.0 2.4 %collective-permute-start.7 = (f32[8,24,384]{2,1,0:T(8,128)}, f32[8,24,384]{2,1,0:T(8,128)S(1)}, u32[]{:S(2)}, u32[]{:S(2)}) collective-permute-start(f32[8,24,384]{2,1,0:T(8,128)} %get-tuple-element.29), channel_id=1, source_target_pairs={{0,32},{32,0},{64,96},{96,64},{128,160},{160,128},{192,224},{224,1... | collective-permute-start | bytes 884744 | tf_op jit(solution)/shard_map/ppermute | solution.py:32
  36.4 4.9 %collective-permute-start.6 = (f32[8,24,384]{2,1,0:T(8,128)S(1)}, f32[8,24,384]{2,1,0:T(8,128)}, u32[]{:S(2)}, u32[]{:S(2)}) collective-permute-start(f32[8,24,384]{2,1,0:T(8,128)S(1)} %get-tuple-element.30), channel_id=1, source_target_pairs={{0,480},{32,64},{64,32},{96,128},{128,96},{160,192},{192,160},{224... | collective-permute-start | bytes 884744 | tf_op jit(solution)/shard_map/ppermute | solution.py:33
  41.3 0.0 collective-permute-done
  41.3 0.0 collective-permute-done.1
  41.3 1.8 %broadcast_select_fusion.10 = (f32[8,24,384]{2,1,0:T(8,128)}, f32[8,24,384]{2,1,0:T(8,128)}) fusion(f32[8,24,384]{2,1,0:T(8,128)} %collective-permute-done.1, f32[8,24,384]{2,1,0:T(8,128)S(1)} %collective-permute-done, pred[]{:T(512)S(6)} %eq.11), kind=kLoop, calls=%fused_computation.18 | loop fusion | flops 147456 | bytes 1179649 | tf_op jit(solution)/shard_map/jit(_where)/select_n | solution.py:35
  43.1 4.8 %shard_map.37 = (f32[16,24,384]{2,1,0:T(8,128)}, f32[8,24,384]{2,1,0:T(8,128)}, f32[8,24,384]{2,1,0:T(8,128)}) custom-call(f32[8,24,384]{2,1,0:T(8,128)} %get-tuple-element.24.left_ref, f32[16,24,384]{2,1,0:T(8,128)} %copy-done.1, f32[8,24,384]{2,1,0:T(8,128)} %get-tuple-element.23.right_ref, f32[24,384]{1,0:T(8,128)} %reshape.36.pot_ref), custom_call_target="tpu_custom_call" | custom-call | tf_op jit(solution)/shard_map/pallas_call | solution.py:98
  47.9 1.8 %broadcast_select_fusion.8 = (f32[8,24,384]{2,1,0:T(8,128)}, f32[8,24,384]{2,1,0:T(8,128)S(1)}) fusion(f32[8,24,384]{2,1,0:T(8,128)} %get-tuple-element.12, f32[8,24,384]{2,1,0:T(8,128)} %get-tuple-element.11, pred[]{:T(512)S(6)} %eq.11), kind=kLoop, calls=%fused_computation.16 | loop fusion | flops 147456 | bytes 1179649 | tf_op jit(solution)/shard_map/jit(_where)/select_n | solution.py:32
  49.7 1.9 %collective-permute-start.3 = (f32[8,24,384]{2,1,0:T(8,128)}, f32[8,24,384]{2,1,0:T(8,128)S(1)}, u32[]{:S(2)}, u32[]{:S(2)}) collective-permute-start(f32[8,24,384]{2,1,0:T(8,128)} %get-tuple-element.21), channel_id=1, source_target_pairs={{0,32},{32,0},{64,96},{96,64},{128,160},{160,128},{192,224},{224,1... | collective-permute-start | bytes 884744 | tf_op jit(solution)/shard_map/ppermute | solution.py:32
  51.6 4.3 %collective-permute-start.2 = (f32[8,24,384]{2,1,0:T(8,128)S(1)}, f32[8,24,384]{2,1,0:T(8,128)}, u32[]{:S(2)}, u32[]{:S(2)}) collective-permute-start(f32[8,24,384]{2,1,0:T(8,128)S(1)} %get-tuple-element.22), channel_id=1, source_target_pairs={{0,480},{32,64},{64,32},{96,128},{128,96},{160,192},{192,160},{224... | collective-permute-start | bytes 884744 | tf_op jit(solution)/shard_map/ppermute | solution.py:33
  55.9 0.0 collective-permute-done.7
  56.0 0.0 collective-permute-done.6
  56.0 1.8 %broadcast_select_fusion = (f32[8,24,384]{2,1,0:T(8,128)}, f32[8,24,384]{2,1,0:T(8,128)}) fusion(f32[8,24,384]{2,1,0:T(8,128)S(1)} %collective-permute-done.7, f32[8,24,384]{2,1,0:T(8,128)} %collective-permute-done.6, pred[]{:T(512)S(6)} %eq.11), kind=kLoop, calls=%fused_computation.8 | loop fusion | flops 147456 | bytes 1179649 | tf_op jit(solution)/shard_map/jit(_where)/select_n | solution.py:35
  57.8 4.7 %shard_map.40 = bf16[16,24,384]{2,1,0:T(8,128)(2,1)} custom-call(f32[8,24,384]{2,1,0:T(8,128)} %get-tuple-element.28.left_ref, f32[16,24,384]{2,1,0:T(8,128)} %get-tuple-element.16.mid_ref, f32[8,24,384]{2,1,0:T(8,128)} %get-tuple-element.27.right_ref, f32[16,24,384]{2,1,0:T(8,128)} %copy-done.2, f32[24,384]{1,0:T(8,128)} %reshape.36.pot_ref), custom_call_target="tpu_custom_call" | custom-call | tf_op jit(solution)/shard_map/pallas_call | solution.py:118
  62.4 0.0 copy-start.3
  62.4 0.0 collective-permute-done.3
  62.5 0.9 collective-permute-done.2
  63.4 1.8 %broadcast_select_fusion.6 = (f32[8,24,384]{2,1,0:T(8,128)}, f32[8,24,384]{2,1,0:T(8,128)}) fusion(f32[8,24,384]{2,1,0:T(8,128)S(1)} %collective-permute-done.3, f32[8,24,384]{2,1,0:T(8,128)} %collective-permute-done.2, pred[]{:T(512)S(6)} %eq.11), kind=kLoop, calls=%fused_computation.14 | loop fusion | flops 147456 | bytes 1179649 | tf_op jit(solution)/shard_map/jit(_where)/select_n | solution.py:35
  65.2 4.7 %shard_map.38 = bf16[16,24,384]{2,1,0:T(8,128)(2,1)} custom-call(f32[8,24,384]{2,1,0:T(8,128)} %get-tuple-element.20.left_ref, f32[16,24,384]{2,1,0:T(8,128)} %get-tuple-element.13.mid_ref, f32[8,24,384]{2,1,0:T(8,128)} %get-tuple-element.19.right_ref, f32[16,24,384]{2,1,0:T(8,128)} %copy-done.1, f32[24,384]{1,0:T(8,128)} %reshape.36.pot_ref), custom_call_target="tpu_custom_call" | custom-call | tf_op jit(solution)/shard_map/pallas_call | solution.py:118
  69.9 0.0 copy-done.3
  69.9 1.0 pad_maximum_fusion
  70.9 1.1 reshape.37
  72.0 1.1 copy.10
  73.2 2.6 %reshape.38 = bf16[32,24,384]{2,1,0:T(8,128)(2,1)S(1)} reshape(bf16[32,32,288]{2,1,0:T(8,128)(2,1)} %bitcast.8) | data formatting | bytes 1179648 | tf_op jit(solution)/shard_map/reshape | solution.py:156
  75.8 49.3 %all_to_all.10 = bf16[32,24,384]{2,1,0:T(8,128)(2,1)S(1)} all-to-all(bf16[32,24,384]{2,1,0:T(8,128)(2,1)S(1)} %reshape.38), channel_id=1, replica_groups=mesh['dom'=16,'band'=32] {'band'}, dimensions={0} | all-to-all | bytes 1179648 | tf_op jit(solution)/shard_map/all_to_all | solution.py:156
  125.0 1.1 reshape.39
  126.1 0.0 copy-done
  126.1 0.8 fusion
  127.0 0.4 copy.7
  127.3 1.4 reshape.40
  128.7 40.2 %all_to_all.11 = bf16[32,24,384]{2,1,0:T(8,128)(2,1)} all-to-all(bf16[32,24,384]{2,1,0:T(8,128)(2,1)S(1)} %reshape.40), channel_id=1, replica_groups=mesh['dom'=16,'band'=32] {'band'}, dimensions={0} | all-to-all | bytes 1179648 | tf_op jit(solution)/shard_map/all_to_all | solution.py:163
  168.9 2.2 %reshape.41 = bf16[32,32,288]{2,1,0:T(8,128)(2,1)S(1)} reshape(bf16[32,24,384]{2,1,0:T(8,128)(2,1)} %all_to_all.11) | data formatting | bytes 1179648 | tf_op jit(solution)/shard_map/reshape | solution.py:164
  171.1 1.1 copy.8
  172.3 3.5 %reshape.42 = bf16[32,12,2,384]{3,2,1,0:T(2,128)(2,1)} reshape(bf16[32,32,288]{2,1,0:T(8,128)(2,1)} %copy.8) | data formatting | bytes 1179648 | tf_op jit(solution)/shard_map/reshape | solution.py:165
Async XLA Ops:
  0.0 126.1 %copy-start = (bf16[1024,1024]{1,0:T(8,128)(2,1)S(1)}, bf16[1024,1024]{1,0:T(8,128)(2,1)}, u32[]{:S(2)}) copy-start(bf16[1024,1024]{1,0:T(8,128)(2,1)} %param.5) | copy-start | bytes 6291460
  3.0 12.8 %copy-start.2 = (f32[16,24,384]{2,1,0:T(8,128)}, f32[16,24,384]{2,1,0:T(8,128)S(1)}, u32[]{:S(2)}) copy-start(f32[16,24,384]{2,1,0:T(8,128)S(1)} %slice.29.mid_ref.psi_ref) | copy-start | bytes 1769476
  5.7 19.8 %collective-permute-start.4 = (f32[8,24,384]{2,1,0:T(8,128)}, f32[8,24,384]{2,1,0:T(8,128)}, u32[]{:S(2)}, u32[]{:S(2)}) collective-permute-start(f32[8,24,384]{2,1,0:T(8,128)} %select_n.109), channel_id=1, source_target_pairs={{0,480},{32,64},{64,32},{96,128},{128,96},{160,192},{192,160},{224... | collective-permute-start | bytes 884744 | tf_op jit(solution)/shard_map/ppermute | solution.py:33
  11.3 13.5 %copy-start.4 = (f32[12,2,384]{2,1,0:T(2,128)S(1)}, f32[12,2,384]{2,1,0:T(2,128)}, u32[]{:S(2)}) copy-start(f32[12,2,384]{2,1,0:T(2,128)} %param.4) | copy-start | bytes 110596
  11.3 14.2 %collective-permute-start.5 = (f32[8,24,384]{2,1,0:T(8,128)}, f32[8,24,384]{2,1,0:T(8,128)}, u32[]{:S(2)}, u32[]{:S(2)}) collective-permute-start(f32[8,24,384]{2,1,0:T(8,128)} %select_n.111), channel_id=1, source_target_pairs={{0,32},{32,0},{64,96},{96,64},{128,160},{160,128},{192,224},{224,1... | collective-permute-start | bytes 884744 | tf_op jit(solution)/shard_map/ppermute | solution.py:32
  14.8 12.6 %copy-start.1 = (f32[16,24,384]{2,1,0:T(8,128)}, f32[16,24,384]{2,1,0:T(8,128)S(1)}, u32[]{:S(2)}) copy-start(f32[16,24,384]{2,1,0:T(8,128)S(1)} %slice.25.mid_ref.psi_ref) | copy-start | bytes 1769476
  16.9 24.4 %collective-permute-start = (f32[8,24,384]{2,1,0:T(8,128)S(1)}, f32[8,24,384]{2,1,0:T(8,128)S(1)}, u32[]{:S(2)}, u32[]{:S(2)}) collective-permute-start(f32[8,24,384]{2,1,0:T(8,128)S(1)} %select_n.99), channel_id=1, source_target_pairs={{0,480},{32,64},{64,32},{96,128},{128,96},{160,192},{192,160},{224... | collective-permute-start | bytes 884744 | tf_op jit(solution)/shard_map/ppermute | solution.py:33
  22.9 18.4 %collective-permute-start.1 = (f32[8,24,384]{2,1,0:T(8,128)}, f32[8,24,384]{2,1,0:T(8,128)}, u32[]{:S(2)}, u32[]{:S(2)}) collective-permute-start(f32[8,24,384]{2,1,0:T(8,128)} %select_n.101), channel_id=1, source_target_pairs={{0,32},{32,0},{64,96},{96,64},{128,160},{160,128},{192,224},{224,1... | collective-permute-start | bytes 884744 | tf_op jit(solution)/shard_map/ppermute | solution.py:32
  34.0 22.0 %collective-permute-start.7 = (f32[8,24,384]{2,1,0:T(8,128)}, f32[8,24,384]{2,1,0:T(8,128)S(1)}, u32[]{:S(2)}, u32[]{:S(2)}) collective-permute-start(f32[8,24,384]{2,1,0:T(8,128)} %get-tuple-element.29), channel_id=1, source_target_pairs={{0,32},{32,0},{64,96},{96,64},{128,160},{160,128},{192,224},{224,1... | collective-permute-start | bytes 884744 | tf_op jit(solution)/shard_map/ppermute | solution.py:32
  36.4 19.6 %collective-permute-start.6 = (f32[8,24,384]{2,1,0:T(8,128)S(1)}, f32[8,24,384]{2,1,0:T(8,128)}, u32[]{:S(2)}, u32[]{:S(2)}) collective-permute-start(f32[8,24,384]{2,1,0:T(8,128)S(1)} %get-tuple-element.30), channel_id=1, source_target_pairs={{0,480},{32,64},{64,32},{96,128},{128,96},{160,192},{192,160},{224... | collective-permute-start | bytes 884744 | tf_op jit(solution)/shard_map/ppermute | solution.py:33
  49.7 12.7 %collective-permute-start.3 = (f32[8,24,384]{2,1,0:T(8,128)}, f32[8,24,384]{2,1,0:T(8,128)S(1)}, u32[]{:S(2)}, u32[]{:S(2)}) collective-permute-start(f32[8,24,384]{2,1,0:T(8,128)} %get-tuple-element.21), channel_id=1, source_target_pairs={{0,32},{32,0},{64,96},{96,64},{128,160},{160,128},{192,224},{224,1... | collective-permute-start | bytes 884744 | tf_op jit(solution)/shard_map/ppermute | solution.py:32
  51.6 11.8 %collective-permute-start.2 = (f32[8,24,384]{2,1,0:T(8,128)S(1)}, f32[8,24,384]{2,1,0:T(8,128)}, u32[]{:S(2)}, u32[]{:S(2)}) collective-permute-start(f32[8,24,384]{2,1,0:T(8,128)S(1)} %get-tuple-element.22), channel_id=1, source_target_pairs={{0,480},{32,64},{64,32},{96,128},{128,96},{160,192},{192,160},{224... | collective-permute-start | bytes 884744 | tf_op jit(solution)/shard_map/ppermute | solution.py:33
  62.4 7.4 %copy-start.3 = (bf16[16,24,384]{2,1,0:T(8,128)(2,1)S(1)}, bf16[16,24,384]{2,1,0:T(8,128)(2,1)}, u32[]{:S(2)}) copy-start(bf16[16,24,384]{2,1,0:T(8,128)(2,1)} %shard_map.40) | copy-start | bytes 884740

commit v5 on v3

v5 whole, which is shorter than its diff:
```python
import jax
import jax.numpy as jnp
from jax import lax
from jax.experimental import pallas as pl
from jax.experimental.pallas import tpu as pltpu
from jax.sharding import PartitionSpec as P

coeffs = (
    -5369.0 / 1800.0,
    12.0 / 7.0,
    -15.0 / 56.0,
    10.0 / 189.0,
    -1.0 / 112.0,
    2.0 / 1925.0,
    -1.0 / 16632.0,
)
center_shift = 32.5
half_width = 27.5
reach = 6
state_block = 8


def swap_rims(head, tail):
    count = lax.axis_size("dom")
    if count % 2:
        left = lax.ppermute(tail, "dom", [(i, (i + 1) % count) for i in range(count)])
        right = lax.ppermute(head, "dom", [((i + 1) % count, i) for i in range(count)])
        return left, right
    even = lax.axis_index("dom") % 2 == 0
    inner = [(i, i + 1) if i % 2 == 0 else (i, i - 1) for i in range(count)]
    outer = [(i, (i - 1) % count) if i % 2 == 0 else (i, (i + 1) % count) for i in range(count)]
    got_inner = lax.ppermute(jnp.where(even, tail, head), "dom", inner)
    got_outer = lax.ppermute(jnp.where(even, head, tail), "dom", outer)
    left = jnp.where(even, got_outer, got_inner)
    right = jnp.where(even, got_inner, got_outer)
    return left, right


def ham_planes(ext_ref, pot_ref, x, z, ny):
    mid = ext_ref[x + reach, z]
    lap = (3.0 * coeffs[0]) * mid
    for k in range(1, 7):
        lap = lap + coeffs[k] * (ext_ref[x + reach + k, z] + ext_ref[x + reach - k, z])
    for k in range(1, 7):
        lap = lap + coeffs[k] * (pltpu.roll(mid, k, 1) + pltpu.roll(mid, ny - k, 1))
    lap = lap + coeffs[1] * ext_ref[x + reach, 1 - z]
    return -2.0 * lap + pot_ref[x, z] * mid, mid


def fill_ext(left_ref, mid_ref, right_ref, ext_ref):
    planes = mid_ref.shape[0]
    ext_ref[pl.ds(0, reach)] = left_ref[...]
    ext_ref[pl.ds(reach, planes)] = mid_ref[...]
    ext_ref[pl.ds(reach + planes, reach)] = right_ref[...]


def first_kernel(left_ref, mid_ref, right_ref, pot_ref, out_ref, head_ref, tail_ref, ext_ref):
    planes, depth, _, ny = out_ref.shape
    fill_ext(left_ref, mid_ref, right_ref, ext_ref)

    def body(x, carry):
        for z in range(depth):
            h, mid = ham_planes(ext_ref, pot_ref, x, z, ny)
            out_ref[x, z] = (h - center_shift * mid) / half_width
        return carry

    lax.fori_loop(0, planes, body, 0)
    head_ref[...] = out_ref[pl.ds(0, reach)]
    tail_ref[...] = out_ref[pl.ds(planes - reach, reach)]


def second_kernel(left_ref, mid_ref, right_ref, psi_ref, pot_ref, out_ref, ext_ref):
    planes, depth, _, ny = out_ref.shape
    fill_ext(left_ref, mid_ref, right_ref, ext_ref)

    def body(x, carry):
        for z in range(depth):
            h, mid = ham_planes(ext_ref, pot_ref, x, z, ny)
            out_ref[x, z] = 2.0 / half_width * (h - center_shift * mid) - psi_ref[x, z]
        return carry

    lax.fori_loop(0, planes, body, 0)


def specs(mid, sb):
    planes, depth, _, ny = mid.shape
    rim = pl.BlockSpec((reach, depth, sb, ny), lambda i: (0, 0, i, 0))
    body = pl.BlockSpec((planes, depth, sb, ny), lambda i: (0, 0, i, 0))
    pot = pl.BlockSpec((planes, depth, 1, ny), lambda i: (0, 0, 0, 0))
    ext = pltpu.VMEM((planes + 2 * reach, depth, sb, ny), jnp.float32)
    return rim, body, pot, ext


def run_first(left, mid, right, pot):
    sb = state_block
    rim, body, pot_spec, ext = specs(mid, sb)
    return pl.pallas_call(
        first_kernel,
        grid=(mid.shape[2] // sb,),
        in_specs=[rim, body, rim, pot_spec],
        out_specs=[body, rim, rim],
        out_shape=[
            jax.ShapeDtypeStruct(mid.shape, jnp.float32),
            jax.ShapeDtypeStruct(left.shape, jnp.float32),
            jax.ShapeDtypeStruct(left.shape, jnp.float32),
        ],
        scratch_shapes=[ext],
    )(left, mid, right, pot)


def run_second(left, mid, right, psi, pot):
    sb = state_block
    rim, body, pot_spec, ext = specs(mid, sb)
    return pl.pallas_call(
        second_kernel,
        grid=(mid.shape[2] // sb,),
        in_specs=[rim, body, rim, body, pot_spec],
        out_specs=body,
        out_shape=jax.ShapeDtypeStruct(mid.shape, jnp.float32),
        scratch_shapes=[ext],
    )(left, mid, right, psi, pot)


def per_device(psi, potential, rotation):
    own_states, planes, depth, ny = psi.shape
    psi_t = psi.transpose(1, 2, 0, 3)
    pot_t = potential[:, :, None, :]
    left, right = swap_rims(psi_t[:reach], psi_t[planes - reach :])
    first, head, tail = run_first(left, psi_t, right, pot_t)
    left, right = swap_rims(head, tail)
    second = run_second(left, first, right, psi_t, pot_t)
    filtered = second.astype(jnp.bfloat16).transpose(2, 0, 1, 3)
    rows = planes * depth
    count = lax.axis_size("band")
    chunk = rows * ny // count
    blocks = filtered.reshape(own_states, count, chunk).transpose(1, 0, 2)
    wire = (count, own_states * chunk // ny, ny)
    gathered = lax.all_to_all(blocks.reshape(wire), "band", 0, 0, tiled=True)
    mixed = lax.dot_general(
        rotation,
        gathered.reshape(own_states * count, chunk),
        (((0,), (0,)), ((), ())),
        preferred_element_type=jnp.float32,
    ).astype(jnp.bfloat16)
    back = lax.all_to_all(mixed.reshape(wire), "band", 0, 0, tiled=True)
    result = back.reshape(count, own_states, chunk).transpose(1, 0, 2)
    return result.reshape(psi.shape)


def solution(mesh):
    in_specs = (P("band", "dom", None, None), P("dom", None, None), P())
    out_specs = P("band", "dom", None, None)
    return jax.shard_map(
        per_device, mesh=mesh, in_specs=in_specs, out_specs=out_specs, check_vma=False
    )
```

time: 163 us -> 167 us (1.025)
  Pallas kernels: 15.2 us -> 19.3 us
  waiting for transfers between devices: 16.6 us -> 20.5 us
  local copies, waits for them, and re-layouts: 21.7 us -> 18.2 us
    pallas_call x2, Pallas kernels: 15.2 us -> 19.3 us  [the longest x1 9.67 us: run_first(): pl.pallas_call(first_kernel, grid=(mid.shape[2] // sb,), in_specs=[rim, b...]
    ppermute x2, waiting for transfers between devices: 16.6 us -> 20.5 us  [swap_rims(): got_outer = lax.ppermute(jnp.where(even, head, tail), 'dom', outer)]
    select_n x2 -> x0, local copies, waits for them, and re-layouts: 2.97 us -> none  [the longest x1 2.09 us: swap_rims(): got_outer = lax.ppermute(jnp.where(even, head, tail), 'dom', outer)]
    reshape x2 -> x0, local copies, waits for them, and re-layouts: 2.87 us -> none  [the longest x1 2.24 us: per_device(): psi_rows = psi.reshape(own_states, rows, ny)]
    unnamed x8 -> x7, local copies, waits for them, and re-layouts: 0.17 us -> 2.56 us
    reshape x2 -> x1, local copies, waits for them, and re-layouts: 3.37 us -> 1.07 us  [per_device(): blocks = filtered.reshape(own_states, count, chunk).transpose(1, 0, 2)]
  transfers between devices with their start and end apart: 4 -> 4, of which waited for: 2 -> 2; matrix products, arithmetic and copies ran while one was open for 1% -> 0% of each run, Pallas kernels for 0% -> 0%
where the time goes in v5:
time: 167 us
  blocking collectives  90 us (54%)
  waiting for transfers between devices  20.5 us (12%)
  Pallas kernels  19.3 us (12%)
  local copies, waits for them, and re-layouts  18.2 us (11%)
  starting transfers between devices  12.9 us (8%)
  other arithmetic  4.97 us (3%)
    all_to_all x1, blocking collectives, per_device(): gathered = lax.all_to_all(blocks.reshape(wire), 'band', 0, 0, tiled=True)  49.8 us
    all_to_all x1, blocking collectives, per_device(): back = lax.all_to_all(mixed.reshape(wire), 'band', 0, 0, tiled=True)  40.2 us
    ppermute x2, waiting for transfers between devices, swap_rims(): got_outer = lax.ppermute(jnp.where(even, head, tail), 'dom', outer)  20.5 us
    pallas_call x1, Pallas kernels, run_first(): pl.pallas_call(first_kernel, grid=(mid.shape[2] // sb,), in_specs=[rim, b...  9.67 us
    pallas_call x1, Pallas kernels, run_second(): pl.pallas_call(second_kernel, grid=(mid.shape[2] // sb,), in_specs=[rim,...  9.62 us
    ppermute x2, starting transfers between devices, swap_rims(): got_outer = lax.ppermute(jnp.where(even, head, tail), 'dom', outer)  8.42 us
    ppermute x2, starting transfers between devices, swap_rims(): got_inner = lax.ppermute(jnp.where(even, tail, head), 'dom', inner)  4.49 us
    reshape x1, local copies, waits for them, and re-layouts, per_device(): return result.reshape(psi.shape)  3.52 us
  transfers between devices with their start and end apart: 4, of which 2 were waited for; matrix products, arithmetic and copies ran while one was open for 0% of the time, Pallas kernels for 0%

profile of v5, /device:TPU:25, one launch (start us, length us, event | category | flops | bytes accessed | tf_op | source)
XLA Modules:
  0.0 166.9 jit_solution(8689384368700493594)
XLA Ops:
  0.0 0.0 copy-start
  0.0 1.6 copy.15
  1.7 0.0 copy-start.1
  1.7 0.0 copy-start.2
  1.7 0.1 slice_select_fusion
  1.8 0.9 copy-done.1
  2.7 2.6 %collective-permute-start.1 = (f32[6,2,32,384]{3,2,1,0:T(8,128)S(1)}, f32[6,2,32,384]{3,2,1,0:T(8,128)S(1)}, u32[]{:S(2)}, u32[]{:S(2)}) collective-permute-start(f32[6,2,32,384]{3,2,1,0:T(8,128)S(1)} %get-tuple-element.17), channel_id=1, source_target_pairs={{0,32},{32,0},{64,96},{96,64},{128,160},{160,128},{192,224},{224,1... | collective-permute-start | bytes 1769480 | tf_op jit(solution)/shard_map/ppermute | solution.py:32
  5.3 4.2 %collective-permute-start = (f32[6,2,32,384]{3,2,1,0:T(8,128)S(1)}, f32[6,2,32,384]{3,2,1,0:T(8,128)S(1)}, u32[]{:S(2)}, u32[]{:S(2)}) collective-permute-start(f32[6,2,32,384]{3,2,1,0:T(8,128)S(1)} %get-tuple-element.18), channel_id=1, source_target_pairs={{0,480},{32,64},{64,32},{96,128},{128,96},{160,192},{192,160},{224... | collective-permute-start | bytes 1769480 | tf_op jit(solution)/shard_map/ppermute | solution.py:33
  9.5 0.0 copy-done.2
  9.5 0.6 broadcast_in_dim.3.pot_ref
  10.1 0.0 collective-permute-done.1
  10.1 10.0 %collective-permute-done = f32[6,2,32,384]{3,2,1,0:T(8,128)S(1)} collective-permute-done((f32[6,2,32,384]{3,2,1,0:T(8,128)S(1)}, f32[6,2,32,384]{3,2,1,0:T(8,128)S(1)}, u32[]{:S(2)}, u32[]{:S(2)}) %collective-permute-start) | collective-permute-done | bytes 589856 | tf_op jit(solution)/shard_map/ppermute | solution.py:33
  20.1 1.1 broadcast_select_fusion.4
  21.2 9.7 %shard_map.37 = (f32[12,2,32,384]{3,2,1,0:T(8,128)}, f32[6,2,32,384]{3,2,1,0:T(8,128)}, f32[6,2,32,384]{3,2,1,0:T(8,128)}) custom-call(f32[6,2,32,384]{3,2,1,0:T(8,128)} %get-tuple-element.16.left_ref, f32[12,2,32,384]{3,2,1,0:T(8,128)} %bitcast.12, f32[6,2,32,384]{3,2,1,0:T(8,128)} %get-tuple-element.15.right_ref, f32[12,2,1,384]{3,2,1,0:T(1,128)} %broadcast_in_dim.3.pot_ref), custom_call_target="tpu_custom_call" | custom-call | tf_op jit(solution)/shard_map/pallas_call | solution.py:97
  30.9 1.3 broadcast_select_fusion.2
  32.2 1.9 %collective-permute-start.3 = (f32[6,2,32,384]{3,2,1,0:T(8,128)S(1)}, f32[6,2,32,384]{3,2,1,0:T(8,128)S(1)}, u32[]{:S(2)}, u32[]{:S(2)}) collective-permute-start(f32[6,2,32,384]{3,2,1,0:T(8,128)S(1)} %get-tuple-element.13), channel_id=1, source_target_pairs={{0,32},{32,0},{64,96},{96,64},{128,160},{160,128},{192,224},{224,1... | collective-permute-start | bytes 1769480 | tf_op jit(solution)/shard_map/ppermute | solution.py:32
  34.1 4.2 %collective-permute-start.2 = (f32[6,2,32,384]{3,2,1,0:T(8,128)S(1)}, f32[6,2,32,384]{3,2,1,0:T(8,128)S(1)}, u32[]{:S(2)}, u32[]{:S(2)}) collective-permute-start(f32[6,2,32,384]{3,2,1,0:T(8,128)S(1)} %get-tuple-element.14), channel_id=1, source_target_pairs={{0,480},{32,64},{64,32},{96,128},{128,96},{160,192},{192,160},{224... | collective-permute-start | bytes 1769480 | tf_op jit(solution)/shard_map/ppermute | solution.py:33
  38.3 0.0 collective-permute-done.3
  38.4 10.6 %collective-permute-done.2 = f32[6,2,32,384]{3,2,1,0:T(8,128)S(1)} collective-permute-done((f32[6,2,32,384]{3,2,1,0:T(8,128)S(1)}, f32[6,2,32,384]{3,2,1,0:T(8,128)S(1)}, u32[]{:S(2)}, u32[]{:S(2)}) %collective-permute-start.2) | collective-permute-done | bytes 589856 | tf_op jit(solution)/shard_map/ppermute | solution.py:33
  48.9 1.1 broadcast_select_fusion
  50.0 9.6 %shard_map.38 = f32[12,2,32,384]{3,2,1,0:T(8,128)} custom-call(f32[6,2,32,384]{3,2,1,0:T(8,128)} %get-tuple-element.12.left_ref, f32[12,2,32,384]{3,2,1,0:T(8,128)} %get-tuple-element.10.mid_ref, f32[6,2,32,384]{3,2,1,0:T(8,128)} %get-tuple-element.11.right_ref, f32[12,2,32,384]{3,2,1,0:T(8,128)} %bitcast.13, f32[12,2,1,384]{3,2,1,0:T(1,128)} %broadcast_in_dim.3.pot_ref), custom_call_target="tpu_custom_call" | custom-call | tf_op jit(solution)/shard_map/pallas_call | solution.py:114
  59.7 1.3 convert_bitcast_fusion
  61.0 0.5 copy.10
  61.5 1.1 reshape.18
  62.6 1.1 copy.11
  63.7 2.6 %reshape.19 = bf16[32,24,384]{2,1,0:T(8,128)(2,1)S(1)} reshape(bf16[32,32,288]{2,1,0:T(8,128)(2,1)} %copy.11) | data formatting | bytes 1179648 | tf_op jit(solution)/shard_map/reshape | solution.py:138
  66.3 49.8 %all_to_all.10 = bf16[32,24,384]{2,1,0:T(8,128)(2,1)S(1)} all-to-all(bf16[32,24,384]{2,1,0:T(8,128)(2,1)S(1)} %reshape.19), channel_id=1, replica_groups=mesh['dom'=16,'band'=32] {'band'}, dimensions={0} | all-to-all | bytes 1179648 | tf_op jit(solution)/shard_map/all_to_all | solution.py:138
  116.1 1.1 reshape.20
  117.2 0.0 copy-done
  117.2 0.8 fusion
  118.0 0.4 copy.12
  118.4 1.4 reshape.21
  119.8 40.2 %all_to_all.11 = bf16[32,24,384]{2,1,0:T(8,128)(2,1)} all-to-all(bf16[32,24,384]{2,1,0:T(8,128)(2,1)S(1)} %reshape.21), channel_id=1, replica_groups=mesh['dom'=16,'band'=32] {'band'}, dimensions={0} | all-to-all | bytes 1179648 | tf_op jit(solution)/shard_map/all_to_all | solution.py:145
  160.0 2.2 %reshape.22 = bf16[32,32,288]{2,1,0:T(8,128)(2,1)S(1)} reshape(bf16[32,24,384]{2,1,0:T(8,128)(2,1)} %all_to_all.11) | data formatting | bytes 1179648 | tf_op jit(solution)/shard_map/reshape | solution.py:146
  162.2 1.1 copy.13
  163.4 3.5 %reshape.23 = bf16[32,12,2,384]{3,2,1,0:T(2,128)(2,1)} reshape(bf16[32,32,288]{2,1,0:T(8,128)(2,1)} %copy.13) | data formatting | bytes 1179648 | tf_op jit(solution)/shard_map/reshape | solution.py:147
Async XLA Ops:
  0.0 117.2 %copy-start = (bf16[1024,1024]{1,0:T(8,128)(2,1)S(1)}, bf16[1024,1024]{1,0:T(8,128)(2,1)}, u32[]{:S(2)}) copy-start(bf16[1024,1024]{1,0:T(8,128)(2,1)} %param.5) | copy-start | bytes 6291460
  1.7 1.0 copy-start.1
  1.7 7.8 %copy-start.2 = (f32[12,2,384]{2,1,0:T(2,128)S(1)}, f32[12,2,384]{2,1,0:T(2,128)}, u32[]{:S(2)}) copy-start(f32[12,2,384]{2,1,0:T(2,128)} %param.4) | copy-start | bytes 110596
  2.7 7.4 %collective-permute-start.1 = (f32[6,2,32,384]{3,2,1,0:T(8,128)S(1)}, f32[6,2,32,384]{3,2,1,0:T(8,128)S(1)}, u32[]{:S(2)}, u32[]{:S(2)}) collective-permute-start(f32[6,2,32,384]{3,2,1,0:T(8,128)S(1)} %get-tuple-element.17), channel_id=1, source_target_pairs={{0,32},{32,0},{64,96},{96,64},{128,160},{160,128},{192,224},{224,1... | collective-permute-start | bytes 1769480 | tf_op jit(solution)/shard_map/ppermute | solution.py:32
  5.3 14.8 %collective-permute-start = (f32[6,2,32,384]{3,2,1,0:T(8,128)S(1)}, f32[6,2,32,384]{3,2,1,0:T(8,128)S(1)}, u32[]{:S(2)}, u32[]{:S(2)}) collective-permute-start(f32[6,2,32,384]{3,2,1,0:T(8,128)S(1)} %get-tuple-element.18), channel_id=1, source_target_pairs={{0,480},{32,64},{64,32},{96,128},{128,96},{160,192},{192,160},{224... | collective-permute-start | bytes 1769480 | tf_op jit(solution)/shard_map/ppermute | solution.py:33
  32.2 6.1 %collective-permute-start.3 = (f32[6,2,32,384]{3,2,1,0:T(8,128)S(1)}, f32[6,2,32,384]{3,2,1,0:T(8,128)S(1)}, u32[]{:S(2)}, u32[]{:S(2)}) collective-permute-start(f32[6,2,32,384]{3,2,1,0:T(8,128)S(1)} %get-tuple-element.13), channel_id=1, source_target_pairs={{0,32},{32,0},{64,96},{96,64},{128,160},{160,128},{192,224},{224,1... | collective-permute-start | bytes 1769480 | tf_op jit(solution)/shard_map/ppermute | solution.py:32
  34.1 14.8 %collective-permute-start.2 = (f32[6,2,32,384]{3,2,1,0:T(8,128)S(1)}, f32[6,2,32,384]{3,2,1,0:T(8,128)S(1)}, u32[]{:S(2)}, u32[]{:S(2)}) collective-permute-start(f32[6,2,32,384]{3,2,1,0:T(8,128)S(1)} %get-tuple-element.14), channel_id=1, source_target_pairs={{0,480},{32,64},{64,32},{96,128},{128,96},{160,192},{192,160},{224... | collective-permute-start | bytes 1769480 | tf_op jit(solution)/shard_map/ppermute | solution.py:33

commit v6 on v5

--- a/solution.py
+++ b/solution.py
@@ -17,7 +17,7 @@
 center_shift = 32.5
 half_width = 27.5
 reach = 6
-state_block = 8
+state_block = 32
 
 
 def swap_rims(head, tail):

time: 167 us -> 164 us (0.982)
  Pallas kernels: 19.3 us -> 15.7 us
    pallas_call x1, Pallas kernels: 9.67 us -> 7.85 us  [run_first(): pl.pallas_call(first_kernel, grid=(mid.shape[2] // sb,), in_specs=[rim, b...]
    pallas_call x1, Pallas kernels: 9.62 us -> 7.88 us  [run_second(): pl.pallas_call(second_kernel, grid=(mid.shape[2] // sb,), in_specs=[rim,...]
where the time goes in v6:
time: 164 us; the launch traced here: 163 us
  blocking collectives  90 us (55%)
  waiting for transfers between devices  20.5 us (12%)
  local copies, waits for them, and re-layouts  18.2 us (11%)
  Pallas kernels  15.7 us (10%)
  starting transfers between devices  12.9 us (8%)
  other arithmetic  4.97 us (3%)
    all_to_all x1, blocking collectives, per_device(): gathered = lax.all_to_all(blocks.reshape(wire), 'band', 0, 0, tiled=True)  49.8 us
    all_to_all x1, blocking collectives, per_device(): back = lax.all_to_all(mixed.reshape(wire), 'band', 0, 0, tiled=True)  40.2 us
    ppermute x2, waiting for transfers between devices, swap_rims(): got_outer = lax.ppermute(jnp.where(even, head, tail), 'dom', outer)  20.5 us
    ppermute x2, starting transfers between devices, swap_rims(): got_outer = lax.ppermute(jnp.where(even, head, tail), 'dom', outer)  8.42 us
    pallas_call x1, Pallas kernels, run_second(): pl.pallas_call(second_kernel, grid=(mid.shape[2] // sb,), in_specs=[rim,...  7.88 us
    pallas_call x1, Pallas kernels, run_first(): pl.pallas_call(first_kernel, grid=(mid.shape[2] // sb,), in_specs=[rim, b...  7.85 us
    ppermute x2, starting transfers between devices, swap_rims(): got_inner = lax.ppermute(jnp.where(even, tail, head), 'dom', inner)  4.49 us
    reshape x1, local copies, waits for them, and re-layouts, per_device(): return result.reshape(psi.shape)  3.52 us
  transfers between devices with their start and end apart: 4, of which 2 were waited for; matrix products, arithmetic and copies ran while one was open for 0% of the time, Pallas kernels for 0%

profile of v6, /device:TPU:25, one launch (start us, length us, event | category | flops | bytes accessed | tf_op | source)
XLA Modules:
  0.0 163.3 jit_solution(14063410136762574959)
XLA Ops:
  0.0 0.0 copy-start
  0.0 1.6 %copy.15 = f32[32,12,2,384]{3,0,2,1:T(8,128)S(1)} copy(f32[32,12,2,384]{3,2,1,0:T(2,128)} %param.3) | data formatting | bytes 2359296 | tf_op args[0]
  1.7 0.0 copy-start.1
  1.7 0.0 copy-start.2
  1.7 0.1 slice_select_fusion
  1.8 0.9 copy-done.1
  2.7 2.6 %collective-permute-start.1 = (f32[6,2,32,384]{3,2,1,0:T(8,128)S(1)}, f32[6,2,32,384]{3,2,1,0:T(8,128)S(1)}, u32[]{:S(2)}, u32[]{:S(2)}) collective-permute-start(f32[6,2,32,384]{3,2,1,0:T(8,128)S(1)} %get-tuple-element.17), channel_id=1, source_target_pairs={{0,32},{32,0},{64,96},{96,64},{128,160},{160,128},{192,224},{224,1... | collective-permute-start | bytes 1769480 | tf_op jit(solution)/shard_map/ppermute | solution.py:32
  5.3 4.2 %collective-permute-start = (f32[6,2,32,384]{3,2,1,0:T(8,128)S(1)}, f32[6,2,32,384]{3,2,1,0:T(8,128)S(1)}, u32[]{:S(2)}, u32[]{:S(2)}) collective-permute-start(f32[6,2,32,384]{3,2,1,0:T(8,128)S(1)} %get-tuple-element.18), channel_id=1, source_target_pairs={{0,480},{32,64},{64,32},{96,128},{128,96},{160,192},{192,160},{224... | collective-permute-start | bytes 1769480 | tf_op jit(solution)/shard_map/ppermute | solution.py:33
  9.5 0.0 copy-done.2
  9.5 0.6 broadcast_in_dim.3.pot_ref
  10.1 0.0 collective-permute-done.1
  10.1 10.0 %collective-permute-done = f32[6,2,32,384]{3,2,1,0:T(8,128)S(1)} collective-permute-done((f32[6,2,32,384]{3,2,1,0:T(8,128)S(1)}, f32[6,2,32,384]{3,2,1,0:T(8,128)S(1)}, u32[]{:S(2)}, u32[]{:S(2)}) %collective-permute-start) | collective-permute-done | bytes 589856 | tf_op jit(solution)/shard_map/ppermute | solution.py:33
  20.1 1.1 broadcast_select_fusion.4
  21.2 7.9 %shard_map.37 = (f32[12,2,32,384]{3,2,1,0:T(8,128)}, f32[6,2,32,384]{3,2,1,0:T(8,128)}, f32[6,2,32,384]{3,2,1,0:T(8,128)}) custom-call(f32[6,2,32,384]{3,2,1,0:T(8,128)} %get-tuple-element.16.left_ref, f32[12,2,32,384]{3,2,1,0:T(8,128)} %bitcast.12, f32[6,2,32,384]{3,2,1,0:T(8,128)} %get-tuple-element.15.right_ref, f32[12,2,1,384]{3,2,1,0:T(1,128)} %broadcast_in_dim.3.pot_ref), custom_call_target="tpu_custom_call" | custom-call | tf_op jit(solution)/shard_map/pallas_call | solution.py:97
  29.0 1.3 broadcast_select_fusion.2
  30.4 1.9 %collective-permute-start.3 = (f32[6,2,32,384]{3,2,1,0:T(8,128)S(1)}, f32[6,2,32,384]{3,2,1,0:T(8,128)S(1)}, u32[]{:S(2)}, u32[]{:S(2)}) collective-permute-start(f32[6,2,32,384]{3,2,1,0:T(8,128)S(1)} %get-tuple-element.13), channel_id=1, source_target_pairs={{0,32},{32,0},{64,96},{96,64},{128,160},{160,128},{192,224},{224,1... | collective-permute-start | bytes 1769480 | tf_op jit(solution)/shard_map/ppermute | solution.py:32
  32.3 4.2 %collective-permute-start.2 = (f32[6,2,32,384]{3,2,1,0:T(8,128)S(1)}, f32[6,2,32,384]{3,2,1,0:T(8,128)S(1)}, u32[]{:S(2)}, u32[]{:S(2)}) collective-permute-start(f32[6,2,32,384]{3,2,1,0:T(8,128)S(1)} %get-tuple-element.14), channel_id=1, source_target_pairs={{0,480},{32,64},{64,32},{96,128},{128,96},{160,192},{192,160},{224... | collective-permute-start | bytes 1769480 | tf_op jit(solution)/shard_map/ppermute | solution.py:33
  36.5 0.0 collective-permute-done.3
  36.5 10.6 %collective-permute-done.2 = f32[6,2,32,384]{3,2,1,0:T(8,128)S(1)} collective-permute-done((f32[6,2,32,384]{3,2,1,0:T(8,128)S(1)}, f32[6,2,32,384]{3,2,1,0:T(8,128)S(1)}, u32[]{:S(2)}, u32[]{:S(2)}) %collective-permute-start.2) | collective-permute-done | bytes 589856 | tf_op jit(solution)/shard_map/ppermute | solution.py:33
  47.1 1.1 broadcast_select_fusion
  48.2 7.9 %shard_map.38 = f32[12,2,32,384]{3,2,1,0:T(8,128)} custom-call(f32[6,2,32,384]{3,2,1,0:T(8,128)} %get-tuple-element.12.left_ref, f32[12,2,32,384]{3,2,1,0:T(8,128)} %get-tuple-element.10.mid_ref, f32[6,2,32,384]{3,2,1,0:T(8,128)} %get-tuple-element.11.right_ref, f32[12,2,32,384]{3,2,1,0:T(8,128)} %bitcast.13, f32[12,2,1,384]{3,2,1,0:T(1,128)} %broadcast_in_dim.3.pot_ref), custom_call_target="tpu_custom_call" | custom-call | tf_op jit(solution)/shard_map/pallas_call | solution.py:114
  56.1 1.3 convert_bitcast_fusion
  57.4 0.5 copy.10
  57.9 1.1 reshape.18
  59.0 1.1 copy.11
  60.1 2.6 %reshape.19 = bf16[32,24,384]{2,1,0:T(8,128)(2,1)S(1)} reshape(bf16[32,32,288]{2,1,0:T(8,128)(2,1)} %copy.11) | data formatting | bytes 1179648 | tf_op jit(solution)/shard_map/reshape | solution.py:138
  62.7 49.8 %all_to_all.10 = bf16[32,24,384]{2,1,0:T(8,128)(2,1)S(1)} all-to-all(bf16[32,24,384]{2,1,0:T(8,128)(2,1)S(1)} %reshape.19), channel_id=1, replica_groups=mesh['dom'=16,'band'=32] {'band'}, dimensions={0} | all-to-all | bytes 1179648 | tf_op jit(solution)/shard_map/all_to_all | solution.py:138
  112.6 1.1 reshape.20
  113.7 0.0 copy-done
  113.7 0.8 fusion
  114.5 0.4 copy.12
  114.8 1.4 reshape.21
  116.2 40.2 %all_to_all.11 = bf16[32,24,384]{2,1,0:T(8,128)(2,1)} all-to-all(bf16[32,24,384]{2,1,0:T(8,128)(2,1)S(1)} %reshape.21), channel_id=1, replica_groups=mesh['dom'=16,'band'=32] {'band'}, dimensions={0} | all-to-all | bytes 1179648 | tf_op jit(solution)/shard_map/all_to_all | solution.py:145
  156.4 2.2 %reshape.22 = bf16[32,32,288]{2,1,0:T(8,128)(2,1)S(1)} reshape(bf16[32,24,384]{2,1,0:T(8,128)(2,1)} %all_to_all.11) | data formatting | bytes 1179648 | tf_op jit(solution)/shard_map/reshape | solution.py:146
  158.7 1.1 copy.13
  159.8 3.5 %reshape.23 = bf16[32,12,2,384]{3,2,1,0:T(2,128)(2,1)} reshape(bf16[32,32,288]{2,1,0:T(8,128)(2,1)} %copy.13) | data formatting | bytes 1179648 | tf_op jit(solution)/shard_map/reshape | solution.py:147
Async XLA Ops:
  0.0 113.7 %copy-start = (bf16[1024,1024]{1,0:T(8,128)(2,1)S(1)}, bf16[1024,1024]{1,0:T(8,128)(2,1)}, u32[]{:S(2)}) copy-start(bf16[1024,1024]{1,0:T(8,128)(2,1)} %param.5) | copy-start | bytes 6291460
  1.7 1.0 copy-start.1
  1.7 7.8 %copy-start.2 = (f32[12,2,384]{2,1,0:T(2,128)S(1)}, f32[12,2,384]{2,1,0:T(2,128)}, u32[]{:S(2)}) copy-start(f32[12,2,384]{2,1,0:T(2,128)} %param.4) | copy-start | bytes 110596
  2.7 7.4 %collective-permute-start.1 = (f32[6,2,32,384]{3,2,1,0:T(8,128)S(1)}, f32[6,2,32,384]{3,2,1,0:T(8,128)S(1)}, u32[]{:S(2)}, u32[]{:S(2)}) collective-permute-start(f32[6,2,32,384]{3,2,1,0:T(8,128)S(1)} %get-tuple-element.17), channel_id=1, source_target_pairs={{0,32},{32,0},{64,96},{96,64},{128,160},{160,128},{192,224},{224,1... | collective-permute-start | bytes 1769480 | tf_op jit(solution)/shard_map/ppermute | solution.py:32
  5.3 14.8 %collective-permute-start = (f32[6,2,32,384]{3,2,1,0:T(8,128)S(1)}, f32[6,2,32,384]{3,2,1,0:T(8,128)S(1)}, u32[]{:S(2)}, u32[]{:S(2)}) collective-permute-start(f32[6,2,32,384]{3,2,1,0:T(8,128)S(1)} %get-tuple-element.18), channel_id=1, source_target_pairs={{0,480},{32,64},{64,32},{96,128},{128,96},{160,192},{192,160},{224... | collective-permute-start | bytes 1769480 | tf_op jit(solution)/shard_map/ppermute | solution.py:33
  30.4 6.1 %collective-permute-start.3 = (f32[6,2,32,384]{3,2,1,0:T(8,128)S(1)}, f32[6,2,32,384]{3,2,1,0:T(8,128)S(1)}, u32[]{:S(2)}, u32[]{:S(2)}) collective-permute-start(f32[6,2,32,384]{3,2,1,0:T(8,128)S(1)} %get-tuple-element.13), channel_id=1, source_target_pairs={{0,32},{32,0},{64,96},{96,64},{128,160},{160,128},{192,224},{224,1... | collective-permute-start | bytes 1769480 | tf_op jit(solution)/shard_map/ppermute | solution.py:32
  32.3 14.8 %collective-permute-start.2 = (f32[6,2,32,384]{3,2,1,0:T(8,128)S(1)}, f32[6,2,32,384]{3,2,1,0:T(8,128)S(1)}, u32[]{:S(2)}, u32[]{:S(2)}) collective-permute-start(f32[6,2,32,384]{3,2,1,0:T(8,128)S(1)} %get-tuple-element.14), channel_id=1, source_target_pairs={{0,480},{32,64},{64,32},{96,128},{128,96},{160,192},{192,160},{224... | collective-permute-start | bytes 1769480 | tf_op jit(solution)/shard_map/ppermute | solution.py:33

commit v7 on v6

--- a/solution.py
+++ b/solution.py
@@ -121,14 +121,109 @@
     )(left, mid, right, psi, pot)
 
 
+def first_half_kernel(side_ref, rim_ref, mid_ref, pot_ref, out_ref, ext_ref):
+    planes = mid_ref.shape[0]
+    depth, ny = out_ref.shape[1], out_ref.shape[3]
+    h = side_ref[0]
+    ext_ref[pl.ds(reach, planes)] = mid_ref[...]
+    ext_ref[pl.ds(h * (reach + planes), reach)] = rim_ref[...]
+    base = h * (planes - reach)
+
+    def body(x, carry):
+        for z in range(depth):
+            hv, mid = ham_planes(ext_ref, pot_ref, base + x, z, ny)
+            out_ref[x, z] = (hv - center_shift * mid) / half_width
+        return carry
+
+    lax.fori_loop(0, planes - reach, body, 0)
+
+
+def second_half_kernel(side_ref, rim_ref, a_ref, b_ref, psi_ref, pot_ref, out_ref, ext_ref):
+    planes = psi_ref.shape[0]
+    half = planes - reach
+    depth, ny = out_ref.shape[1], out_ref.shape[3]
+    h = side_ref[0]
+    a_side = side_ref[1]
+    ext_ref[pl.ds(reach + a_side * half, half)] = a_ref[...]
+    ext_ref[pl.ds(reach + (1 - a_side) * half, half)] = b_ref[...]
+    ext_ref[pl.ds(h * (reach + planes), reach)] = rim_ref[...]
+    base = h * half
+
+    def body(x, carry):
+        for z in range(depth):
+            hv, mid = ham_planes(ext_ref, pot_ref, base + x, z, ny)
+            out_ref[x, z] = 2.0 / half_width * (hv - center_shift * mid) - psi_ref[base + x, z]
+        return carry
+
+    lax.fori_loop(0, half, body, 0)
+
+
+def smem():
+    return pl.BlockSpec(memory_space=pltpu.SMEM)
+
+
+def whole(shape):
+    return pl.BlockSpec(shape, lambda i: (0,) * len(shape))
+
+
+def run_first_half(side, rim, mid, pot):
+    planes, depth, states, ny = mid.shape
+    half = (planes - reach, depth, states, ny)
+    return pl.pallas_call(
+        first_half_kernel,
+        grid=(1,),
+        in_specs=[smem(), whole(rim.shape), whole(mid.shape), whole(pot.shape)],
+        out_specs=whole(half),
+        out_shape=jax.ShapeDtypeStruct(half, jnp.float32),
+        scratch_shapes=[pltpu.VMEM((planes + 2 * reach, depth, states, ny), jnp.float32)],
+    )(side, rim, mid, pot)
+
+
+def run_second_half(side, rim, a, b, psi, pot):
+    planes, depth, states, ny = psi.shape
+    return pl.pallas_call(
+        second_half_kernel,
+        grid=(1,),
+        in_specs=[smem(), whole(rim.shape), whole(a.shape), whole(b.shape), whole(psi.shape), whole(pot.shape)],
+        out_specs=whole(a.shape),
+        out_shape=jax.ShapeDtypeStruct(a.shape, jnp.float32),
+        scratch_shapes=[pltpu.VMEM((planes + 2 * reach, depth, states, ny), jnp.float32)],
+    )(side, rim, a, b, psi, pot)
+
+
+def inner_outer(send_inner, send_outer):
+    count = lax.axis_size("dom")
+    inner = [(i, i + 1) if i % 2 == 0 else (i, i - 1) for i in range(count)]
+    outer = [(i, (i - 1) % count) if i % 2 == 0 else (i, (i + 1) % count) for i in range(count)]
+    return lax.ppermute(send_inner, "dom", inner), lax.ppermute(send_outer, "dom", outer)
+
+
 def per_device(psi, potential, rotation):
     own_states, planes, depth, ny = psi.shape
     psi_t = psi.transpose(1, 2, 0, 3)
     pot_t = potential[:, :, None, :]
-    left, right = swap_rims(psi_t[:reach], psi_t[planes - reach :])
-    first, head, tail = run_first(left, psi_t, right, pot_t)
-    left, right = swap_rims(head, tail)
-    second = run_second(left, first, right, psi_t, pot_t)
+    if lax.axis_size("dom") % 2 or planes != 2 * reach:
+        left, right = swap_rims(psi_t[:reach], psi_t[planes - reach :])
+        first, head, tail = run_first(left, psi_t, right, pot_t)
+        left, right = swap_rims(head, tail)
+        second = run_second(left, first, right, psi_t, pot_t)
+    else:
+        even = lax.axis_index("dom") % 2 == 0
+        hi = jnp.where(even, 1, 0).astype(jnp.int32)
+        head, tail = psi_t[:reach], psi_t[planes - reach :]
+        rim_in, rim_out = inner_outer(jnp.where(even, tail, head), jnp.where(even, head, tail))
+        part_a = run_first_half(hi.reshape(1), rim_in, psi_t, pot_t)
+        part_b = run_first_half((1 - hi).reshape(1), rim_out, psi_t, pot_t)
+        rim_in, rim_out = inner_outer(part_a, part_b)
+        sides_a = jnp.stack([hi, hi])
+        sides_b = jnp.stack([1 - hi, hi])
+        second_a = run_second_half(sides_a, rim_in, part_a, part_b, psi_t, pot_t)
+        second_b = run_second_half(sides_b, rim_out, part_a, part_b, psi_t, pot_t)
+        second = jnp.where(
+            even,
+            jnp.concatenate([second_b, second_a], axis=0),
+            jnp.concatenate([second_a, second_b], axis=0),
+        )
     filtered = second.astype(jnp.bfloat16).transpose(2, 0, 1, 3)
     rows = planes * depth
     count = lax.axis_size("band")

time: 164 us -> 148 us (0.902); the launches traced: 163 us -> 145 us
  waiting for transfers between devices: 20.5 us -> 7.91 us
  blocking collectives: 90 us -> 81.8 us
  Pallas kernels: 15.7 us -> 19.6 us
  other arithmetic: 4.97 us -> 3.24 us
    ppermute x4, waiting for transfers between devices: 20.5 us -> 7.91 us  [the longest x2 7.91 us: inner_outer(): lax.ppermute(send_outer, 'dom', outer)]
    all_to_all x1, blocking collectives: 40.2 us -> 36.1 us  [per_device(): back = lax.all_to_all(mixed.reshape(wire), 'band', 0, 0, tiled=True)]
    all_to_all x1, blocking collectives: 49.8 us -> 45.7 us  [per_device(): gathered = lax.all_to_all(blocks.reshape(wire), 'band', 0, 0, tiled=True)]
    pallas_call x2 -> x4, Pallas kernels: 15.7 us -> 19.6 us  [the longest x2 10.2 us: run_second_half(): pl.pallas_call(second_half_kernel, grid=(1,), in_specs=[smem(), whole(rim...]
    select_n x4 -> x1, other arithmetic: 3.63 us -> 1.25 us  [per_device(): jnp.where(even, tail, head)]
    unnamed x7 -> x13, local copies, waits for them, and re-layouts: 2.56 us -> 3.32 us
  transfers between devices with their start and end apart: 4 -> 4, of which waited for: 2 -> 2; matrix products, arithmetic and copies ran while one was open for 0% -> 1% of each run, Pallas kernels for 0% -> 10%
where the time goes in v7:
time: 148 us; the launch traced here: 145 us
  blocking collectives  81.8 us (55%)
  Pallas kernels  19.6 us (13%)
  local copies, waits for them, and re-layouts  18.9 us (13%)
  starting transfers between devices  12.9 us (9%)
  waiting for transfers between devices  7.91 us (5%)
  other arithmetic  3.24 us (2%)
    all_to_all x1, blocking collectives, per_device(): gathered = lax.all_to_all(blocks.reshape(wire), 'band', 0, 0, tiled=True)  45.7 us
    all_to_all x1, blocking collectives, per_device(): back = lax.all_to_all(mixed.reshape(wire), 'band', 0, 0, tiled=True)  36.1 us
    pallas_call x2, Pallas kernels, run_second_half(): pl.pallas_call(second_half_kernel, grid=(1,), in_specs=[smem(), whole(rim...  10.2 us
    pallas_call x2, Pallas kernels, run_first_half(): pl.pallas_call(first_half_kernel, grid=(1,), in_specs=[smem(), whole(rim....  9.43 us
    ppermute x2, starting transfers between devices, inner_outer(): lax.ppermute(send_outer, 'dom', outer)  8.4 us
    ppermute x2, waiting for transfers between devices, inner_outer(): lax.ppermute(send_outer, 'dom', outer)  7.91 us
    ppermute x2, starting transfers between devices, inner_outer(): lax.ppermute(send_inner, 'dom', inner)  4.48 us
    reshape x1, local copies, waits for them, and re-layouts, per_device(): return result.reshape(psi.shape)  3.52 us
  transfers between devices with their start and end apart: 4, of which 2 were waited for; matrix products, arithmetic and copies ran while one was open for 1% of the time, Pallas kernels for 10%

profile of v7, /device:TPU:25, one launch (start us, length us, event | category | flops | bytes accessed | tf_op | source)
XLA Modules:
  0.0 145.3 jit_solution(10867005344514017527)
XLA Ops:
  0.0 0.0 copy-start
  0.0 0.0 copy-start.5
  0.0 1.7 %copy.15 = f32[32,12,2,384]{3,0,2,1:T(8,128)S(1)} copy(f32[32,12,2,384]{3,2,1,0:T(2,128)} %param.3) | data formatting | bytes 2359296 | tf_op args[0]
  1.7 0.0 copy-start.1
  1.7 1.3 slice_select_fusion
  2.9 2.6 %collective-permute-start.2 = (f32[6,2,32,384]{3,2,1,0:T(8,128)}, f32[6,2,32,384]{3,2,1,0:T(8,128)}, u32[]{:S(2)}, u32[]{:S(2)}) collective-permute-start(f32[6,2,32,384]{3,2,1,0:T(8,128)} %get-tuple-element.5), channel_id=1, source_target_pairs={{0,32},{32,0},{64,96},{96,64},{128,160},{160,128},{192,224},{224,1... | collective-permute-start | bytes 1769480 | tf_op jit(solution)/shard_map/ppermute | solution.py:198
  5.5 4.2 %collective-permute-start = (f32[6,2,32,384]{3,2,1,0:T(8,128)}, f32[6,2,32,384]{3,2,1,0:T(8,128)}, u32[]{:S(2)}, u32[]{:S(2)}) collective-permute-start(f32[6,2,32,384]{3,2,1,0:T(8,128)} %get-tuple-element.6), channel_id=1, source_target_pairs={{0,480},{32,64},{64,32},{96,128},{128,96},{160,192},{192,160},{224... | collective-permute-start | bytes 1769480 | tf_op jit(solution)/shard_map/ppermute | solution.py:198
  9.7 0.0 copy-done.5
  9.7 0.6 broadcast_in_dim.3.pot_ref
  10.4 0.0 collective-permute-done.2.rim_ref
  10.4 0.0 copy-done.1
  10.4 4.7 %shard_map.38.a_ref = f32[6,2,32,384]{3,2,1,0:T(8,128)} custom-call(s32[1]{0:T(128)} %bitcast.1.side_ref, f32[6,2,32,384]{3,2,1,0:T(8,128)} %collective-permute-done.2.rim_ref, f32[12,2,32,384]{3,2,1,0:T(8,128)} %bitcast.14, f32[12,2,1,384]{3,2,1,0:T(1,128)} %broadcast_in_dim.3.pot_ref), custom_call_target="tpu_custom_call" | custom-call | tf_op jit(solution)/shard_map/pallas_call | solution.py:172
  15.1 1.9 %collective-permute-start.3 = (f32[6,2,32,384]{3,2,1,0:T(8,128)}, f32[6,2,32,384]{3,2,1,0:T(8,128)S(1)}, u32[]{:S(2)}, u32[]{:S(2)}) collective-permute-start(f32[6,2,32,384]{3,2,1,0:T(8,128)} %shard_map.38.a_ref), channel_id=1, source_target_pairs={{0,32},{32,0},{64,96},{96,64},{128,160},{160,128},{192,224},{224,1... | collective-permute-start | bytes 1769480 | tf_op jit(solution)/shard_map/ppermute | solution.py:198
  17.0 3.6 %collective-permute-done.rim_ref = f32[6,2,32,384]{3,2,1,0:T(8,128)} collective-permute-done((f32[6,2,32,384]{3,2,1,0:T(8,128)}, f32[6,2,32,384]{3,2,1,0:T(8,128)}, u32[]{:S(2)}, u32[]{:S(2)}) %collective-permute-start) | collective-permute-done | bytes 589856 | tf_op jit(solution)/shard_map/ppermute | solution.py:198
  20.6 4.7 %shard_map.37.b_ref = f32[6,2,32,384]{3,2,1,0:T(8,128)} custom-call(s32[1]{0:T(128)} %bitcast.side_ref, f32[6,2,32,384]{3,2,1,0:T(8,128)} %collective-permute-done.rim_ref, f32[12,2,32,384]{3,2,1,0:T(8,128)} %bitcast.15, f32[12,2,1,384]{3,2,1,0:T(1,128)} %broadcast_in_dim.3.pot_ref), custom_call_target="tpu_custom_call" | custom-call | tf_op jit(solution)/shard_map/pallas_call | solution.py:172
  25.3 4.2 %collective-permute-start.1 = (f32[6,2,32,384]{3,2,1,0:T(8,128)}, f32[6,2,32,384]{3,2,1,0:T(8,128)S(1)}, u32[]{:S(2)}, u32[]{:S(2)}) collective-permute-start(f32[6,2,32,384]{3,2,1,0:T(8,128)} %shard_map.37.b_ref), channel_id=1, source_target_pairs={{0,480},{32,64},{64,32},{96,128},{128,96},{160,192},{192,160},{224... | collective-permute-start | bytes 1769480 | tf_op jit(solution)/shard_map/ppermute | solution.py:198
  29.5 0.6 pad_add_fusion
  30.1 0.0 collective-permute-done.3.rim_ref
  30.1 0.0 copy-start.4
  30.2 0.8 copy-done.4
  31.0 5.1 %shard_map.40 = f32[6,2,32,384]{3,2,1,0:T(8,128)} custom-call(s32[2]{0:T(128)} %get-tuple-element.8.side_ref, f32[6,2,32,384]{3,2,1,0:T(8,128)} %copy-done.4, f32[6,2,32,384]{3,2,1,0:T(8,128)} %shard_map.38.a_ref, f32[6,2,32,384]{3,2,1,0:T(8,128)} %shard_map.37.b_ref, f32[12,2,32,384]{3,2,1,0:T(8,128)} %bitcast.16, f32[12,2,1,384]{3,2,1,0:T(1,128)} %broadcast_in_dim.3.pot_ref), custom_call_target="tpu_custom_call" | custom-call | tf_op jit(solution)/shard_map/pallas_call | solution.py:184
  36.1 0.0 copy-start.2
  36.1 4.3 %collective-permute-done.1.rim_ref = f32[6,2,32,384]{3,2,1,0:T(8,128)S(1)} collective-permute-done((f32[6,2,32,384]{3,2,1,0:T(8,128)}, f32[6,2,32,384]{3,2,1,0:T(8,128)S(1)}, u32[]{:S(2)}, u32[]{:S(2)}) %collective-permute-start.1) | collective-permute-done | bytes 589856 | tf_op jit(solution)/shard_map/ppermute | solution.py:198
  40.4 0.0 copy-start.3
  40.4 0.8 copy-done.3
  41.2 5.1 %shard_map.39 = f32[6,2,32,384]{3,2,1,0:T(8,128)} custom-call(s32[2]{0:T(128)} %get-tuple-element.7.side_ref, f32[6,2,32,384]{3,2,1,0:T(8,128)} %copy-done.3, f32[6,2,32,384]{3,2,1,0:T(8,128)} %shard_map.38.a_ref, f32[6,2,32,384]{3,2,1,0:T(8,128)} %shard_map.37.b_ref, f32[12,2,32,384]{3,2,1,0:T(8,128)} %bitcast.17, f32[12,2,1,384]{3,2,1,0:T(1,128)} %broadcast_in_dim.3.pot_ref), custom_call_target="tpu_custom_call" | custom-call | tf_op jit(solution)/shard_map/pallas_call | solution.py:184
  46.3 0.0 copy-done.2
  46.3 1.4 fusion.2
  47.7 0.5 copy.10
  48.1 1.1 reshape.20
  49.2 1.1 copy.11
  50.4 2.6 %reshape.21 = bf16[32,24,384]{2,1,0:T(8,128)(2,1)S(1)} reshape(bf16[32,32,288]{2,1,0:T(8,128)(2,1)} %copy.11) | data formatting | bytes 1179648 | tf_op jit(solution)/shard_map/reshape | solution.py:233
  53.0 45.7 %all_to_all.10 = bf16[32,24,384]{2,1,0:T(8,128)(2,1)S(1)} all-to-all(bf16[32,24,384]{2,1,0:T(8,128)(2,1)S(1)} %reshape.21), channel_id=1, replica_groups=mesh['dom'=16,'band'=32] {'band'}, dimensions={0} | all-to-all | bytes 1179648 | tf_op jit(solution)/shard_map/all_to_all | solution.py:233
  98.7 1.1 reshape.22
  99.8 0.0 copy-done
  99.8 0.8 fusion
  100.6 0.4 copy.12
  101.0 1.4 reshape.23
  102.4 36.1 %all_to_all.11 = bf16[32,24,384]{2,1,0:T(8,128)(2,1)} all-to-all(bf16[32,24,384]{2,1,0:T(8,128)(2,1)S(1)} %reshape.23), channel_id=1, replica_groups=mesh['dom'=16,'band'=32] {'band'}, dimensions={0} | all-to-all | bytes 1179648 | tf_op jit(solution)/shard_map/all_to_all | solution.py:240
  138.4 2.2 %reshape.24 = bf16[32,32,288]{2,1,0:T(8,128)(2,1)S(1)} reshape(bf16[32,24,384]{2,1,0:T(8,128)(2,1)} %all_to_all.11) | data formatting | bytes 1179648 | tf_op jit(solution)/shard_map/reshape | solution.py:241
  140.7 1.1 copy.13
  141.8 3.5 %reshape.25 = bf16[32,12,2,384]{3,2,1,0:T(2,128)(2,1)} reshape(bf16[32,32,288]{2,1,0:T(8,128)(2,1)} %copy.13) | data formatting | bytes 1179648 | tf_op jit(solution)/shard_map/reshape | solution.py:242
Async XLA Ops:
  0.0 99.8 %copy-start = (bf16[1024,1024]{1,0:T(8,128)(2,1)S(1)}, bf16[1024,1024]{1,0:T(8,128)(2,1)}, u32[]{:S(2)}) copy-start(bf16[1024,1024]{1,0:T(8,128)(2,1)} %param.5) | copy-start | bytes 6291460
  0.0 9.7 %copy-start.5 = (f32[12,2,384]{2,1,0:T(2,128)S(1)}, f32[12,2,384]{2,1,0:T(2,128)}, u32[]{:S(2)}) copy-start(f32[12,2,384]{2,1,0:T(2,128)} %param.4) | copy-start | bytes 110596
  1.7 8.7 %copy-start.1 = (f32[32,12,2,384]{3,0,2,1:T(8,128)}, f32[32,12,2,384]{3,0,2,1:T(8,128)S(1)}, u32[]{:S(2)}) copy-start(f32[32,12,2,384]{3,0,2,1:T(8,128)S(1)} %copy.15) | copy-start | bytes 3538948
  2.9 7.4 %collective-permute-start.2 = (f32[6,2,32,384]{3,2,1,0:T(8,128)}, f32[6,2,32,384]{3,2,1,0:T(8,128)}, u32[]{:S(2)}, u32[]{:S(2)}) collective-permute-start(f32[6,2,32,384]{3,2,1,0:T(8,128)} %get-tuple-element.5), channel_id=1, source_target_pairs={{0,32},{32,0},{64,96},{96,64},{128,160},{160,128},{192,224},{224,1... | collective-permute-start | bytes 1769480 | tf_op jit(solution)/shard_map/ppermute | solution.py:198
  5.5 15.1 %collective-permute-start = (f32[6,2,32,384]{3,2,1,0:T(8,128)}, f32[6,2,32,384]{3,2,1,0:T(8,128)}, u32[]{:S(2)}, u32[]{:S(2)}) collective-permute-start(f32[6,2,32,384]{3,2,1,0:T(8,128)} %get-tuple-element.6), channel_id=1, source_target_pairs={{0,480},{32,64},{64,32},{96,128},{128,96},{160,192},{192,160},{224... | collective-permute-start | bytes 1769480 | tf_op jit(solution)/shard_map/ppermute | solution.py:198
  15.1 15.0 %collective-permute-start.3 = (f32[6,2,32,384]{3,2,1,0:T(8,128)}, f32[6,2,32,384]{3,2,1,0:T(8,128)S(1)}, u32[]{:S(2)}, u32[]{:S(2)}) collective-permute-start(f32[6,2,32,384]{3,2,1,0:T(8,128)} %shard_map.38.a_ref), channel_id=1, source_target_pairs={{0,32},{32,0},{64,96},{96,64},{128,160},{160,128},{192,224},{224,1... | collective-permute-start | bytes 1769480 | tf_op jit(solution)/shard_map/ppermute | solution.py:198
  25.3 15.0 %collective-permute-start.1 = (f32[6,2,32,384]{3,2,1,0:T(8,128)}, f32[6,2,32,384]{3,2,1,0:T(8,128)S(1)}, u32[]{:S(2)}, u32[]{:S(2)}) collective-permute-start(f32[6,2,32,384]{3,2,1,0:T(8,128)} %shard_map.37.b_ref), channel_id=1, source_target_pairs={{0,480},{32,64},{64,32},{96,128},{128,96},{160,192},{192,160},{224... | collective-permute-start | bytes 1769480 | tf_op jit(solution)/shard_map/ppermute | solution.py:198
  30.1 0.8 copy-start.4
  36.1 10.2 %copy-start.2 = (f32[6,2,32,384]{3,2,1,0:T(8,128)S(1)}, f32[6,2,32,384]{3,2,1,0:T(8,128)}, u32[]{:S(2)}) copy-start(f32[6,2,32,384]{3,2,1,0:T(8,128)} %shard_map.40) | copy-start | bytes 1769476
  40.4 0.8 copy-start.3

commit v8 on v7

--- a/solution.py
+++ b/solution.py
@@ -121,40 +121,124 @@
     )(left, mid, right, psi, pot)
 
 
-def first_half_kernel(side_ref, rim_ref, mid_ref, pot_ref, out_ref, ext_ref):
+def half_planes(ext_ref, pot_ref, h, base, out_fn, planes):
+    depth, ny = ext_ref.shape[1], ext_ref.shape[3]
+
+    def body(x, carry):
+        for z in range(depth):
+            hv, mid = ham_planes(ext_ref, pot_ref, x, z, ny)
+            out_fn(x, z, hv, mid)
+        return carry
+
+    lax.fori_loop(0, planes, body, 0)
+
+
+def rim_terms(ext_ref, xx, z):
+    acc = None
+    for k in range(1, 7):
+        term = coeffs[k] * (ext_ref[xx + reach + k, z] + ext_ref[xx + reach - k, z])
+        acc = term if acc is None else acc + term
+    return -2.0 * acc
+
+
+def fill_near(side_ref, rim_ref, mid_ref, ext_ref):
     planes = mid_ref.shape[0]
-    depth, ny = out_ref.shape[1], out_ref.shape[3]
     h = side_ref[0]
+    ext_ref[pl.ds((1 - h) * (reach + planes), reach)] = jnp.zeros(rim_ref.shape, jnp.float32)
     ext_ref[pl.ds(reach, planes)] = mid_ref[...]
     ext_ref[pl.ds(h * (reach + planes), reach)] = rim_ref[...]
-    base = h * (planes - reach)
-
-    def body(x, carry):
-        for z in range(depth):
-            hv, mid = ham_planes(ext_ref, pot_ref, base + x, z, ny)
-            out_ref[x, z] = (hv - center_shift * mid) / half_width
-        return carry
-
-    lax.fori_loop(0, planes - reach, body, 0)
-
-
-def second_half_kernel(side_ref, rim_ref, a_ref, b_ref, psi_ref, pot_ref, out_ref, ext_ref):
+    return h
+
+
+def fill_far(side_ref, rim_ref, ext_ref, planes):
+    h = side_ref[0]
+    ext_ref[pl.ds((1 - h) * reach, planes + reach)] = jnp.zeros(
+        (planes + reach,) + rim_ref.shape[1:], jnp.float32
+    )
+    ext_ref[pl.ds(h * (reach + planes), reach)] = rim_ref[...]
+    return h
+
+
+def first_near_kernel(side_ref, rim_ref, mid_ref, pot_ref, done_ref, part_ref, ext_ref):
+    planes = mid_ref.shape[0]
+    half = planes - reach
+    h = fill_near(side_ref, rim_ref, mid_ref, ext_ref)
+    base = h * half
+
+    def out_fn(x, z, hv, mid):
+        mine = (x >= base) & (x < base + half)
+
+        @pl.when(mine)
+        def _():
+            done_ref[x - base, z] = (hv - center_shift * mid) / half_width
+
+        @pl.when(jnp.logical_not(mine))
+        def _():
+            part_ref[x - (1 - h) * half, z] = hv
+
+    half_planes(ext_ref, pot_ref, h, base, out_fn, planes)
+
+
+def first_far_kernel(side_ref, rim_ref, part_ref, mid_ref, out_ref, ext_ref):
+    planes = mid_ref.shape[0]
+    half = planes - reach
+    depth = out_ref.shape[1]
+    h = fill_far(side_ref, rim_ref, ext_ref, planes)
+    base = h * half
+
+    def body(x, carry):
+        for z in range(depth):
+            hv = part_ref[x, z] + rim_terms(ext_ref, base + x, z)
+            out_ref[x, z] = (hv - center_shift * mid_ref[base + x, z]) / half_width
+        return carry
+
+    lax.fori_loop(0, half, body, 0)
+
+
+def second_near_kernel(side_ref, rim_ref, a_ref, b_ref, psi_ref, pot_ref, done_ref, part_ref, ext_ref):
     planes = psi_ref.shape[0]
     half = planes - reach
-    depth, ny = out_ref.shape[1], out_ref.shape[3]
     h = side_ref[0]
     a_side = side_ref[1]
+    ext_ref[pl.ds((1 - h) * (reach + planes), reach)] = jnp.zeros(rim_ref.shape, jnp.float32)
     ext_ref[pl.ds(reach + a_side * half, half)] = a_ref[...]
     ext_ref[pl.ds(reach + (1 - a_side) * half, half)] = b_ref[...]
     ext_ref[pl.ds(h * (reach + planes), reach)] = rim_ref[...]
     base = h * half
 
-    def body(x, carry):
-        for z in range(depth):
-            hv, mid = ham_planes(ext_ref, pot_ref, base + x, z, ny)
+    def out_fn(x, z, hv, mid):
+        mine = (x >= base) & (x < base + half)
+
+        @pl.when(mine)
+        def _():
+            done_ref[x - base, z] = (
+                2.0 / half_width * (hv - center_shift * mid) - psi_ref[x, z]
+            )
+
+        @pl.when(jnp.logical_not(mine))
+        def _():
+            part_ref[x - (1 - h) * half, z] = hv
+
+    half_planes(ext_ref, pot_ref, h, base, out_fn, planes)
+
+
+def second_far_kernel(side_ref, rim_ref, part_ref, a_ref, b_ref, psi_ref, out_ref, ext_ref):
+    planes = psi_ref.shape[0]
+    half = planes - reach
+    depth = out_ref.shape[1]
+    h = fill_far(side_ref, rim_ref, ext_ref, planes)
+    a_side = side_ref[1]
+    base = h * half
+    mids = (b_ref, a_ref)
+
+    def body(x, carry):
+        for z in range(depth):
+            hv = part_ref[x, z] + rim_terms(ext_ref, base + x, z)
+            mid = jnp.where(h == a_side, a_ref[x, z], b_ref[x, z])
             out_ref[x, z] = 2.0 / half_width * (hv - center_shift * mid) - psi_ref[base + x, z]
         return carry
 
+    del mids
     lax.fori_loop(0, half, body, 0)
 
 
@@ -166,29 +250,19 @@
     return pl.BlockSpec(shape, lambda i: (0,) * len(shape))
 
 
-def run_first_half(side, rim, mid, pot):
-    planes, depth, states, ny = mid.shape
-    half = (planes - reach, depth, states, ny)
+def call(kernel, args, outs, ext_shape):
+    specs = [smem()] + [whole(a.shape) for a in args[1:]]
+    many = isinstance(outs, list)
     return pl.pallas_call(
-        first_half_kernel,
+        kernel,
         grid=(1,),
-        in_specs=[smem(), whole(rim.shape), whole(mid.shape), whole(pot.shape)],
-        out_specs=whole(half),
-        out_shape=jax.ShapeDtypeStruct(half, jnp.float32),
-        scratch_shapes=[pltpu.VMEM((planes + 2 * reach, depth, states, ny), jnp.float32)],
-    )(side, rim, mid, pot)
-
-
-def run_second_half(side, rim, a, b, psi, pot):
-    planes, depth, states, ny = psi.shape
-    return pl.pallas_call(
-        second_half_kernel,
-        grid=(1,),
-        in_specs=[smem(), whole(rim.shape), whole(a.shape), whole(b.shape), whole(psi.shape), whole(pot.shape)],
-        out_specs=whole(a.shape),
-        out_shape=jax.ShapeDtypeStruct(a.shape, jnp.float32),
-        scratch_shapes=[pltpu.VMEM((planes + 2 * reach, depth, states, ny), jnp.float32)],
-    )(side, rim, a, b, psi, pot)
+        in_specs=specs,
+        out_specs=[whole(o) for o in outs] if many else whole(outs),
+        out_shape=[jax.ShapeDtypeStruct(o, jnp.float32) for o in outs]
+        if many
+        else jax.ShapeDtypeStruct(outs, jnp.float32),
+        scratch_shapes=[pltpu.VMEM(ext_shape, jnp.float32)],
+    )(*args)
 
 
 def inner_outer(send_inner, send_outer):
@@ -212,13 +286,19 @@
         hi = jnp.where(even, 1, 0).astype(jnp.int32)
         head, tail = psi_t[:reach], psi_t[planes - reach :]
         rim_in, rim_out = inner_outer(jnp.where(even, tail, head), jnp.where(even, head, tail))
-        part_a = run_first_half(hi.reshape(1), rim_in, psi_t, pot_t)
-        part_b = run_first_half((1 - hi).reshape(1), rim_out, psi_t, pot_t)
+        half = (planes - reach, depth, own_states, ny)
+        ext_shape = (planes + 2 * reach, depth, own_states, ny)
+        part_a, near_b = call(first_near_kernel, (hi.reshape(1), rim_in, psi_t, pot_t), [half, half], ext_shape)
+        part_b = call(first_far_kernel, ((1 - hi).reshape(1), rim_out, near_b, psi_t), half, ext_shape)
         rim_in, rim_out = inner_outer(part_a, part_b)
         sides_a = jnp.stack([hi, hi])
         sides_b = jnp.stack([1 - hi, hi])
-        second_a = run_second_half(sides_a, rim_in, part_a, part_b, psi_t, pot_t)
-        second_b = run_second_half(sides_b, rim_out, part_a, part_b, psi_t, pot_t)
+        second_a, near_b = call(
+            second_near_kernel, (sides_a, rim_in, part_a, part_b, psi_t, pot_t), [half, half], ext_shape
+        )
+        second_b = call(
+            second_far_kernel, (sides_b, rim_out, near_b, part_a, part_b, psi_t), half, ext_shape
+        )
         second = jnp.where(
             even,
             jnp.concatenate([second_b, second_a], axis=0),

time: 148 us -> 150 us (1.014); the launches traced: 145 us -> 149 us
  waiting for transfers between devices: 7.91 us -> 0.11 us
  blocking collectives: 81.8 us -> 88.8 us
  Pallas kernels: 19.6 us -> 23.6 us
    ppermute x2, waiting for transfers between devices: 7.91 us -> 0.1 us  [inner_outer(): lax.ppermute(send_outer, 'dom', outer)]
    pallas_call x4, Pallas kernels: 19.6 us -> 23.6 us  [call(): pl.pallas_call(kernel, grid=(1,), in_specs=specs, out_specs=[whole(o) for...]
    all_to_all x1, blocking collectives: 45.7 us -> 49.5 us  [per_device(): gathered = lax.all_to_all(blocks.reshape(wire), 'band', 0, 0, tiled=True)]
    all_to_all x1, blocking collectives: 36.1 us -> 39.3 us  [per_device(): back = lax.all_to_all(mixed.reshape(wire), 'band', 0, 0, tiled=True)]
  transfers between devices with their start and end apart: 4 -> 4, of which waited for: 2 -> 1; matrix products, arithmetic and copies ran while one was open for 1% -> 1% of each run, Pallas kernels for 10% -> 13%
where the time goes in v8:
time: 150 us; the launch traced here: 149 us
  blocking collectives  88.8 us (59%)
  Pallas kernels  23.6 us (16%)
  local copies, waits for them, and re-layouts  18.9 us (13%)
  starting transfers between devices  13.6 us (9%)
  other arithmetic  3.27 us (2%)
    all_to_all x1, blocking collectives, per_device(): gathered = lax.all_to_all(blocks.reshape(wire), 'band', 0, 0, tiled=True)  49.5 us
    all_to_all x1, blocking collectives, per_device(): back = lax.all_to_all(mixed.reshape(wire), 'band', 0, 0, tiled=True)  39.3 us
    pallas_call x4, Pallas kernels, call(): pl.pallas_call(kernel, grid=(1,), in_specs=specs, out_specs=[whole(o) for...  23.6 us
    ppermute x2, starting transfers between devices, inner_outer(): lax.ppermute(send_outer, 'dom', outer)  9.1 us
    ppermute x2, starting transfers between devices, inner_outer(): lax.ppermute(send_inner, 'dom', inner)  4.48 us
    reshape x1, local copies, waits for them, and re-layouts, per_device(): return result.reshape(psi.shape)  3.52 us
    unnamed x13, local copies, waits for them, and re-layouts  3.3 us
  transfers between devices with their start and end apart: 4, of which 1 were waited for; matrix products, arithmetic and copies ran while one was open for 1% of the time, Pallas kernels for 13%

profile of v8, /device:TPU:25, one launch (start us, length us, event | category | flops | bytes accessed | tf_op | source)
XLA Modules:
  0.0 149.2 jit_solution(1238986591244632976)
XLA Ops:
  0.0 0.0 copy-start
  0.0 0.0 copy-start.5
  0.0 1.7 %copy.15 = f32[32,12,2,384]{3,0,2,1:T(8,128)S(1)} copy(f32[32,12,2,384]{3,2,1,0:T(2,128)} %param.3) | data formatting | bytes 2359296 | tf_op args[0]
  1.7 0.0 copy-start.1
  1.7 1.3 slice_select_fusion
  3.0 2.6 %collective-permute-start.1 = (f32[6,2,32,384]{3,2,1,0:T(8,128)}, f32[6,2,32,384]{3,2,1,0:T(8,128)}, u32[]{:S(2)}, u32[]{:S(2)}) collective-permute-start(f32[6,2,32,384]{3,2,1,0:T(8,128)} %get-tuple-element.13), channel_id=1, source_target_pairs={{0,32},{32,0},{64,96},{96,64},{128,160},{160,128},{192,224},{224,1... | collective-permute-start | bytes 1769480 | tf_op jit(solution)/shard_map/ppermute | solution.py:272
  5.5 4.2 %collective-permute-start = (f32[6,2,32,384]{3,2,1,0:T(8,128)}, f32[6,2,32,384]{3,2,1,0:T(8,128)}, u32[]{:S(2)}, u32[]{:S(2)}) collective-permute-start(f32[6,2,32,384]{3,2,1,0:T(8,128)} %get-tuple-element.14), channel_id=1, source_target_pairs={{0,480},{32,64},{64,32},{96,128},{128,96},{160,192},{192,160},{224... | collective-permute-start | bytes 1769480 | tf_op jit(solution)/shard_map/ppermute | solution.py:272
  9.8 0.0 copy-done.5
  9.8 0.6 broadcast_in_dim.3.pot_ref
  10.4 0.0 collective-permute-done.1.rim_ref
  10.4 0.0 copy-done.1
  10.4 8.3 %shard_map.37 = (f32[6,2,32,384]{3,2,1,0:T(8,128)}, f32[6,2,32,384]{3,2,1,0:T(8,128)}) custom-call(s32[1]{0:T(128)} %bitcast.1.side_ref, f32[6,2,32,384]{3,2,1,0:T(8,128)} %collective-permute-done.1.rim_ref, f32[12,2,32,384]{3,2,1,0:T(8,128)} %bitcast.14, f32[12,2,1,384]{3,2,1,0:T(1,128)} %broadcast_in_dim.3.pot_ref), custom_call_target="tpu_custom_call" | custom-call | tf_op jit(solution)/shard_map/pallas_call | solution.py:256
  18.7 1.9 %collective-permute-start.3 = (f32[6,2,32,384]{3,2,1,0:T(8,128)}, f32[6,2,32,384]{3,2,1,0:T(8,128)S(1)}, u32[]{:S(2)}, u32[]{:S(2)}) collective-permute-start(f32[6,2,32,384]{3,2,1,0:T(8,128)} %get-tuple-element.10.a_ref), channel_id=1, source_target_pairs={{0,32},{32,0},{64,96},{96,64},{128,160},{160,128},{192,224},{224,1... | collective-permute-start | bytes 1769480 | tf_op jit(solution)/shard_map/ppermute | solution.py:272
  20.6 0.1 collective-permute-done.rim_ref
  20.7 3.1 %shard_map.38.b_ref = f32[6,2,32,384]{3,2,1,0:T(8,128)} custom-call(s32[1]{0:T(128)} %bitcast.side_ref, f32[6,2,32,384]{3,2,1,0:T(8,128)} %collective-permute-done.rim_ref, f32[6,2,32,384]{3,2,1,0:T(8,128)} %get-tuple-element.9.part_ref, f32[12,2,32,384]{3,2,1,0:T(8,128)} %bitcast.15), custom_call_target="tpu_custom_call" | custom-call | tf_op jit(solution)/shard_map/pallas_call | solution.py:256
  23.8 4.9 %collective-permute-start.2 = (f32[6,2,32,384]{3,2,1,0:T(8,128)}, f32[6,2,32,384]{3,2,1,0:T(8,128)S(1)}, u32[]{:S(2)}, u32[]{:S(2)}) collective-permute-start(f32[6,2,32,384]{3,2,1,0:T(8,128)} %shard_map.38.b_ref), channel_id=1, source_target_pairs={{0,480},{32,64},{64,32},{96,128},{128,96},{160,192},{192,160},{224... | collective-permute-start | bytes 1769480 | tf_op jit(solution)/shard_map/ppermute | solution.py:272
  28.7 0.6 pad_add_fusion
  29.3 0.0 collective-permute-done.3.rim_ref
  29.3 0.0 copy-start.3
  29.3 0.8 copy-done.3
  30.1 8.7 %shard_map.39 = (f32[6,2,32,384]{3,2,1,0:T(8,128)}, f32[6,2,32,384]{3,2,1,0:T(8,128)}) custom-call(s32[2]{0:T(128)} %get-tuple-element.16.side_ref, f32[6,2,32,384]{3,2,1,0:T(8,128)} %copy-done.3, f32[6,2,32,384]{3,2,1,0:T(8,128)} %get-tuple-element.10.a_ref, f32[6,2,32,384]{3,2,1,0:T(8,128)} %shard_map.38.b_ref, f32[12,2,32,384]{3,2,1,0:T(8,128)} %bitcast.16, ...), custom_call_target="tpu_custom_call" | custom-call | tf_op jit(solution)/shard_map/pallas_call | solution.py:256
  38.8 0.0 copy-start.4
  38.8 0.0 collective-permute-done.2.rim_ref
  38.8 0.0 copy-start.2
  38.8 0.8 copy-done.2
  39.6 3.5 %shard_map.40 = f32[6,2,32,384]{3,2,1,0:T(8,128)} custom-call(s32[2]{0:T(128)} %get-tuple-element.15.side_ref, f32[6,2,32,384]{3,2,1,0:T(8,128)} %copy-done.2, f32[6,2,32,384]{3,2,1,0:T(8,128)} %get-tuple-element.11.part_ref, f32[6,2,32,384]{3,2,1,0:T(8,128)} %get-tuple-element.10.a_ref, f32[6,2,32,384]{3,2,1,0:T(8,128)} %shard_map.38.b_ref, ...), custom_call_target="tpu_custom_call" | custom-call | tf_op jit(solution)/shard_map/pallas_call | solution.py:256
  43.1 0.0 copy-done.4
  43.1 1.4 fusion.2
  44.5 0.5 copy.10
  45.0 1.1 reshape.20
  46.1 1.2 copy.11
  47.2 2.6 %reshape.21 = bf16[32,24,384]{2,1,0:T(8,128)(2,1)S(1)} reshape(bf16[32,32,288]{2,1,0:T(8,128)(2,1)} %copy.11) | data formatting | bytes 1179648 | tf_op jit(solution)/shard_map/reshape | solution.py:313
  49.8 49.5 %all_to_all.10 = bf16[32,24,384]{2,1,0:T(8,128)(2,1)S(1)} all-to-all(bf16[32,24,384]{2,1,0:T(8,128)(2,1)S(1)} %reshape.21), channel_id=1, replica_groups=mesh['dom'=16,'band'=32] {'band'}, dimensions={0} | all-to-all | bytes 1179648 | tf_op jit(solution)/shard_map/all_to_all | solution.py:313
  99.3 1.1 reshape.22
  100.4 0.0 copy-done
  100.4 0.8 fusion
  101.2 0.4 copy.12
  101.6 1.4 reshape.23
  103.0 39.3 %all_to_all.11 = bf16[32,24,384]{2,1,0:T(8,128)(2,1)} all-to-all(bf16[32,24,384]{2,1,0:T(8,128)(2,1)S(1)} %reshape.23), channel_id=1, replica_groups=mesh['dom'=16,'band'=32] {'band'}, dimensions={0} | all-to-all | bytes 1179648 | tf_op jit(solution)/shard_map/all_to_all | solution.py:320
  142.2 2.2 %reshape.24 = bf16[32,32,288]{2,1,0:T(8,128)(2,1)S(1)} reshape(bf16[32,24,384]{2,1,0:T(8,128)(2,1)} %all_to_all.11) | data formatting | bytes 1179648 | tf_op jit(solution)/shard_map/reshape | solution.py:321
  144.5 1.2 copy.13
  145.6 3.5 %reshape.25 = bf16[32,12,2,384]{3,2,1,0:T(2,128)(2,1)} reshape(bf16[32,32,288]{2,1,0:T(8,128)(2,1)} %copy.13) | data formatting | bytes 1179648 | tf_op jit(solution)/shard_map/reshape | solution.py:322
Async XLA Ops:
  0.0 100.4 %copy-start = (bf16[1024,1024]{1,0:T(8,128)(2,1)S(1)}, bf16[1024,1024]{1,0:T(8,128)(2,1)}, u32[]{:S(2)}) copy-start(bf16[1024,1024]{1,0:T(8,128)(2,1)} %param.5) | copy-start | bytes 6291460
  0.0 9.8 %copy-start.5 = (f32[12,2,384]{2,1,0:T(2,128)S(1)}, f32[12,2,384]{2,1,0:T(2,128)}, u32[]{:S(2)}) copy-start(f32[12,2,384]{2,1,0:T(2,128)} %param.4) | copy-start | bytes 110596
  1.7 8.8 %copy-start.1 = (f32[32,12,2,384]{3,0,2,1:T(8,128)}, f32[32,12,2,384]{3,0,2,1:T(8,128)S(1)}, u32[]{:S(2)}) copy-start(f32[32,12,2,384]{3,0,2,1:T(8,128)S(1)} %copy.15) | copy-start | bytes 3538948
  3.0 7.5 %collective-permute-start.1 = (f32[6,2,32,384]{3,2,1,0:T(8,128)}, f32[6,2,32,384]{3,2,1,0:T(8,128)}, u32[]{:S(2)}, u32[]{:S(2)}) collective-permute-start(f32[6,2,32,384]{3,2,1,0:T(8,128)} %get-tuple-element.13), channel_id=1, source_target_pairs={{0,32},{32,0},{64,96},{96,64},{128,160},{160,128},{192,224},{224,1... | collective-permute-start | bytes 1769480 | tf_op jit(solution)/shard_map/ppermute | solution.py:272
  5.5 15.1 %collective-permute-start = (f32[6,2,32,384]{3,2,1,0:T(8,128)}, f32[6,2,32,384]{3,2,1,0:T(8,128)}, u32[]{:S(2)}, u32[]{:S(2)}) collective-permute-start(f32[6,2,32,384]{3,2,1,0:T(8,128)} %get-tuple-element.14), channel_id=1, source_target_pairs={{0,480},{32,64},{64,32},{96,128},{128,96},{160,192},{192,160},{224... | collective-permute-start | bytes 1769480 | tf_op jit(solution)/shard_map/ppermute | solution.py:272
  18.7 10.6 %collective-permute-start.3 = (f32[6,2,32,384]{3,2,1,0:T(8,128)}, f32[6,2,32,384]{3,2,1,0:T(8,128)S(1)}, u32[]{:S(2)}, u32[]{:S(2)}) collective-permute-start(f32[6,2,32,384]{3,2,1,0:T(8,128)} %get-tuple-element.10.a_ref), channel_id=1, source_target_pairs={{0,32},{32,0},{64,96},{96,64},{128,160},{160,128},{192,224},{224,1... | collective-permute-start | bytes 1769480 | tf_op jit(solution)/shard_map/ppermute | solution.py:272
  23.8 15.0 %collective-permute-start.2 = (f32[6,2,32,384]{3,2,1,0:T(8,128)}, f32[6,2,32,384]{3,2,1,0:T(8,128)S(1)}, u32[]{:S(2)}, u32[]{:S(2)}) collective-permute-start(f32[6,2,32,384]{3,2,1,0:T(8,128)} %shard_map.38.b_ref), channel_id=1, source_target_pairs={{0,480},{32,64},{64,32},{96,128},{128,96},{160,192},{192,160},{224... | collective-permute-start | bytes 1769480 | tf_op jit(solution)/shard_map/ppermute | solution.py:272
  29.3 0.8 copy-start.3
  38.8 4.4 %copy-start.4 = (f32[6,2,32,384]{3,2,1,0:T(8,128)S(1)}, f32[6,2,32,384]{3,2,1,0:T(8,128)}, u32[]{:S(2)}) copy-start(f32[6,2,32,384]{3,2,1,0:T(8,128)} %get-tuple-element.12) | copy-start | bytes 1769476
  38.8 0.8 copy-start.2

commit v9 on v7

--- a/solution.py
+++ b/solution.py
@@ -210,8 +210,10 @@
     else:
         even = lax.axis_index("dom") % 2 == 0
         hi = jnp.where(even, 1, 0).astype(jnp.int32)
-        head, tail = psi_t[:reach], psi_t[planes - reach :]
-        rim_in, rim_out = inner_outer(jnp.where(even, tail, head), jnp.where(even, head, tail))
+        rim_in, rim_out = inner_outer(
+            lax.dynamic_slice_in_dim(psi, hi * reach, reach, 1).transpose(1, 2, 0, 3),
+            lax.dynamic_slice_in_dim(psi, (1 - hi) * reach, reach, 1).transpose(1, 2, 0, 3),
+        )
         part_a = run_first_half(hi.reshape(1), rim_in, psi_t, pot_t)
         part_b = run_first_half((1 - hi).reshape(1), rim_out, psi_t, pot_t)
         rim_in, rim_out = inner_outer(part_a, part_b)

time: 148 us -> 150 us (1.014)
  the two profiles are of different devices: /device:TPU:25 before, /device:TPU:2 now
where the time goes in v9:
time: 150 us; the launch traced here: 149 us
  blocking collectives  86.6 us (58%)
  local copies, waits for them, and re-layouts  20.8 us (14%)
  Pallas kernels  19.6 us (13%)
  starting transfers between devices  17 us (11%)
  waiting for transfers between devices  2.3 us (2%)
  other arithmetic  2.05 us (1%)
    all_to_all x1, blocking collectives, per_device(): gathered = lax.all_to_all(blocks.reshape(wire), 'band', 0, 0, tiled=True)  48.9 us
    all_to_all x1, blocking collectives, per_device(): back = lax.all_to_all(mixed.reshape(wire), 'band', 0, 0, tiled=True)  37.6 us
    ppermute x2, starting transfers between devices, inner_outer(): lax.ppermute(send_outer, 'dom', outer)  13.2 us
    pallas_call x2, Pallas kernels, run_second_half(): pl.pallas_call(second_half_kernel, grid=(1,), in_specs=[smem(), whole(rim...  10.2 us
    pallas_call x2, Pallas kernels, run_first_half(): pl.pallas_call(first_half_kernel, grid=(1,), in_specs=[smem(), whole(rim....  9.41 us
    unnamed x15, local copies, waits for them, and re-layouts  4.14 us
    ppermute x2, starting transfers between devices, inner_outer(): lax.ppermute(send_inner, 'dom', inner)  3.82 us
    reshape x1, local copies, waits for them, and re-layouts, per_device(): return result.reshape(psi.shape)  3.52 us
  transfers between devices with their start and end apart: 4, of which 2 were waited for; matrix products, arithmetic and copies ran while one was open for 1% of the time, Pallas kernels for 10%

profile of v9, /device:TPU:2, one launch (start us, length us, event | category | flops | bytes accessed | tf_op | source)
XLA Modules:
  0.0 149.2 jit_solution(8703969008615361135)
XLA Ops:
  0.0 0.0 copy-start
  0.0 0.0 copy-start.6
  0.0 1.7 %copy.22 = f32[32,12,2,384]{3,0,2,1:T(8,128)S(1)} copy(f32[32,12,2,384]{3,2,1,0:T(2,128)} %param.3) | data formatting | bytes 2359296 | tf_op args[0]
  1.7 0.0 copy-start.1
  1.7 1.1 dynamic-slice_bitcast_fusion
  2.7 1.9 %collective-permute-start.2 = (f32[6,2,32,384]{3,2,1,0:T(8,128)S(1)}, f32[6,2,32,384]{3,2,1,0:T(8,128)S(1)}, u32[]{:S(2)}, u32[]{:S(2)}) collective-permute-start(f32[6,2,32,384]{3,2,1,0:T(8,128)S(1)} %get-tuple-element.5), channel_id=1, source_target_pairs={{0,32},{32,0},{64,96},{96,64},{128,160},{160,128},{192,224},{224,1... | collective-permute-start | bytes 1769480 | tf_op jit(solution)/shard_map/ppermute | solution.py:198
  4.7 6.6 %collective-permute-start = (f32[6,2,32,384]{3,2,1,0:T(8,128)}, f32[6,2,32,384]{3,2,1,0:T(8,128)}, u32[]{:S(2)}, u32[]{:S(2)}) collective-permute-start(f32[6,2,32,384]{3,2,1,0:T(8,128)} %get-tuple-element.6), channel_id=1, source_target_pairs={{0,480},{32,64},{64,32},{96,128},{128,96},{160,192},{192,160},{224... | collective-permute-start | bytes 1769480 | tf_op jit(solution)/shard_map/ppermute | solution.py:198
  11.3 0.0 copy-done.6
  11.3 0.6 broadcast_in_dim.3.pot_ref
  11.9 0.0 collective-permute-done.2.rim_ref
  11.9 0.0 copy-start.5
  11.9 0.8 copy-done.5
  12.7 0.0 copy-done.1
  12.7 4.7 %shard_map.38.a_ref = f32[6,2,32,384]{3,2,1,0:T(8,128)} custom-call(s32[1]{0:T(128)} %bitcast.1.side_ref, f32[6,2,32,384]{3,2,1,0:T(8,128)} %copy-done.5, f32[12,2,32,384]{3,2,1,0:T(8,128)} %bitcast.17, f32[12,2,1,384]{3,2,1,0:T(1,128)} %broadcast_in_dim.3.pot_ref), custom_call_target="tpu_custom_call" | custom-call | tf_op jit(solution)/shard_map/pallas_call | solution.py:172
  17.4 1.9 %collective-permute-start.3 = (f32[6,2,32,384]{3,2,1,0:T(8,128)}, f32[6,2,32,384]{3,2,1,0:T(8,128)S(1)}, u32[]{:S(2)}, u32[]{:S(2)}) collective-permute-start(f32[6,2,32,384]{3,2,1,0:T(8,128)} %shard_map.38.a_ref), channel_id=1, source_target_pairs={{0,32},{32,0},{64,96},{96,64},{128,160},{160,128},{192,224},{224,1... | collective-permute-start | bytes 1769480 | tf_op jit(solution)/shard_map/ppermute | solution.py:198
  19.4 0.4 collective-permute-done.rim_ref
  19.8 4.7 %shard_map.37.b_ref = f32[6,2,32,384]{3,2,1,0:T(8,128)} custom-call(s32[1]{0:T(128)} %bitcast.side_ref, f32[6,2,32,384]{3,2,1,0:T(8,128)} %collective-permute-done.rim_ref, f32[12,2,32,384]{3,2,1,0:T(8,128)} %bitcast.18, f32[12,2,1,384]{3,2,1,0:T(1,128)} %broadcast_in_dim.3.pot_ref), custom_call_target="tpu_custom_call" | custom-call | tf_op jit(solution)/shard_map/pallas_call | solution.py:172
  24.5 6.6 %collective-permute-start.1 = (f32[6,2,32,384]{3,2,1,0:T(8,128)}, f32[6,2,32,384]{3,2,1,0:T(8,128)S(1)}, u32[]{:S(2)}, u32[]{:S(2)}) collective-permute-start(f32[6,2,32,384]{3,2,1,0:T(8,128)} %shard_map.37.b_ref), channel_id=1, source_target_pairs={{0,480},{32,64},{64,32},{96,128},{128,96},{160,192},{192,160},{224... | collective-permute-start | bytes 1769480 | tf_op jit(solution)/shard_map/ppermute | solution.py:198
  31.1 0.6 pad_add_fusion
  31.7 0.0 collective-permute-done.3.rim_ref
  31.7 0.0 copy-start.4
  31.7 0.8 copy-done.4
  32.6 5.1 %shard_map.40 = f32[6,2,32,384]{3,2,1,0:T(8,128)} custom-call(s32[2]{0:T(128)} %get-tuple-element.10.side_ref, f32[6,2,32,384]{3,2,1,0:T(8,128)} %copy-done.4, f32[6,2,32,384]{3,2,1,0:T(8,128)} %shard_map.38.a_ref, f32[6,2,32,384]{3,2,1,0:T(8,128)} %shard_map.37.b_ref, f32[12,2,32,384]{3,2,1,0:T(8,128)} %bitcast.19, f32[12,2,1,384]{3,2,1,0:T(1,128)} %broadcast_in_dim.3.pot_ref), custom_call_target="tpu_custom_call" | custom-call | tf_op jit(solution)/shard_map/pallas_call | solution.py:184
  37.6 0.0 copy-start.2
  37.6 1.9 %collective-permute-done.1.rim_ref = f32[6,2,32,384]{3,2,1,0:T(8,128)S(1)} collective-permute-done((f32[6,2,32,384]{3,2,1,0:T(8,128)}, f32[6,2,32,384]{3,2,1,0:T(8,128)S(1)}, u32[]{:S(2)}, u32[]{:S(2)}) %collective-permute-start.1) | collective-permute-done | bytes 589856 | tf_op jit(solution)/shard_map/ppermute | solution.py:198
  39.5 0.0 copy-start.3
  39.5 0.8 copy-done.3
  40.3 5.1 %shard_map.39 = f32[6,2,32,384]{3,2,1,0:T(8,128)} custom-call(s32[2]{0:T(128)} %get-tuple-element.9.side_ref, f32[6,2,32,384]{3,2,1,0:T(8,128)} %copy-done.3, f32[6,2,32,384]{3,2,1,0:T(8,128)} %shard_map.38.a_ref, f32[6,2,32,384]{3,2,1,0:T(8,128)} %shard_map.37.b_ref, f32[12,2,32,384]{3,2,1,0:T(8,128)} %bitcast.20, f32[12,2,1,384]{3,2,1,0:T(1,128)} %broadcast_in_dim.3.pot_ref), custom_call_target="tpu_custom_call" | custom-call | tf_op jit(solution)/shard_map/pallas_call | solution.py:184
  45.4 0.0 copy-done.2
  45.4 1.4 fusion.2
  46.8 0.5 copy.16
  47.3 1.1 reshape.20
  48.4 1.1 copy.17
  49.5 2.6 %reshape.21 = bf16[32,24,384]{2,1,0:T(8,128)(2,1)S(1)} reshape(bf16[32,32,288]{2,1,0:T(8,128)(2,1)} %copy.17) | data formatting | bytes 1179648 | tf_op jit(solution)/shard_map/reshape | solution.py:235
  52.1 48.9 %all_to_all.10 = bf16[32,24,384]{2,1,0:T(8,128)(2,1)S(1)} all-to-all(bf16[32,24,384]{2,1,0:T(8,128)(2,1)S(1)} %reshape.21), channel_id=1, replica_groups=mesh['dom'=16,'band'=32] {'band'}, dimensions={0} | all-to-all | bytes 1179648 | tf_op jit(solution)/shard_map/all_to_all | solution.py:235
  101.0 1.1 reshape.22
  102.1 0.0 copy-done
  102.2 0.8 fusion
  103.0 0.4 copy.18
  103.3 1.4 reshape.23
  104.7 37.6 %all_to_all.11 = bf16[32,24,384]{2,1,0:T(8,128)(2,1)} all-to-all(bf16[32,24,384]{2,1,0:T(8,128)(2,1)S(1)} %reshape.23), channel_id=1, replica_groups=mesh['dom'=16,'band'=32] {'band'}, dimensions={0} | all-to-all | bytes 1179648 | tf_op jit(solution)/shard_map/all_to_all | solution.py:242
  142.3 2.2 %reshape.24 = bf16[32,32,288]{2,1,0:T(8,128)(2,1)S(1)} reshape(bf16[32,24,384]{2,1,0:T(8,128)(2,1)} %all_to_all.11) | data formatting | bytes 1179648 | tf_op jit(solution)/shard_map/reshape | solution.py:243
  144.6 1.1 copy.19
  145.7 3.5 %reshape.25 = bf16[32,12,2,384]{3,2,1,0:T(2,128)(2,1)} reshape(bf16[32,32,288]{2,1,0:T(8,128)(2,1)} %copy.19) | data formatting | bytes 1179648 | tf_op jit(solution)/shard_map/reshape | solution.py:244
Async XLA Ops:
  0.0 102.1 %copy-start = (bf16[1024,1024]{1,0:T(8,128)(2,1)S(1)}, bf16[1024,1024]{1,0:T(8,128)(2,1)}, u32[]{:S(2)}) copy-start(bf16[1024,1024]{1,0:T(8,128)(2,1)} %param.5) | copy-start | bytes 6291460
  0.0 11.3 %copy-start.6 = (f32[12,2,384]{2,1,0:T(2,128)S(1)}, f32[12,2,384]{2,1,0:T(2,128)}, u32[]{:S(2)}) copy-start(f32[12,2,384]{2,1,0:T(2,128)} %param.4) | copy-start | bytes 110596
  1.7 11.1 %copy-start.1 = (f32[32,12,2,384]{3,0,2,1:T(8,128)}, f32[32,12,2,384]{3,0,2,1:T(8,128)S(1)}, u32[]{:S(2)}) copy-start(f32[32,12,2,384]{3,0,2,1:T(8,128)S(1)} %copy.22) | copy-start | bytes 3538948
  2.7 9.2 %collective-permute-start.2 = (f32[6,2,32,384]{3,2,1,0:T(8,128)S(1)}, f32[6,2,32,384]{3,2,1,0:T(8,128)S(1)}, u32[]{:S(2)}, u32[]{:S(2)}) collective-permute-start(f32[6,2,32,384]{3,2,1,0:T(8,128)S(1)} %get-tuple-element.5), channel_id=1, source_target_pairs={{0,32},{32,0},{64,96},{96,64},{128,160},{160,128},{192,224},{224,1... | collective-permute-start | bytes 1769480 | tf_op jit(solution)/shard_map/ppermute | solution.py:198
  4.7 15.1 %collective-permute-start = (f32[6,2,32,384]{3,2,1,0:T(8,128)}, f32[6,2,32,384]{3,2,1,0:T(8,128)}, u32[]{:S(2)}, u32[]{:S(2)}) collective-permute-start(f32[6,2,32,384]{3,2,1,0:T(8,128)} %get-tuple-element.6), channel_id=1, source_target_pairs={{0,480},{32,64},{64,32},{96,128},{128,96},{160,192},{192,160},{224... | collective-permute-start | bytes 1769480 | tf_op jit(solution)/shard_map/ppermute | solution.py:198
  11.9 0.8 copy-start.5
  17.4 14.3 %collective-permute-start.3 = (f32[6,2,32,384]{3,2,1,0:T(8,128)}, f32[6,2,32,384]{3,2,1,0:T(8,128)S(1)}, u32[]{:S(2)}, u32[]{:S(2)}) collective-permute-start(f32[6,2,32,384]{3,2,1,0:T(8,128)} %shard_map.38.a_ref), channel_id=1, source_target_pairs={{0,32},{32,0},{64,96},{96,64},{128,160},{160,128},{192,224},{224,1... | collective-permute-start | bytes 1769480 | tf_op jit(solution)/shard_map/ppermute | solution.py:198
  24.5 15.0 %collective-permute-start.1 = (f32[6,2,32,384]{3,2,1,0:T(8,128)}, f32[6,2,32,384]{3,2,1,0:T(8,128)S(1)}, u32[]{:S(2)}, u32[]{:S(2)}) collective-permute-start(f32[6,2,32,384]{3,2,1,0:T(8,128)} %shard_map.37.b_ref), channel_id=1, source_target_pairs={{0,480},{32,64},{64,32},{96,128},{128,96},{160,192},{192,160},{224... | collective-permute-start | bytes 1769480 | tf_op jit(solution)/shard_map/ppermute | solution.py:198
  31.7 0.8 copy-start.4
  37.6 7.8 %copy-start.2 = (f32[6,2,32,384]{3,2,1,0:T(8,128)S(1)}, f32[6,2,32,384]{3,2,1,0:T(8,128)}, u32[]{:S(2)}) copy-start(f32[6,2,32,384]{3,2,1,0:T(8,128)} %shard_map.40) | copy-start | bytes 1769476
  39.5 0.8 copy-start.3

commit v10 on v7

--- a/solution.py
+++ b/solution.py
@@ -219,10 +219,10 @@
         sides_b = jnp.stack([1 - hi, hi])
         second_a = run_second_half(sides_a, rim_in, part_a, part_b, psi_t, pot_t)
         second_b = run_second_half(sides_b, rim_out, part_a, part_b, psi_t, pot_t)
-        second = jnp.where(
-            even,
-            jnp.concatenate([second_b, second_a], axis=0),
-            jnp.concatenate([second_a, second_b], axis=0),
+        second = jnp.zeros(psi_t.shape, jnp.bfloat16)
+        second = lax.dynamic_update_slice_in_dim(second, second_a.astype(jnp.bfloat16), hi * reach, 0)
+        second = lax.dynamic_update_slice_in_dim(
+            second, second_b.astype(jnp.bfloat16), (1 - hi) * reach, 0
         )
     filtered = second.astype(jnp.bfloat16).transpose(2, 0, 1, 3)
     rows = planes * depth

time: 148 us -> 157 us (1.061); the launches traced: 145 us -> 157 us
  blocking collectives: 81.8 us -> 89.2 us
  waiting for transfers between devices: 7.91 us -> 10.6 us
    all_to_all x1, blocking collectives: 45.7 us -> 49.6 us  [per_device(): gathered = lax.all_to_all(blocks.reshape(wire), 'band', 0, 0, tiled=True)]
    all_to_all x1, blocking collectives: 36.1 us -> 39.6 us  [per_device(): back = lax.all_to_all(mixed.reshape(wire), 'band', 0, 0, tiled=True)]
    ppermute x2, waiting for transfers between devices: 7.91 us -> 10.6 us  [inner_outer(): lax.ppermute(send_outer, 'dom', outer)]
    convert_element_type x0 -> x2, other arithmetic: none -> 2.2 us  [the longest x1 1.1 us: per_device(): second_b.astype(jnp.bfloat16)]
    unnamed x13 -> x9, local copies, waits for them, and re-layouts: 3.32 us -> 2.48 us
  transfers between devices with their start and end apart: 4 -> 4, of which waited for: 2 -> 2; matrix products, arithmetic and copies ran while one was open for 1% -> 2% of each run, Pallas kernels for 10% -> 9%
where the time goes in v10:
time: 157 us
  blocking collectives  89.2 us (57%)
  Pallas kernels  19.6 us (12%)
  local copies, waits for them, and re-layouts  18.5 us (12%)
  starting transfers between devices  13.6 us (9%)
  waiting for transfers between devices  10.6 us (7%)
  other arithmetic  4.12 us (3%)
    all_to_all x1, blocking collectives, per_device(): gathered = lax.all_to_all(blocks.reshape(wire), 'band', 0, 0, tiled=True)  49.6 us
    all_to_all x1, blocking collectives, per_device(): back = lax.all_to_all(mixed.reshape(wire), 'band', 0, 0, tiled=True)  39.6 us
    ppermute x2, waiting for transfers between devices, inner_outer(): lax.ppermute(send_outer, 'dom', outer)  10.6 us
    pallas_call x2, Pallas kernels, run_second_half(): pl.pallas_call(second_half_kernel, grid=(1,), in_specs=[smem(), whole(rim...  10.2 us
    ppermute x2, starting transfers between devices, inner_outer(): lax.ppermute(send_outer, 'dom', outer)  9.72 us
    pallas_call x2, Pallas kernels, run_first_half(): pl.pallas_call(first_half_kernel, grid=(1,), in_specs=[smem(), whole(rim....  9.43 us
    ppermute x2, starting transfers between devices, inner_outer(): lax.ppermute(send_inner, 'dom', inner)  3.83 us
    reshape x1, local copies, waits for them, and re-layouts, per_device(): return result.reshape(psi.shape)  3.52 us
  transfers between devices with their start and end apart: 4, of which 2 were waited for; matrix products, arithmetic and copies ran while one was open for 2% of the time, Pallas kernels for 9%

profile of v10, /device:TPU:25, one launch (start us, length us, event | category | flops | bytes accessed | tf_op | source)
XLA Modules:
  0.0 156.6 jit_solution(11045830498117494935)
XLA Ops:
  0.0 0.0 copy-start
  0.0 0.0 copy-start.3
  0.0 1.7 %copy.19 = f32[32,12,2,384]{3,0,2,1:T(8,128)S(1)} copy(f32[32,12,2,384]{3,2,1,0:T(2,128)} %param.3) | data formatting | bytes 2359296 | tf_op args[0]
  1.7 0.0 copy-start.1
  1.7 1.3 slice_select_fusion
  2.9 4.9 %collective-permute-start.2 = (f32[6,2,32,384]{3,2,1,0:T(8,128)}, f32[6,2,32,384]{3,2,1,0:T(8,128)}, u32[]{:S(2)}, u32[]{:S(2)}) collective-permute-start(f32[6,2,32,384]{3,2,1,0:T(8,128)} %get-tuple-element.5), channel_id=1, source_target_pairs={{0,480},{32,64},{64,32},{96,128},{128,96},{160,192},{192,160},{224... | collective-permute-start | bytes 1769480 | tf_op jit(solution)/shard_map/ppermute | solution.py:198
  7.8 1.9 %collective-permute-start = (f32[6,2,32,384]{3,2,1,0:T(8,128)}, f32[6,2,32,384]{3,2,1,0:T(8,128)}, u32[]{:S(2)}, u32[]{:S(2)}) collective-permute-start(f32[6,2,32,384]{3,2,1,0:T(8,128)} %get-tuple-element.6), channel_id=1, source_target_pairs={{0,32},{32,0},{64,96},{96,64},{128,160},{160,128},{192,224},{224,1... | collective-permute-start | bytes 1769480 | tf_op jit(solution)/shard_map/ppermute | solution.py:198
  9.7 0.0 copy-done.3
  9.7 0.6 broadcast_in_dim.7.pot_ref
  10.4 7.7 %collective-permute-done.2.rim_ref = f32[6,2,32,384]{3,2,1,0:T(8,128)} collective-permute-done((f32[6,2,32,384]{3,2,1,0:T(8,128)}, f32[6,2,32,384]{3,2,1,0:T(8,128)}, u32[]{:S(2)}, u32[]{:S(2)}) %collective-permute-start.2) | collective-permute-done | bytes 589856 | tf_op jit(solution)/shard_map/ppermute | solution.py:198
  18.0 0.0 copy-done.1
  18.1 4.7 %shard_map.38.b_ref = f32[6,2,32,384]{3,2,1,0:T(8,128)} custom-call(s32[1]{0:T(128)} %bitcast.2.side_ref, f32[6,2,32,384]{3,2,1,0:T(8,128)} %collective-permute-done.2.rim_ref, f32[12,2,32,384]{3,2,1,0:T(8,128)} %bitcast.13, f32[12,2,1,384]{3,2,1,0:T(1,128)} %broadcast_in_dim.7.pot_ref), custom_call_target="tpu_custom_call" | custom-call | tf_op jit(solution)/shard_map/pallas_call | solution.py:172
  22.8 4.9 %collective-permute-start.3 = (f32[6,2,32,384]{3,2,1,0:T(8,128)}, f32[6,2,32,384]{3,2,1,0:T(8,128)}, u32[]{:S(2)}, u32[]{:S(2)}) collective-permute-start(f32[6,2,32,384]{3,2,1,0:T(8,128)} %shard_map.38.b_ref), channel_id=1, source_target_pairs={{0,480},{32,64},{64,32},{96,128},{128,96},{160,192},{192,160},{224... | collective-permute-start | bytes 1769480 | tf_op jit(solution)/shard_map/ppermute | solution.py:198
  27.6 0.0 collective-permute-done.rim_ref
  27.7 4.7 %shard_map.37.a_ref = f32[6,2,32,384]{3,2,1,0:T(8,128)} custom-call(s32[1]{0:T(128)} %bitcast.side_ref, f32[6,2,32,384]{3,2,1,0:T(8,128)} %collective-permute-done.rim_ref, f32[12,2,32,384]{3,2,1,0:T(8,128)} %bitcast.14, f32[12,2,1,384]{3,2,1,0:T(1,128)} %broadcast_in_dim.7.pot_ref), custom_call_target="tpu_custom_call" | custom-call | tf_op jit(solution)/shard_map/pallas_call | solution.py:172
  32.4 1.9 %collective-permute-start.1 = (f32[6,2,32,384]{3,2,1,0:T(8,128)}, f32[6,2,32,384]{3,2,1,0:T(8,128)S(1)}, u32[]{:S(2)}, u32[]{:S(2)}) collective-permute-start(f32[6,2,32,384]{3,2,1,0:T(8,128)} %shard_map.37.a_ref), channel_id=1, source_target_pairs={{0,32},{32,0},{64,96},{96,64},{128,160},{160,128},{192,224},{224,1... | collective-permute-start | bytes 1769480 | tf_op jit(solution)/shard_map/ppermute | solution.py:198
  34.3 0.7 pad_add_fusion
  34.9 3.0 %collective-permute-done.3.rim_ref = f32[6,2,32,384]{3,2,1,0:T(8,128)} collective-permute-done((f32[6,2,32,384]{3,2,1,0:T(8,128)}, f32[6,2,32,384]{3,2,1,0:T(8,128)}, u32[]{:S(2)}, u32[]{:S(2)}) %collective-permute-start.3) | collective-permute-done | bytes 589856 | tf_op jit(solution)/shard_map/ppermute | solution.py:198
  37.9 5.1 %shard_map.40 = f32[6,2,32,384]{3,2,1,0:T(8,128)} custom-call(s32[2]{0:T(128)} %get-tuple-element.8.side_ref, f32[6,2,32,384]{3,2,1,0:T(8,128)} %collective-permute-done.3.rim_ref, f32[6,2,32,384]{3,2,1,0:T(8,128)} %shard_map.37.a_ref, f32[6,2,32,384]{3,2,1,0:T(8,128)} %shard_map.38.b_ref, f32[12,2,32,384]{3,2,1,0:T(8,128)} %bitcast.15, ...), custom_call_target="tpu_custom_call" | custom-call | tf_op jit(solution)/shard_map/pallas_call | solution.py:184
  43.0 1.1 convert_element_type.13
  44.1 0.0 collective-permute-done.1.rim_ref
  44.1 0.0 copy-start.2
  44.1 0.8 copy-done.2
  44.9 5.1 %shard_map.39 = f32[6,2,32,384]{3,2,1,0:T(8,128)} custom-call(s32[2]{0:T(128)} %get-tuple-element.7.side_ref, f32[6,2,32,384]{3,2,1,0:T(8,128)} %copy-done.2, f32[6,2,32,384]{3,2,1,0:T(8,128)} %shard_map.37.a_ref, f32[6,2,32,384]{3,2,1,0:T(8,128)} %shard_map.38.b_ref, f32[12,2,32,384]{3,2,1,0:T(8,128)} %bitcast.16, f32[12,2,1,384]{3,2,1,0:T(1,128)} %broadcast_in_dim.7.pot_ref), custom_call_target="tpu_custom_call" | custom-call | tf_op jit(solution)/shard_map/pallas_call | solution.py:184
  50.0 1.1 convert_element_type.12
  51.1 0.3 broadcast_in_dim.6
  51.5 0.3 copy_dynamic-update-slice_fusion.1
  51.8 0.3 copy_dynamic-update-slice_fusion
  52.1 1.1 reshape.23
  53.1 1.1 copy.13
  54.3 2.6 %reshape.24 = bf16[32,24,384]{2,1,0:T(8,128)(2,1)S(1)} reshape(bf16[32,32,288]{2,1,0:T(8,128)(2,1)} %copy.13) | data formatting | bytes 1179648 | tf_op jit(solution)/shard_map/reshape | solution.py:233
  56.9 49.6 %all_to_all.10 = bf16[32,24,384]{2,1,0:T(8,128)(2,1)S(1)} all-to-all(bf16[32,24,384]{2,1,0:T(8,128)(2,1)S(1)} %reshape.24), channel_id=1, replica_groups=mesh['dom'=16,'band'=32] {'band'}, dimensions={0} | all-to-all | bytes 1179648 | tf_op jit(solution)/shard_map/all_to_all | solution.py:233
  106.5 1.1 reshape.25
  107.6 0.0 copy-done
  107.6 0.8 fusion
  108.4 0.4 copy.14
  108.8 1.4 reshape.26
  110.1 39.6 %all_to_all.11 = bf16[32,24,384]{2,1,0:T(8,128)(2,1)} all-to-all(bf16[32,24,384]{2,1,0:T(8,128)(2,1)S(1)} %reshape.26), channel_id=1, replica_groups=mesh['dom'=16,'band'=32] {'band'}, dimensions={0} | all-to-all | bytes 1179648 | tf_op jit(solution)/shard_map/all_to_all | solution.py:240
  149.7 2.2 %reshape.27 = bf16[32,32,288]{2,1,0:T(8,128)(2,1)S(1)} reshape(bf16[32,24,384]{2,1,0:T(8,128)(2,1)} %all_to_all.11) | data formatting | bytes 1179648 | tf_op jit(solution)/shard_map/reshape | solution.py:241
  151.9 1.1 copy.15
  153.1 3.5 %reshape.28 = bf16[32,12,2,384]{3,2,1,0:T(2,128)(2,1)} reshape(bf16[32,32,288]{2,1,0:T(8,128)(2,1)} %copy.15) | data formatting | bytes 1179648 | tf_op jit(solution)/shard_map/reshape | solution.py:242
Async XLA Ops:
  0.0 107.6 %copy-start = (bf16[1024,1024]{1,0:T(8,128)(2,1)S(1)}, bf16[1024,1024]{1,0:T(8,128)(2,1)}, u32[]{:S(2)}) copy-start(bf16[1024,1024]{1,0:T(8,128)(2,1)} %param.5) | copy-start | bytes 6291460
  0.0 9.7 %copy-start.3 = (f32[12,2,384]{2,1,0:T(2,128)S(1)}, f32[12,2,384]{2,1,0:T(2,128)}, u32[]{:S(2)}) copy-start(f32[12,2,384]{2,1,0:T(2,128)} %param.4) | copy-start | bytes 110596
  1.7 16.4 %copy-start.1 = (f32[32,12,2,384]{3,0,2,1:T(8,128)}, f32[32,12,2,384]{3,0,2,1:T(8,128)S(1)}, u32[]{:S(2)}) copy-start(f32[32,12,2,384]{3,0,2,1:T(8,128)S(1)} %copy.19) | copy-start | bytes 3538948
  2.9 15.1 %collective-permute-start.2 = (f32[6,2,32,384]{3,2,1,0:T(8,128)}, f32[6,2,32,384]{3,2,1,0:T(8,128)}, u32[]{:S(2)}, u32[]{:S(2)}) collective-permute-start(f32[6,2,32,384]{3,2,1,0:T(8,128)} %get-tuple-element.5), channel_id=1, source_target_pairs={{0,480},{32,64},{64,32},{96,128},{128,96},{160,192},{192,160},{224... | collective-permute-start | bytes 1769480 | tf_op jit(solution)/shard_map/ppermute | solution.py:198
  7.8 19.9 %collective-permute-start = (f32[6,2,32,384]{3,2,1,0:T(8,128)}, f32[6,2,32,384]{3,2,1,0:T(8,128)}, u32[]{:S(2)}, u32[]{:S(2)}) collective-permute-start(f32[6,2,32,384]{3,2,1,0:T(8,128)} %get-tuple-element.6), channel_id=1, source_target_pairs={{0,32},{32,0},{64,96},{96,64},{128,160},{160,128},{192,224},{224,1... | collective-permute-start | bytes 1769480 | tf_op jit(solution)/shard_map/ppermute | solution.py:198
  22.8 15.1 %collective-permute-start.3 = (f32[6,2,32,384]{3,2,1,0:T(8,128)}, f32[6,2,32,384]{3,2,1,0:T(8,128)}, u32[]{:S(2)}, u32[]{:S(2)}) collective-permute-start(f32[6,2,32,384]{3,2,1,0:T(8,128)} %shard_map.38.b_ref), channel_id=1, source_target_pairs={{0,480},{32,64},{64,32},{96,128},{128,96},{160,192},{192,160},{224... | collective-permute-start | bytes 1769480 | tf_op jit(solution)/shard_map/ppermute | solution.py:198
  32.4 11.7 %collective-permute-start.1 = (f32[6,2,32,384]{3,2,1,0:T(8,128)}, f32[6,2,32,384]{3,2,1,0:T(8,128)S(1)}, u32[]{:S(2)}, u32[]{:S(2)}) collective-permute-start(f32[6,2,32,384]{3,2,1,0:T(8,128)} %shard_map.37.a_ref), channel_id=1, source_target_pairs={{0,32},{32,0},{64,96},{96,64},{128,160},{160,128},{192,224},{224,1... | collective-permute-start | bytes 1769480 | tf_op jit(solution)/shard_map/ppermute | solution.py:198
  44.1 0.8 copy-start.2

commit v11 on v7

--- a/solution.py
+++ b/solution.py
@@ -152,7 +152,8 @@
     def body(x, carry):
         for z in range(depth):
             hv, mid = ham_planes(ext_ref, pot_ref, base + x, z, ny)
-            out_ref[x, z] = 2.0 / half_width * (hv - center_shift * mid) - psi_ref[base + x, z]
+            second = 2.0 / half_width * (hv - center_shift * mid) - psi_ref[base + x, z]
+            out_ref[x, z] = second.astype(out_ref.dtype)
         return carry
 
     lax.fori_loop(0, half, body, 0)
@@ -186,7 +187,7 @@
         grid=(1,),
         in_specs=[smem(), whole(rim.shape), whole(a.shape), whole(b.shape), whole(psi.shape), whole(pot.shape)],
         out_specs=whole(a.shape),
-        out_shape=jax.ShapeDtypeStruct(a.shape, jnp.float32),
+        out_shape=jax.ShapeDtypeStruct(a.shape, jnp.bfloat16),
         scratch_shapes=[pltpu.VMEM((planes + 2 * reach, depth, states, ny), jnp.float32)],
     )(side, rim, a, b, psi, pot)
 

time: 148 us -> 155 us (1.047); the launches traced: 145 us -> 155 us
  blocking collectives: 81.8 us -> 88.8 us
  waiting for transfers between devices: 7.91 us -> 10.7 us
    all_to_all x1, blocking collectives: 45.7 us -> 49.5 us  [per_device(): gathered = lax.all_to_all(blocks.reshape(wire), 'band', 0, 0, tiled=True)]
    all_to_all x1, blocking collectives: 36.1 us -> 39.3 us  [per_device(): back = lax.all_to_all(mixed.reshape(wire), 'band', 0, 0, tiled=True)]
    ppermute x2, waiting for transfers between devices: 7.91 us -> 10.7 us  [inner_outer(): lax.ppermute(send_outer, 'dom', outer)]
    unnamed x13 -> x11, local copies, waits for them, and re-layouts: 3.32 us -> 2.48 us
  transfers between devices with their start and end apart: 4 -> 4, of which waited for: 2 -> 2; matrix products, arithmetic and copies ran while one was open for 1% -> 1% of each run, Pallas kernels for 10% -> 9%
where the time goes in v11:
time: 155 us
  blocking collectives  88.8 us (57%)
  Pallas kernels  19.4 us (13%)
  local copies, waits for them, and re-layouts  18.1 us (12%)
  starting transfers between devices  13.6 us (9%)
  waiting for transfers between devices  10.7 us (7%)
  other arithmetic  3.04 us (2%)
    all_to_all x1, blocking collectives, per_device(): gathered = lax.all_to_all(blocks.reshape(wire), 'band', 0, 0, tiled=True)  49.5 us
    all_to_all x1, blocking collectives, per_device(): back = lax.all_to_all(mixed.reshape(wire), 'band', 0, 0, tiled=True)  39.3 us
    ppermute x2, waiting for transfers between devices, inner_outer(): lax.ppermute(send_outer, 'dom', outer)  10.7 us
    pallas_call x2, Pallas kernels, run_second_half(): pl.pallas_call(second_half_kernel, grid=(1,), in_specs=[smem(), whole(rim...  9.96 us
    ppermute x2, starting transfers between devices, inner_outer(): lax.ppermute(send_outer, 'dom', outer)  9.72 us
    pallas_call x2, Pallas kernels, run_first_half(): pl.pallas_call(first_half_kernel, grid=(1,), in_specs=[smem(), whole(rim....  9.43 us
    ppermute x2, starting transfers between devices, inner_outer(): lax.ppermute(send_inner, 'dom', inner)  3.83 us
    reshape x1, local copies, waits for them, and re-layouts, per_device(): return result.reshape(psi.shape)  3.52 us
  transfers between devices with their start and end apart: 4, of which 2 were waited for; matrix products, arithmetic and copies ran while one was open for 1% of the time, Pallas kernels for 9%

profile of v11, /device:TPU:25, one launch (start us, length us, event | category | flops | bytes accessed | tf_op | source)
XLA Modules:
  0.0 154.5 jit_solution(15704363078520929833)
XLA Ops:
  0.0 0.0 copy-start
  0.0 0.0 copy-start.4
  0.0 1.7 %copy.15 = f32[32,12,2,384]{3,0,2,1:T(8,128)S(1)} copy(f32[32,12,2,384]{3,2,1,0:T(2,128)} %param.3) | data formatting | bytes 2359296 | tf_op args[0]
  1.7 0.0 copy-start.1
  1.7 1.3 slice_select_fusion.1
  2.9 4.9 %collective-permute-start = (f32[6,2,32,384]{3,2,1,0:T(8,128)}, f32[6,2,32,384]{3,2,1,0:T(8,128)}, u32[]{:S(2)}, u32[]{:S(2)}) collective-permute-start(f32[6,2,32,384]{3,2,1,0:T(8,128)} %get-tuple-element.5), channel_id=1, source_target_pairs={{0,480},{32,64},{64,32},{96,128},{128,96},{160,192},{192,160},{224... | collective-permute-start | bytes 1769480 | tf_op jit(solution)/shard_map/ppermute | solution.py:199
  7.8 1.9 %collective-permute-start.2 = (f32[6,2,32,384]{3,2,1,0:T(8,128)}, f32[6,2,32,384]{3,2,1,0:T(8,128)}, u32[]{:S(2)}, u32[]{:S(2)}) collective-permute-start(f32[6,2,32,384]{3,2,1,0:T(8,128)} %get-tuple-element.6), channel_id=1, source_target_pairs={{0,32},{32,0},{64,96},{96,64},{128,160},{160,128},{192,224},{224,1... | collective-permute-start | bytes 1769480 | tf_op jit(solution)/shard_map/ppermute | solution.py:199
  9.7 0.0 copy-done.4
  9.7 0.6 broadcast_in_dim.3.pot_ref
  10.4 7.7 %collective-permute-done.rim_ref = f32[6,2,32,384]{3,2,1,0:T(8,128)} collective-permute-done((f32[6,2,32,384]{3,2,1,0:T(8,128)}, f32[6,2,32,384]{3,2,1,0:T(8,128)}, u32[]{:S(2)}, u32[]{:S(2)}) %collective-permute-start) | collective-permute-done | bytes 589856 | tf_op jit(solution)/shard_map/ppermute | solution.py:199
  18.1 0.0 copy-done.1
  18.1 4.7 %shard_map.37.b_ref = f32[6,2,32,384]{3,2,1,0:T(8,128)} custom-call(s32[1]{0:T(128)} %bitcast.side_ref, f32[6,2,32,384]{3,2,1,0:T(8,128)} %collective-permute-done.rim_ref, f32[12,2,32,384]{3,2,1,0:T(8,128)} %bitcast.14, f32[12,2,1,384]{3,2,1,0:T(1,128)} %broadcast_in_dim.3.pot_ref), custom_call_target="tpu_custom_call" | custom-call | tf_op jit(solution)/shard_map/pallas_call | solution.py:173
  22.8 4.9 %collective-permute-start.1 = (f32[6,2,32,384]{3,2,1,0:T(8,128)}, f32[6,2,32,384]{3,2,1,0:T(8,128)}, u32[]{:S(2)}, u32[]{:S(2)}) collective-permute-start(f32[6,2,32,384]{3,2,1,0:T(8,128)} %shard_map.37.b_ref), channel_id=1, source_target_pairs={{0,480},{32,64},{64,32},{96,128},{128,96},{160,192},{192,160},{224... | collective-permute-start | bytes 1769480 | tf_op jit(solution)/shard_map/ppermute | solution.py:199
  27.6 0.0 collective-permute-done.2.rim_ref
  27.7 4.7 %shard_map.38.a_ref = f32[6,2,32,384]{3,2,1,0:T(8,128)} custom-call(s32[1]{0:T(128)} %bitcast.1.side_ref, f32[6,2,32,384]{3,2,1,0:T(8,128)} %collective-permute-done.2.rim_ref, f32[12,2,32,384]{3,2,1,0:T(8,128)} %bitcast.15, f32[12,2,1,384]{3,2,1,0:T(1,128)} %broadcast_in_dim.3.pot_ref), custom_call_target="tpu_custom_call" | custom-call | tf_op jit(solution)/shard_map/pallas_call | solution.py:173
  32.4 1.9 %collective-permute-start.3 = (f32[6,2,32,384]{3,2,1,0:T(8,128)}, f32[6,2,32,384]{3,2,1,0:T(8,128)S(1)}, u32[]{:S(2)}, u32[]{:S(2)}) collective-permute-start(f32[6,2,32,384]{3,2,1,0:T(8,128)} %shard_map.38.a_ref), channel_id=1, source_target_pairs={{0,32},{32,0},{64,96},{96,64},{128,160},{160,128},{192,224},{224,1... | collective-permute-start | bytes 1769480 | tf_op jit(solution)/shard_map/ppermute | solution.py:199
  34.3 0.6 pad_add_fusion
  34.9 3.0 %collective-permute-done.1.rim_ref = f32[6,2,32,384]{3,2,1,0:T(8,128)} collective-permute-done((f32[6,2,32,384]{3,2,1,0:T(8,128)}, f32[6,2,32,384]{3,2,1,0:T(8,128)}, u32[]{:S(2)}, u32[]{:S(2)}) %collective-permute-start.1) | collective-permute-done | bytes 589856 | tf_op jit(solution)/shard_map/ppermute | solution.py:199
  37.9 5.0 %shard_map.39 = bf16[6,2,32,384]{3,2,1,0:T(8,128)(2,1)} custom-call(s32[2]{0:T(128)} %get-tuple-element.7.side_ref, f32[6,2,32,384]{3,2,1,0:T(8,128)} %collective-permute-done.1.rim_ref, f32[6,2,32,384]{3,2,1,0:T(8,128)} %shard_map.38.a_ref, f32[6,2,32,384]{3,2,1,0:T(8,128)} %shard_map.37.b_ref, f32[12,2,32,384]{3,2,1,0:T(8,128)} %bitcast.16, ...), custom_call_target="tpu_custom_call" | custom-call | tf_op jit(solution)/shard_map/pallas_call | solution.py:185
  42.9 0.0 copy-start.2
  42.9 0.0 collective-permute-done.3.rim_ref
  42.9 0.0 copy-start.3
  42.9 0.8 copy-done.3
  43.7 5.0 %shard_map.40 = bf16[6,2,32,384]{3,2,1,0:T(8,128)(2,1)} custom-call(s32[2]{0:T(128)} %get-tuple-element.8.side_ref, f32[6,2,32,384]{3,2,1,0:T(8,128)} %copy-done.3, f32[6,2,32,384]{3,2,1,0:T(8,128)} %shard_map.38.a_ref, f32[6,2,32,384]{3,2,1,0:T(8,128)} %shard_map.37.b_ref, f32[12,2,32,384]{3,2,1,0:T(8,128)} %bitcast.17, ...), custom_call_target="tpu_custom_call" | custom-call | tf_op jit(solution)/shard_map/pallas_call | solution.py:185
  48.7 0.0 copy-done.2
  48.7 1.2 fusion.1
  49.9 0.5 copy.10
  50.3 1.1 reshape.20
  51.4 1.1 copy.11
  52.6 2.6 %reshape.21 = bf16[32,24,384]{2,1,0:T(8,128)(2,1)S(1)} reshape(bf16[32,32,288]{2,1,0:T(8,128)(2,1)} %copy.11) | data formatting | bytes 1179648 | tf_op jit(solution)/shard_map/reshape | solution.py:234
  55.1 49.5 %all_to_all.10 = bf16[32,24,384]{2,1,0:T(8,128)(2,1)S(1)} all-to-all(bf16[32,24,384]{2,1,0:T(8,128)(2,1)S(1)} %reshape.21), channel_id=1, replica_groups=mesh['dom'=16,'band'=32] {'band'}, dimensions={0} | all-to-all | bytes 1179648 | tf_op jit(solution)/shard_map/all_to_all | solution.py:234
  104.7 1.1 reshape.22
  105.8 0.0 copy-done
  105.8 0.8 fusion
  106.6 0.4 copy.12
  106.9 1.4 reshape.23
  108.3 39.3 %all_to_all.11 = bf16[32,24,384]{2,1,0:T(8,128)(2,1)} all-to-all(bf16[32,24,384]{2,1,0:T(8,128)(2,1)S(1)} %reshape.23), channel_id=1, replica_groups=mesh['dom'=16,'band'=32] {'band'}, dimensions={0} | all-to-all | bytes 1179648 | tf_op jit(solution)/shard_map/all_to_all | solution.py:241
  147.6 2.2 %reshape.24 = bf16[32,32,288]{2,1,0:T(8,128)(2,1)S(1)} reshape(bf16[32,24,384]{2,1,0:T(8,128)(2,1)} %all_to_all.11) | data formatting | bytes 1179648 | tf_op jit(solution)/shard_map/reshape | solution.py:242
  149.9 1.1 copy.13
  151.0 3.5 %reshape.25 = bf16[32,12,2,384]{3,2,1,0:T(2,128)(2,1)} reshape(bf16[32,32,288]{2,1,0:T(8,128)(2,1)} %copy.13) | data formatting | bytes 1179648 | tf_op jit(solution)/shard_map/reshape | solution.py:243
Async XLA Ops:
  0.0 105.8 %copy-start = (bf16[1024,1024]{1,0:T(8,128)(2,1)S(1)}, bf16[1024,1024]{1,0:T(8,128)(2,1)}, u32[]{:S(2)}) copy-start(bf16[1024,1024]{1,0:T(8,128)(2,1)} %param.5) | copy-start | bytes 6291460
  0.0 9.7 %copy-start.4 = (f32[12,2,384]{2,1,0:T(2,128)S(1)}, f32[12,2,384]{2,1,0:T(2,128)}, u32[]{:S(2)}) copy-start(f32[12,2,384]{2,1,0:T(2,128)} %param.4) | copy-start | bytes 110596
  1.7 16.4 %copy-start.1 = (f32[32,12,2,384]{3,0,2,1:T(8,128)}, f32[32,12,2,384]{3,0,2,1:T(8,128)S(1)}, u32[]{:S(2)}) copy-start(f32[32,12,2,384]{3,0,2,1:T(8,128)S(1)} %copy.15) | copy-start | bytes 3538948
  2.9 15.1 %collective-permute-start = (f32[6,2,32,384]{3,2,1,0:T(8,128)}, f32[6,2,32,384]{3,2,1,0:T(8,128)}, u32[]{:S(2)}, u32[]{:S(2)}) collective-permute-start(f32[6,2,32,384]{3,2,1,0:T(8,128)} %get-tuple-element.5), channel_id=1, source_target_pairs={{0,480},{32,64},{64,32},{96,128},{128,96},{160,192},{192,160},{224... | collective-permute-start | bytes 1769480 | tf_op jit(solution)/shard_map/ppermute | solution.py:199
  7.8 19.8 %collective-permute-start.2 = (f32[6,2,32,384]{3,2,1,0:T(8,128)}, f32[6,2,32,384]{3,2,1,0:T(8,128)}, u32[]{:S(2)}, u32[]{:S(2)}) collective-permute-start(f32[6,2,32,384]{3,2,1,0:T(8,128)} %get-tuple-element.6), channel_id=1, source_target_pairs={{0,32},{32,0},{64,96},{96,64},{128,160},{160,128},{192,224},{224,1... | collective-permute-start | bytes 1769480 | tf_op jit(solution)/shard_map/ppermute | solution.py:199
  22.8 15.1 %collective-permute-start.1 = (f32[6,2,32,384]{3,2,1,0:T(8,128)}, f32[6,2,32,384]{3,2,1,0:T(8,128)}, u32[]{:S(2)}, u32[]{:S(2)}) collective-permute-start(f32[6,2,32,384]{3,2,1,0:T(8,128)} %shard_map.37.b_ref), channel_id=1, source_target_pairs={{0,480},{32,64},{64,32},{96,128},{128,96},{160,192},{192,160},{224... | collective-permute-start | bytes 1769480 | tf_op jit(solution)/shard_map/ppermute | solution.py:199
  32.4 10.5 %collective-permute-start.3 = (f32[6,2,32,384]{3,2,1,0:T(8,128)}, f32[6,2,32,384]{3,2,1,0:T(8,128)S(1)}, u32[]{:S(2)}, u32[]{:S(2)}) collective-permute-start(f32[6,2,32,384]{3,2,1,0:T(8,128)} %shard_map.38.a_ref), channel_id=1, source_target_pairs={{0,32},{32,0},{64,96},{96,64},{128,160},{160,128},{192,224},{224,1... | collective-permute-start | bytes 1769480 | tf_op jit(solution)/shard_map/ppermute | solution.py:199
  42.9 5.8 %copy-start.2 = (bf16[6,2,32,384]{3,2,1,0:T(8,128)(2,1)S(1)}, bf16[6,2,32,384]{3,2,1,0:T(8,128)(2,1)}, u32[]{:S(2)}) copy-start(bf16[6,2,32,384]{3,2,1,0:T(8,128)(2,1)} %shard_map.39) | copy-start | bytes 884740
  42.9 0.8 copy-start.3

commit v12 on v7

--- a/solution.py
+++ b/solution.py
@@ -198,15 +198,27 @@
     return lax.ppermute(send_inner, "dom", inner), lax.ppermute(send_outer, "dom", outer)
 
 
+def to_wire(second, parts):
+    planes, depth, states, ny = second.shape
+    chunk = planes * depth * ny // parts
+    flat = second.astype(jnp.bfloat16).transpose(2, 0, 1, 3).reshape(states, parts, chunk)
+    return flat.transpose(1, 0, 2).reshape(parts, states * chunk // ny, ny)
+
+
 def per_device(psi, potential, rotation):
     own_states, planes, depth, ny = psi.shape
     psi_t = psi.transpose(1, 2, 0, 3)
     pot_t = potential[:, :, None, :]
-    if lax.axis_size("dom") % 2 or planes != 2 * reach:
+    rows = planes * depth
+    count = lax.axis_size("band")
+    chunk = rows * ny // count
+    wire = (count, own_states * chunk // ny, ny)
+    if lax.axis_size("dom") % 2 or planes != 2 * reach or count % 2:
         left, right = swap_rims(psi_t[:reach], psi_t[planes - reach :])
         first, head, tail = run_first(left, psi_t, right, pot_t)
         left, right = swap_rims(head, tail)
         second = run_second(left, first, right, psi_t, pot_t)
+        blocks = to_wire(second, count)
     else:
         even = lax.axis_index("dom") % 2 == 0
         hi = jnp.where(even, 1, 0).astype(jnp.int32)
@@ -219,18 +231,14 @@
         sides_b = jnp.stack([1 - hi, hi])
         second_a = run_second_half(sides_a, rim_in, part_a, part_b, psi_t, pot_t)
         second_b = run_second_half(sides_b, rim_out, part_a, part_b, psi_t, pot_t)
-        second = jnp.where(
+        wire_a = to_wire(second_a, count // 2)
+        wire_b = to_wire(second_b, count // 2)
+        blocks = jnp.where(
             even,
-            jnp.concatenate([second_b, second_a], axis=0),
-            jnp.concatenate([second_a, second_b], axis=0),
+            jnp.concatenate([wire_b, wire_a], axis=0),
+            jnp.concatenate([wire_a, wire_b], axis=0),
         )
-    filtered = second.astype(jnp.bfloat16).transpose(2, 0, 1, 3)
-    rows = planes * depth
-    count = lax.axis_size("band")
-    chunk = rows * ny // count
-    blocks = filtered.reshape(own_states, count, chunk).transpose(1, 0, 2)
-    wire = (count, own_states * chunk // ny, ny)
-    gathered = lax.all_to_all(blocks.reshape(wire), "band", 0, 0, tiled=True)
+    gathered = lax.all_to_all(blocks, "band", 0, 0, tiled=True)
     mixed = lax.dot_general(
         rotation,
         gathered.reshape(own_states * count, chunk),

time: 148 us -> 155 us (1.047); the launches traced: 145 us -> 155 us
  blocking collectives: 81.8 us -> 89.9 us
  local copies, waits for them, and re-layouts: 18.9 us -> 15.9 us
  waiting for transfers between devices: 7.91 us -> 10.5 us
    all_to_all x1, blocking collectives: 36.1 us -> 40.2 us  [per_device(): back = lax.all_to_all(mixed.reshape(wire), 'band', 0, 0, tiled=True)]
    all_to_all x1, blocking collectives: 45.7 us -> 49.7 us  [per_device(): gathered = lax.all_to_all(blocks, 'band', 0, 0, tiled=True)]
    ppermute x2, waiting for transfers between devices: 7.91 us -> 10.5 us  [inner_outer(): lax.ppermute(send_outer, 'dom', outer)]
    reshape x2 -> x4, local copies, waits for them, and re-layouts: 3.65 us -> 2.43 us  [the longest x2 1.38 us: to_wire(): return flat.transpose(1, 0, 2).reshape(parts, states * chunk // ny, ny)]
    unnamed x13 -> x9, local copies, waits for them, and re-layouts: 3.32 us -> 2.5 us
  transfers between devices with their start and end apart: 4 -> 4, of which waited for: 2 -> 2; matrix products, arithmetic and copies ran while one was open for 1% -> 3% of each run, Pallas kernels for 10% -> 9%
where the time goes in v12:
time: 155 us
  blocking collectives  89.9 us (58%)
  Pallas kernels  19.6 us (13%)
  local copies, waits for them, and re-layouts  15.9 us (10%)
  starting transfers between devices  13.6 us (9%)
  waiting for transfers between devices  10.5 us (7%)
  other arithmetic  4.23 us (3%)
    all_to_all x1, blocking collectives, per_device(): gathered = lax.all_to_all(blocks, 'band', 0, 0, tiled=True)  49.7 us
    all_to_all x1, blocking collectives, per_device(): back = lax.all_to_all(mixed.reshape(wire), 'band', 0, 0, tiled=True)  40.2 us
    ppermute x2, waiting for transfers between devices, inner_outer(): lax.ppermute(send_outer, 'dom', outer)  10.5 us
    pallas_call x2, Pallas kernels, run_second_half(): pl.pallas_call(second_half_kernel, grid=(1,), in_specs=[smem(), whole(rim...  10.2 us
    ppermute x2, starting transfers between devices, inner_outer(): lax.ppermute(send_outer, 'dom', outer)  9.72 us
    pallas_call x2, Pallas kernels, run_first_half(): pl.pallas_call(first_half_kernel, grid=(1,), in_specs=[smem(), whole(rim....  9.43 us
    ppermute x2, starting transfers between devices, inner_outer(): lax.ppermute(send_inner, 'dom', inner)  3.83 us
    reshape x1, local copies, waits for them, and re-layouts, per_device(): return result.reshape(psi.shape)  3.52 us
  transfers between devices with their start and end apart: 4, of which 2 were waited for; matrix products, arithmetic and copies ran while one was open for 3% of the time, Pallas kernels for 9%

profile of v12, /device:TPU:25, one launch (start us, length us, event | category | flops | bytes accessed | tf_op | source)
XLA Modules:
  0.0 154.8 jit_solution(2654329621790304430)
XLA Ops:
  0.0 0.0 copy-start
  0.0 0.0 copy-start.3
  0.0 1.7 %copy.17 = f32[32,12,2,384]{3,0,2,1:T(8,128)S(1)} copy(f32[32,12,2,384]{3,2,1,0:T(2,128)} %param.3) | data formatting | bytes 2359296 | tf_op args[0]
  1.7 0.0 copy-start.1
  1.7 1.3 slice_select_fusion.1
  2.9 4.9 %collective-permute-start = (f32[6,2,32,384]{3,2,1,0:T(8,128)}, f32[6,2,32,384]{3,2,1,0:T(8,128)}, u32[]{:S(2)}, u32[]{:S(2)}) collective-permute-start(f32[6,2,32,384]{3,2,1,0:T(8,128)} %get-tuple-element.5), channel_id=1, source_target_pairs={{0,480},{32,64},{64,32},{96,128},{128,96},{160,192},{192,160},{224... | collective-permute-start | bytes 1769480 | tf_op jit(solution)/shard_map/ppermute | solution.py:198
  7.8 1.9 %collective-permute-start.2 = (f32[6,2,32,384]{3,2,1,0:T(8,128)}, f32[6,2,32,384]{3,2,1,0:T(8,128)}, u32[]{:S(2)}, u32[]{:S(2)}) collective-permute-start(f32[6,2,32,384]{3,2,1,0:T(8,128)} %get-tuple-element.6), channel_id=1, source_target_pairs={{0,32},{32,0},{64,96},{96,64},{128,160},{160,128},{192,224},{224,1... | collective-permute-start | bytes 1769480 | tf_op jit(solution)/shard_map/ppermute | solution.py:198
  9.7 0.0 copy-done.3
  9.7 0.6 broadcast_in_dim.3.pot_ref
  10.4 7.7 %collective-permute-done.rim_ref = f32[6,2,32,384]{3,2,1,0:T(8,128)} collective-permute-done((f32[6,2,32,384]{3,2,1,0:T(8,128)}, f32[6,2,32,384]{3,2,1,0:T(8,128)}, u32[]{:S(2)}, u32[]{:S(2)}) %collective-permute-start) | collective-permute-done | bytes 589856 | tf_op jit(solution)/shard_map/ppermute | solution.py:198
  18.0 0.0 copy-done.1
  18.1 4.7 %shard_map.37.b_ref = f32[6,2,32,384]{3,2,1,0:T(8,128)} custom-call(s32[1]{0:T(128)} %bitcast.side_ref, f32[6,2,32,384]{3,2,1,0:T(8,128)} %collective-permute-done.rim_ref, f32[12,2,32,384]{3,2,1,0:T(8,128)} %bitcast.17, f32[12,2,1,384]{3,2,1,0:T(1,128)} %broadcast_in_dim.3.pot_ref), custom_call_target="tpu_custom_call" | custom-call | tf_op jit(solution)/shard_map/pallas_call | solution.py:172
  22.8 4.9 %collective-permute-start.1 = (f32[6,2,32,384]{3,2,1,0:T(8,128)}, f32[6,2,32,384]{3,2,1,0:T(8,128)S(1)}, u32[]{:S(2)}, u32[]{:S(2)}) collective-permute-start(f32[6,2,32,384]{3,2,1,0:T(8,128)} %shard_map.37.b_ref), channel_id=1, source_target_pairs={{0,480},{32,64},{64,32},{96,128},{128,96},{160,192},{192,160},{224... | collective-permute-start | bytes 1769480 | tf_op jit(solution)/shard_map/ppermute | solution.py:198
  27.6 0.0 collective-permute-done.2.rim_ref
  27.7 4.7 %shard_map.38.a_ref = f32[6,2,32,384]{3,2,1,0:T(8,128)} custom-call(s32[1]{0:T(128)} %bitcast.1.side_ref, f32[6,2,32,384]{3,2,1,0:T(8,128)} %collective-permute-done.2.rim_ref, f32[12,2,32,384]{3,2,1,0:T(8,128)} %bitcast.18, f32[12,2,1,384]{3,2,1,0:T(1,128)} %broadcast_in_dim.3.pot_ref), custom_call_target="tpu_custom_call" | custom-call | tf_op jit(solution)/shard_map/pallas_call | solution.py:172
  32.4 1.9 %collective-permute-start.3 = (f32[6,2,32,384]{3,2,1,0:T(8,128)}, f32[6,2,32,384]{3,2,1,0:T(8,128)}, u32[]{:S(2)}, u32[]{:S(2)}) collective-permute-start(f32[6,2,32,384]{3,2,1,0:T(8,128)} %shard_map.38.a_ref), channel_id=1, source_target_pairs={{0,32},{32,0},{64,96},{96,64},{128,160},{160,128},{192,224},{224,1... | collective-permute-start | bytes 1769480 | tf_op jit(solution)/shard_map/ppermute | solution.py:198
  34.3 0.7 pad_add_fusion
  35.0 2.8 %collective-permute-done.1.rim_ref = f32[6,2,32,384]{3,2,1,0:T(8,128)S(1)} collective-permute-done((f32[6,2,32,384]{3,2,1,0:T(8,128)}, f32[6,2,32,384]{3,2,1,0:T(8,128)S(1)}, u32[]{:S(2)}, u32[]{:S(2)}) %collective-permute-start.1) | collective-permute-done | bytes 589856 | tf_op jit(solution)/shard_map/ppermute | solution.py:198
  37.8 0.0 copy-start.2
  37.8 0.8 copy-done.2
  38.6 5.1 %shard_map.39 = f32[6,2,32,384]{3,2,1,0:T(8,128)} custom-call(s32[2]{0:T(128)} %get-tuple-element.7.side_ref, f32[6,2,32,384]{3,2,1,0:T(8,128)} %copy-done.2, f32[6,2,32,384]{3,2,1,0:T(8,128)} %shard_map.38.a_ref, f32[6,2,32,384]{3,2,1,0:T(8,128)} %shard_map.37.b_ref, f32[12,2,32,384]{3,2,1,0:T(8,128)} %bitcast.19, f32[12,2,1,384]{3,2,1,0:T(1,128)} %broadcast_in_dim.3.pot_ref), custom_call_target="tpu_custom_call" | custom-call | tf_op jit(solution)/shard_map/pallas_call | solution.py:184
  43.7 1.1 convert_bitcast_fusion.1
  44.8 0.2 copy.10
  45.1 0.5 reshape.26
  45.6 0.1 copy.11
  45.7 0.7 reshape.27
  46.4 0.0 collective-permute-done.3.rim_ref
  46.4 5.1 %shard_map.40 = f32[6,2,32,384]{3,2,1,0:T(8,128)} custom-call(s32[2]{0:T(128)} %get-tuple-element.8.side_ref, f32[6,2,32,384]{3,2,1,0:T(8,128)} %collective-permute-done.3.rim_ref, f32[6,2,32,384]{3,2,1,0:T(8,128)} %shard_map.38.a_ref, f32[6,2,32,384]{3,2,1,0:T(8,128)} %shard_map.37.b_ref, f32[12,2,32,384]{3,2,1,0:T(8,128)} %bitcast.20, ...), custom_call_target="tpu_custom_call" | custom-call | tf_op jit(solution)/shard_map/pallas_call | solution.py:184
  51.5 1.1 convert_bitcast_fusion
  52.6 0.2 copy.12
  52.8 0.5 reshape.28
  53.4 0.1 copy.13
  53.5 0.7 reshape.29
  54.1 0.1 maximum_select_fusion
  54.3 49.7 %all_to_all.10 = bf16[32,24,384]{2,1,0:T(8,128)(2,1)S(1)} all-to-all(bf16[32,24,384]{2,1,0:T(8,128)(2,1)S(1)} %maximum_select_fusion), channel_id=1, replica_groups=mesh['dom'=16,'band'=32] {'band'}, dimensions={0} | all-to-all | bytes 1179648 | tf_op jit(solution)/shard_map/all_to_all | solution.py:241
  104.0 1.1 reshape.30
  105.1 0.0 copy-done
  105.1 0.8 fusion
  105.9 0.4 copy.14
  106.3 1.4 reshape.31
  107.6 40.2 %all_to_all.11 = bf16[32,24,384]{2,1,0:T(8,128)(2,1)} all-to-all(bf16[32,24,384]{2,1,0:T(8,128)(2,1)S(1)} %reshape.31), channel_id=1, replica_groups=mesh['dom'=16,'band'=32] {'band'}, dimensions={0} | all-to-all | bytes 1179648 | tf_op jit(solution)/shard_map/all_to_all | solution.py:248
  147.9 2.2 %reshape.32 = bf16[32,32,288]{2,1,0:T(8,128)(2,1)S(1)} reshape(bf16[32,24,384]{2,1,0:T(8,128)(2,1)} %all_to_all.11) | data formatting | bytes 1179648 | tf_op jit(solution)/shard_map/reshape | solution.py:249
  150.1 1.1 copy.15
  151.2 3.5 %reshape.33 = bf16[32,12,2,384]{3,2,1,0:T(2,128)(2,1)} reshape(bf16[32,32,288]{2,1,0:T(8,128)(2,1)} %copy.15) | data formatting | bytes 1179648 | tf_op jit(solution)/shard_map/reshape | solution.py:250
Async XLA Ops:
  0.0 105.1 %copy-start = (bf16[1024,1024]{1,0:T(8,128)(2,1)S(1)}, bf16[1024,1024]{1,0:T(8,128)(2,1)}, u32[]{:S(2)}) copy-start(bf16[1024,1024]{1,0:T(8,128)(2,1)} %param.5) | copy-start | bytes 6291460
  0.0 9.7 %copy-start.3 = (f32[12,2,384]{2,1,0:T(2,128)S(1)}, f32[12,2,384]{2,1,0:T(2,128)}, u32[]{:S(2)}) copy-start(f32[12,2,384]{2,1,0:T(2,128)} %param.4) | copy-start | bytes 110596
  1.7 16.4 %copy-start.1 = (f32[32,12,2,384]{3,0,2,1:T(8,128)}, f32[32,12,2,384]{3,0,2,1:T(8,128)S(1)}, u32[]{:S(2)}) copy-start(f32[32,12,2,384]{3,0,2,1:T(8,128)S(1)} %copy.17) | copy-start | bytes 3538948
  2.9 15.1 %collective-permute-start = (f32[6,2,32,384]{3,2,1,0:T(8,128)}, f32[6,2,32,384]{3,2,1,0:T(8,128)}, u32[]{:S(2)}, u32[]{:S(2)}) collective-permute-start(f32[6,2,32,384]{3,2,1,0:T(8,128)} %get-tuple-element.5), channel_id=1, source_target_pairs={{0,480},{32,64},{64,32},{96,128},{128,96},{160,192},{192,160},{224... | collective-permute-start | bytes 1769480 | tf_op jit(solution)/shard_map/ppermute | solution.py:198
  7.8 19.9 %collective-permute-start.2 = (f32[6,2,32,384]{3,2,1,0:T(8,128)}, f32[6,2,32,384]{3,2,1,0:T(8,128)}, u32[]{:S(2)}, u32[]{:S(2)}) collective-permute-start(f32[6,2,32,384]{3,2,1,0:T(8,128)} %get-tuple-element.6), channel_id=1, source_target_pairs={{0,32},{32,0},{64,96},{96,64},{128,160},{160,128},{192,224},{224,1... | collective-permute-start | bytes 1769480 | tf_op jit(solution)/shard_map/ppermute | solution.py:198
  22.8 15.0 %collective-permute-start.1 = (f32[6,2,32,384]{3,2,1,0:T(8,128)}, f32[6,2,32,384]{3,2,1,0:T(8,128)S(1)}, u32[]{:S(2)}, u32[]{:S(2)}) collective-permute-start(f32[6,2,32,384]{3,2,1,0:T(8,128)} %shard_map.37.b_ref), channel_id=1, source_target_pairs={{0,480},{32,64},{64,32},{96,128},{128,96},{160,192},{192,160},{224... | collective-permute-start | bytes 1769480 | tf_op jit(solution)/shard_map/ppermute | solution.py:198
  32.4 14.0 %collective-permute-start.3 = (f32[6,2,32,384]{3,2,1,0:T(8,128)}, f32[6,2,32,384]{3,2,1,0:T(8,128)}, u32[]{:S(2)}, u32[]{:S(2)}) collective-permute-start(f32[6,2,32,384]{3,2,1,0:T(8,128)} %shard_map.38.a_ref), channel_id=1, source_target_pairs={{0,32},{32,0},{64,96},{96,64},{128,160},{160,128},{192,224},{224,1... | collective-permute-start | bytes 1769480 | tf_op jit(solution)/shard_map/ppermute | solution.py:198
  37.8 0.8 copy-start.2

commit v13 on v12

--- a/solution.py
+++ b/solution.py
@@ -225,11 +225,13 @@
         head, tail = psi_t[:reach], psi_t[planes - reach :]
         rim_in, rim_out = inner_outer(jnp.where(even, tail, head), jnp.where(even, head, tail))
         part_a = run_first_half(hi.reshape(1), rim_in, psi_t, pot_t)
+        _, rim_out = lax.optimization_barrier((part_a, rim_out))
         part_b = run_first_half((1 - hi).reshape(1), rim_out, psi_t, pot_t)
         rim_in, rim_out = inner_outer(part_a, part_b)
         sides_a = jnp.stack([hi, hi])
         sides_b = jnp.stack([1 - hi, hi])
         second_a = run_second_half(sides_a, rim_in, part_a, part_b, psi_t, pot_t)
+        _, rim_out = lax.optimization_barrier((second_a, rim_out))
         second_b = run_second_half(sides_b, rim_out, part_a, part_b, psi_t, pot_t)
         wire_a = to_wire(second_a, count // 2)
         wire_b = to_wire(second_b, count // 2)

time: 155 us -> 145 us (0.935); the launches traced: 155 us -> 142 us
  blocking collectives: 89.9 us -> 83.2 us
  waiting for transfers between devices: 10.5 us -> 5.3 us
    ppermute x2, waiting for transfers between devices: 10.5 us -> 5.29 us  [inner_outer(): lax.ppermute(send_outer, 'dom', outer)]
    all_to_all x1, blocking collectives: 49.7 us -> 46.2 us  [per_device(): gathered = lax.all_to_all(blocks, 'band', 0, 0, tiled=True)]
    all_to_all x1, blocking collectives: 40.2 us -> 36.9 us  [per_device(): back = lax.all_to_all(mixed.reshape(wire), 'band', 0, 0, tiled=True)]
  transfers between devices with their start and end apart: 4 -> 4, of which waited for: 2 -> 2; matrix products, arithmetic and copies ran while one was open for 3% -> 3% of each run, Pallas kernels for 9% -> 10%
where the time goes in v13:
time: 145 us; the launch traced here: 142 us
  blocking collectives  83.2 us (57%)
  Pallas kernels  19.6 us (14%)
  local copies, waits for them, and re-layouts  15.9 us (11%)
  starting transfers between devices  12.9 us (9%)
  waiting for transfers between devices  5.3 us (4%)
  other arithmetic  4.27 us (3%)
    all_to_all x1, blocking collectives, per_device(): gathered = lax.all_to_all(blocks, 'band', 0, 0, tiled=True)  46.2 us
    all_to_all x1, blocking collectives, per_device(): back = lax.all_to_all(mixed.reshape(wire), 'band', 0, 0, tiled=True)  36.9 us
    pallas_call x2, Pallas kernels, run_second_half(): pl.pallas_call(second_half_kernel, grid=(1,), in_specs=[smem(), whole(rim...  10.2 us
    pallas_call x2, Pallas kernels, run_first_half(): pl.pallas_call(first_half_kernel, grid=(1,), in_specs=[smem(), whole(rim....  9.43 us
    ppermute x2, starting transfers between devices, inner_outer(): lax.ppermute(send_outer, 'dom', outer)  8.41 us
    ppermute x2, waiting for transfers between devices, inner_outer(): lax.ppermute(send_outer, 'dom', outer)  5.29 us
    ppermute x2, starting transfers between devices, inner_outer(): lax.ppermute(send_inner, 'dom', inner)  4.48 us
    reshape x1, local copies, waits for them, and re-layouts, per_device(): return result.reshape(psi.shape)  3.52 us
  transfers between devices with their start and end apart: 4, of which 2 were waited for; matrix products, arithmetic and copies ran while one was open for 3% of the time, Pallas kernels for 10%

profile of v13, /device:TPU:25, one launch (start us, length us, event | category | flops | bytes accessed | tf_op | source)
XLA Modules:
  0.0 142.1 jit_solution(7087620886389399559)
XLA Ops:
  0.0 0.0 copy-start
  0.0 0.0 copy-start.3
  0.0 1.7 %copy.17 = f32[32,12,2,384]{3,0,2,1:T(8,128)S(1)} copy(f32[32,12,2,384]{3,2,1,0:T(2,128)} %param.3) | data formatting | bytes 2359296 | tf_op args[0]
  1.7 0.0 copy-start.1
  1.7 1.3 slice_select_fusion
  3.0 2.6 %collective-permute-start = (f32[6,2,32,384]{3,2,1,0:T(8,128)}, f32[6,2,32,384]{3,2,1,0:T(8,128)}, u32[]{:S(2)}, u32[]{:S(2)}) collective-permute-start(f32[6,2,32,384]{3,2,1,0:T(8,128)} %get-tuple-element.10), channel_id=1, source_target_pairs={{0,32},{32,0},{64,96},{96,64},{128,160},{160,128},{192,224},{224,1... | collective-permute-start | bytes 1769480 | tf_op jit(solution)/shard_map/ppermute | solution.py:198
  5.5 4.2 %collective-permute-start.2 = (f32[6,2,32,384]{3,2,1,0:T(8,128)}, f32[6,2,32,384]{3,2,1,0:T(8,128)}, u32[]{:S(2)}, u32[]{:S(2)}) collective-permute-start(f32[6,2,32,384]{3,2,1,0:T(8,128)} %get-tuple-element.9), channel_id=1, source_target_pairs={{0,480},{32,64},{64,32},{96,128},{128,96},{160,192},{192,160},{224... | collective-permute-start | bytes 1769480 | tf_op jit(solution)/shard_map/ppermute | solution.py:198
  9.8 0.0 copy-done.3
  9.8 0.6 broadcast_in_dim.3.pot_ref
  10.4 0.0 collective-permute-done.rim_ref
  10.4 0.0 copy-done.1
  10.4 4.7 %shard_map.37.a_ref = f32[6,2,32,384]{3,2,1,0:T(8,128)} custom-call(s32[1]{0:T(128)} %bitcast.1.side_ref, f32[6,2,32,384]{3,2,1,0:T(8,128)} %collective-permute-done.rim_ref, f32[12,2,32,384]{3,2,1,0:T(8,128)} %bitcast.17, f32[12,2,1,384]{3,2,1,0:T(1,128)} %broadcast_in_dim.3.pot_ref), custom_call_target="tpu_custom_call" | custom-call | tf_op jit(solution)/shard_map/pallas_call | solution.py:172
  15.1 1.9 %collective-permute-start.1 = (f32[6,2,32,384]{3,2,1,0:T(8,128)}, f32[6,2,32,384]{3,2,1,0:T(8,128)S(1)}, u32[]{:S(2)}, u32[]{:S(2)}) collective-permute-start(f32[6,2,32,384]{3,2,1,0:T(8,128)} %shard_map.37.a_ref), channel_id=1, source_target_pairs={{0,32},{32,0},{64,96},{96,64},{128,160},{160,128},{192,224},{224,1... | collective-permute-start | bytes 1769480 | tf_op jit(solution)/shard_map/ppermute | solution.py:198
  17.1 3.6 %collective-permute-done.2.rim_ref = f32[6,2,32,384]{3,2,1,0:T(8,128)} collective-permute-done((f32[6,2,32,384]{3,2,1,0:T(8,128)}, f32[6,2,32,384]{3,2,1,0:T(8,128)}, u32[]{:S(2)}, u32[]{:S(2)}) %collective-permute-start.2) | collective-permute-done | bytes 589856 | tf_op jit(solution)/shard_map/ppermute | solution.py:198
  20.7 4.7 %shard_map.38.b_ref = f32[6,2,32,384]{3,2,1,0:T(8,128)} custom-call(s32[1]{0:T(128)} %bitcast.side_ref, f32[6,2,32,384]{3,2,1,0:T(8,128)} %collective-permute-done.2.rim_ref, f32[12,2,32,384]{3,2,1,0:T(8,128)} %bitcast.18, f32[12,2,1,384]{3,2,1,0:T(1,128)} %broadcast_in_dim.3.pot_ref), custom_call_target="tpu_custom_call" | custom-call | tf_op jit(solution)/shard_map/pallas_call | solution.py:172
  25.4 4.2 %collective-permute-start.3 = (f32[6,2,32,384]{3,2,1,0:T(8,128)}, f32[6,2,32,384]{3,2,1,0:T(8,128)}, u32[]{:S(2)}, u32[]{:S(2)}) collective-permute-start(f32[6,2,32,384]{3,2,1,0:T(8,128)} %shard_map.38.b_ref), channel_id=1, source_target_pairs={{0,480},{32,64},{64,32},{96,128},{128,96},{160,192},{192,160},{224... | collective-permute-start | bytes 1769480 | tf_op jit(solution)/shard_map/ppermute | solution.py:198
  29.6 0.7 pad_add_fusion
  30.3 0.0 collective-permute-done.1.rim_ref
  30.3 0.0 copy-start.2
  30.3 0.8 copy-done.2
  31.1 5.1 %shard_map.39 = f32[6,2,32,384]{3,2,1,0:T(8,128)} custom-call(s32[2]{0:T(128)} %get-tuple-element.12.side_ref, f32[6,2,32,384]{3,2,1,0:T(8,128)} %copy-done.2, f32[6,2,32,384]{3,2,1,0:T(8,128)} %shard_map.37.a_ref, f32[6,2,32,384]{3,2,1,0:T(8,128)} %shard_map.38.b_ref, f32[12,2,32,384]{3,2,1,0:T(8,128)} %bitcast.19, f32[12,2,1,384]{3,2,1,0:T(1,128)} %broadcast_in_dim.3.pot_ref), custom_call_target="tpu_custom_call" | custom-call | tf_op jit(solution)/shard_map/pallas_call | solution.py:184
  36.2 1.1 convert_bitcast_fusion
  37.3 0.2 copy.12
  37.5 0.5 reshape.28
  38.0 0.1 copy.13
  38.1 0.7 reshape.29
  38.8 1.7 %collective-permute-done.3.rim_ref = f32[6,2,32,384]{3,2,1,0:T(8,128)} collective-permute-done((f32[6,2,32,384]{3,2,1,0:T(8,128)}, f32[6,2,32,384]{3,2,1,0:T(8,128)}, u32[]{:S(2)}, u32[]{:S(2)}) %collective-permute-start.3) | collective-permute-done | bytes 589856 | tf_op jit(solution)/shard_map/ppermute | solution.py:198
  40.5 5.1 %shard_map.40 = f32[6,2,32,384]{3,2,1,0:T(8,128)} custom-call(s32[2]{0:T(128)} %get-tuple-element.11.side_ref, f32[6,2,32,384]{3,2,1,0:T(8,128)} %collective-permute-done.3.rim_ref, f32[6,2,32,384]{3,2,1,0:T(8,128)} %shard_map.37.a_ref, f32[6,2,32,384]{3,2,1,0:T(8,128)} %shard_map.38.b_ref, f32[12,2,32,384]{3,2,1,0:T(8,128)} %bitcast.20, ...), custom_call_target="tpu_custom_call" | custom-call | tf_op jit(solution)/shard_map/pallas_call | solution.py:184
  45.6 1.1 convert_bitcast_fusion.1
  46.7 0.2 copy.10
  46.9 0.5 reshape.26
  47.5 0.1 copy.11
  47.6 0.7 reshape.27
  48.3 0.1 maximum_select_fusion
  48.4 46.2 %all_to_all.10 = bf16[32,24,384]{2,1,0:T(8,128)(2,1)S(1)} all-to-all(bf16[32,24,384]{2,1,0:T(8,128)(2,1)S(1)} %maximum_select_fusion), channel_id=1, replica_groups=mesh['dom'=16,'band'=32] {'band'}, dimensions={0} | all-to-all | bytes 1179648 | tf_op jit(solution)/shard_map/all_to_all | solution.py:243
  94.6 1.1 reshape.30
  95.7 0.0 copy-done
  95.7 0.8 fusion
  96.5 0.4 copy.14
  96.9 1.4 reshape.31
  98.3 36.9 %all_to_all.11 = bf16[32,24,384]{2,1,0:T(8,128)(2,1)} all-to-all(bf16[32,24,384]{2,1,0:T(8,128)(2,1)S(1)} %reshape.31), channel_id=1, replica_groups=mesh['dom'=16,'band'=32] {'band'}, dimensions={0} | all-to-all | bytes 1179648 | tf_op jit(solution)/shard_map/all_to_all | solution.py:250
  135.2 2.2 %reshape.32 = bf16[32,32,288]{2,1,0:T(8,128)(2,1)S(1)} reshape(bf16[32,24,384]{2,1,0:T(8,128)(2,1)} %all_to_all.11) | data formatting | bytes 1179648 | tf_op jit(solution)/shard_map/reshape | solution.py:251
  137.4 1.1 copy.15
  138.6 3.5 %reshape.33 = bf16[32,12,2,384]{3,2,1,0:T(2,128)(2,1)} reshape(bf16[32,32,288]{2,1,0:T(8,128)(2,1)} %copy.15) | data formatting | bytes 1179648 | tf_op jit(solution)/shard_map/reshape | solution.py:252
Async XLA Ops:
  0.0 95.7 %copy-start = (bf16[1024,1024]{1,0:T(8,128)(2,1)S(1)}, bf16[1024,1024]{1,0:T(8,128)(2,1)}, u32[]{:S(2)}) copy-start(bf16[1024,1024]{1,0:T(8,128)(2,1)} %param.5) | copy-start | bytes 6291460
  0.0 9.8 %copy-start.3 = (f32[12,2,384]{2,1,0:T(2,128)S(1)}, f32[12,2,384]{2,1,0:T(2,128)}, u32[]{:S(2)}) copy-start(f32[12,2,384]{2,1,0:T(2,128)} %param.4) | copy-start | bytes 110596
  1.7 8.8 %copy-start.1 = (f32[32,12,2,384]{3,0,2,1:T(8,128)}, f32[32,12,2,384]{3,0,2,1:T(8,128)S(1)}, u32[]{:S(2)}) copy-start(f32[32,12,2,384]{3,0,2,1:T(8,128)S(1)} %copy.17) | copy-start | bytes 3538948
  3.0 7.5 %collective-permute-start = (f32[6,2,32,384]{3,2,1,0:T(8,128)}, f32[6,2,32,384]{3,2,1,0:T(8,128)}, u32[]{:S(2)}, u32[]{:S(2)}) collective-permute-start(f32[6,2,32,384]{3,2,1,0:T(8,128)} %get-tuple-element.10), channel_id=1, source_target_pairs={{0,32},{32,0},{64,96},{96,64},{128,160},{160,128},{192,224},{224,1... | collective-permute-start | bytes 1769480 | tf_op jit(solution)/shard_map/ppermute | solution.py:198
  5.5 15.1 %collective-permute-start.2 = (f32[6,2,32,384]{3,2,1,0:T(8,128)}, f32[6,2,32,384]{3,2,1,0:T(8,128)}, u32[]{:S(2)}, u32[]{:S(2)}) collective-permute-start(f32[6,2,32,384]{3,2,1,0:T(8,128)} %get-tuple-element.9), channel_id=1, source_target_pairs={{0,480},{32,64},{64,32},{96,128},{128,96},{160,192},{192,160},{224... | collective-permute-start | bytes 1769480 | tf_op jit(solution)/shard_map/ppermute | solution.py:198
  15.1 15.1 %collective-permute-start.1 = (f32[6,2,32,384]{3,2,1,0:T(8,128)}, f32[6,2,32,384]{3,2,1,0:T(8,128)S(1)}, u32[]{:S(2)}, u32[]{:S(2)}) collective-permute-start(f32[6,2,32,384]{3,2,1,0:T(8,128)} %shard_map.37.a_ref), channel_id=1, source_target_pairs={{0,32},{32,0},{64,96},{96,64},{128,160},{160,128},{192,224},{224,1... | collective-permute-start | bytes 1769480 | tf_op jit(solution)/shard_map/ppermute | solution.py:198
  25.4 15.1 %collective-permute-start.3 = (f32[6,2,32,384]{3,2,1,0:T(8,128)}, f32[6,2,32,384]{3,2,1,0:T(8,128)}, u32[]{:S(2)}, u32[]{:S(2)}) collective-permute-start(f32[6,2,32,384]{3,2,1,0:T(8,128)} %shard_map.38.b_ref), channel_id=1, source_target_pairs={{0,480},{32,64},{64,32},{96,128},{128,96},{160,192},{192,160},{224... | collective-permute-start | bytes 1769480 | tf_op jit(solution)/shard_map/ppermute | solution.py:198
  30.3 0.8 copy-start.2

commit v14 on v13

--- a/solution.py
+++ b/solution.py
@@ -152,7 +152,8 @@
     def body(x, carry):
         for z in range(depth):
             hv, mid = ham_planes(ext_ref, pot_ref, base + x, z, ny)
-            out_ref[x, z] = 2.0 / half_width * (hv - center_shift * mid) - psi_ref[base + x, z]
+            second = 2.0 / half_width * (hv - center_shift * mid) - psi_ref[base + x, z]
+            out_ref[x, z] = second.astype(out_ref.dtype)
         return carry
 
     lax.fori_loop(0, half, body, 0)
@@ -186,7 +187,7 @@
         grid=(1,),
         in_specs=[smem(), whole(rim.shape), whole(a.shape), whole(b.shape), whole(psi.shape), whole(pot.shape)],
         out_specs=whole(a.shape),
-        out_shape=jax.ShapeDtypeStruct(a.shape, jnp.float32),
+        out_shape=jax.ShapeDtypeStruct(a.shape, jnp.bfloat16),
         scratch_shapes=[pltpu.VMEM((planes + 2 * reach, depth, states, ny), jnp.float32)],
     )(side, rim, a, b, psi, pot)
 

time: 145 us -> 144 us (level)
  the two profiles are of different devices: /device:TPU:25 before, /device:TPU:16 now
where the time goes in v14:
time: 144 us
  blocking collectives  89.2 us (62%)
  Pallas kernels  19.4 us (13%)
  local copies, waits for them, and re-layouts  17.8 us (12%)
  starting transfers between devices  13.2 us (9%)
  other arithmetic  2.06 us (1%)
    all_to_all x1, blocking collectives, per_device(): gathered = lax.all_to_all(blocks, 'band', 0, 0, tiled=True)  49.3 us
    all_to_all x1, blocking collectives, per_device(): back = lax.all_to_all(mixed.reshape(wire), 'band', 0, 0, tiled=True)  39.9 us
    pallas_call x2, Pallas kernels, run_second_half(): pl.pallas_call(second_half_kernel, grid=(1,), in_specs=[smem(), whole(rim...  9.98 us
    pallas_call x2, Pallas kernels, run_first_half(): pl.pallas_call(first_half_kernel, grid=(1,), in_specs=[smem(), whole(rim....  9.43 us
    ppermute x2, starting transfers between devices, inner_outer(): lax.ppermute(send_outer, 'dom', outer)  8.52 us
    ppermute x2, starting transfers between devices, inner_outer(): lax.ppermute(send_inner, 'dom', inner)  4.65 us
    reshape x1, local copies, waits for them, and re-layouts, per_device(): return result.reshape(psi.shape)  3.52 us
  transfers between devices with their start and end apart: 4, of which 1 were waited for; matrix products, arithmetic and copies ran while one was open for 3% of the time, Pallas kernels for 10%

profile of v14, /device:TPU:16, one launch (start us, length us, event | category | flops | bytes accessed | tf_op | source)
XLA Modules:
  0.0 143.5 jit_solution(7451368229500125323)
XLA Ops:
  0.0 0.0 copy-start
  0.0 0.0 copy-start.3
  0.0 1.7 %copy.17 = f32[32,12,2,384]{3,0,2,1:T(8,128)S(1)} copy(f32[32,12,2,384]{3,2,1,0:T(2,128)} %param.3) | data formatting | bytes 2359296 | tf_op args[0]
  1.7 0.0 copy-start.1
  1.7 1.3 slice_select_fusion
  3.0 1.9 %collective-permute-start = (f32[6,2,32,384]{3,2,1,0:T(8,128)}, f32[6,2,32,384]{3,2,1,0:T(8,128)}, u32[]{:S(2)}, u32[]{:S(2)}) collective-permute-start(f32[6,2,32,384]{3,2,1,0:T(8,128)} %get-tuple-element.10), channel_id=1, source_target_pairs={{0,32},{32,0},{64,96},{96,64},{128,160},{160,128},{192,224},{224,1... | collective-permute-start | bytes 1769480 | tf_op jit(solution)/shard_map/ppermute | solution.py:199
  4.9 2.5 %collective-permute-start.2 = (f32[6,2,32,384]{3,2,1,0:T(8,128)}, f32[6,2,32,384]{3,2,1,0:T(8,128)}, u32[]{:S(2)}, u32[]{:S(2)}) collective-permute-start(f32[6,2,32,384]{3,2,1,0:T(8,128)} %get-tuple-element.9), channel_id=1, source_target_pairs={{0,480},{32,64},{64,32},{96,128},{128,96},{160,192},{192,160},{224... | collective-permute-start | bytes 1769480 | tf_op jit(solution)/shard_map/ppermute | solution.py:199
  7.4 0.0 copy-done.3
  7.4 0.6 broadcast_in_dim.3.pot_ref
  8.0 0.0 collective-permute-done.rim_ref
  8.0 0.0 copy-done.1
  8.0 4.7 %shard_map.37.a_ref = f32[6,2,32,384]{3,2,1,0:T(8,128)} custom-call(s32[1]{0:T(128)} %bitcast.1.side_ref, f32[6,2,32,384]{3,2,1,0:T(8,128)} %collective-permute-done.rim_ref, f32[12,2,32,384]{3,2,1,0:T(8,128)} %bitcast.15, f32[12,2,1,384]{3,2,1,0:T(1,128)} %broadcast_in_dim.3.pot_ref), custom_call_target="tpu_custom_call" | custom-call | tf_op jit(solution)/shard_map/pallas_call | solution.py:173
  12.7 2.7 %collective-permute-start.1 = (f32[6,2,32,384]{3,2,1,0:T(8,128)}, f32[6,2,32,384]{3,2,1,0:T(8,128)S(1)}, u32[]{:S(2)}, u32[]{:S(2)}) collective-permute-start(f32[6,2,32,384]{3,2,1,0:T(8,128)} %shard_map.37.a_ref), channel_id=1, source_target_pairs={{0,32},{32,0},{64,96},{96,64},{128,160},{160,128},{192,224},{224,1... | collective-permute-start | bytes 1769480 | tf_op jit(solution)/shard_map/ppermute | solution.py:199
  15.5 0.9 collective-permute-done.2.rim_ref
  16.4 4.7 %shard_map.38.b_ref = f32[6,2,32,384]{3,2,1,0:T(8,128)} custom-call(s32[1]{0:T(128)} %bitcast.side_ref, f32[6,2,32,384]{3,2,1,0:T(8,128)} %collective-permute-done.2.rim_ref, f32[12,2,32,384]{3,2,1,0:T(8,128)} %bitcast.16, f32[12,2,1,384]{3,2,1,0:T(1,128)} %broadcast_in_dim.3.pot_ref), custom_call_target="tpu_custom_call" | custom-call | tf_op jit(solution)/shard_map/pallas_call | solution.py:173
  21.1 6.1 %collective-permute-start.3 = (f32[6,2,32,384]{3,2,1,0:T(8,128)}, f32[6,2,32,384]{3,2,1,0:T(8,128)}, u32[]{:S(2)}, u32[]{:S(2)}) collective-permute-start(f32[6,2,32,384]{3,2,1,0:T(8,128)} %shard_map.38.b_ref), channel_id=1, source_target_pairs={{0,480},{32,64},{64,32},{96,128},{128,96},{160,192},{192,160},{224... | collective-permute-start | bytes 1769480 | tf_op jit(solution)/shard_map/ppermute | solution.py:199
  27.2 0.7 pad_add_fusion
  27.8 0.0 collective-permute-done.1.rim_ref
  27.8 0.0 copy-start.2
  27.8 0.8 copy-done.2
  28.7 5.0 %shard_map.39 = bf16[6,2,32,384]{3,2,1,0:T(8,128)(2,1)} custom-call(s32[2]{0:T(128)} %get-tuple-element.12.side_ref, f32[6,2,32,384]{3,2,1,0:T(8,128)} %copy-done.2, f32[6,2,32,384]{3,2,1,0:T(8,128)} %shard_map.37.a_ref, f32[6,2,32,384]{3,2,1,0:T(8,128)} %shard_map.38.b_ref, f32[12,2,32,384]{3,2,1,0:T(8,128)} %bitcast.17, ...), custom_call_target="tpu_custom_call" | custom-call | tf_op jit(solution)/shard_map/pallas_call | solution.py:185
  33.7 1.2 copy.12
  34.8 0.5 reshape.28
  35.4 0.1 copy.13
  35.5 0.7 reshape.29
  36.2 0.0 collective-permute-done.3.rim_ref
  36.2 5.0 %shard_map.40 = bf16[6,2,32,384]{3,2,1,0:T(8,128)(2,1)} custom-call(s32[2]{0:T(128)} %get-tuple-element.11.side_ref, f32[6,2,32,384]{3,2,1,0:T(8,128)} %collective-permute-done.3.rim_ref, f32[6,2,32,384]{3,2,1,0:T(8,128)} %shard_map.37.a_ref, f32[6,2,32,384]{3,2,1,0:T(8,128)} %shard_map.38.b_ref, f32[12,2,32,384]{3,2,1,0:T(8,128)} %bitcast.18, ...), custom_call_target="tpu_custom_call" | custom-call | tf_op jit(solution)/shard_map/pallas_call | solution.py:185
  41.1 1.2 copy.10
  42.3 0.5 reshape.26
  42.9 0.1 copy.11
  43.0 0.7 reshape.27
  43.7 0.1 maximum_select_fusion
  43.8 49.3 %all_to_all.10 = bf16[32,24,384]{2,1,0:T(8,128)(2,1)S(1)} all-to-all(bf16[32,24,384]{2,1,0:T(8,128)(2,1)S(1)} %maximum_select_fusion), channel_id=1, replica_groups=mesh['dom'=16,'band'=32] {'band'}, dimensions={0} | all-to-all | bytes 1179648 | tf_op jit(solution)/shard_map/all_to_all | solution.py:244
  93.0 1.1 reshape.30
  94.1 0.0 copy-done
  94.1 0.8 fusion
  95.0 0.4 copy.14
  95.3 1.4 reshape.31
  96.7 39.9 %all_to_all.11 = bf16[32,24,384]{2,1,0:T(8,128)(2,1)} all-to-all(bf16[32,24,384]{2,1,0:T(8,128)(2,1)S(1)} %reshape.31), channel_id=1, replica_groups=mesh['dom'=16,'band'=32] {'band'}, dimensions={0} | all-to-all | bytes 1179648 | tf_op jit(solution)/shard_map/all_to_all | solution.py:251
  136.6 2.2 %reshape.32 = bf16[32,32,288]{2,1,0:T(8,128)(2,1)S(1)} reshape(bf16[32,24,384]{2,1,0:T(8,128)(2,1)} %all_to_all.11) | data formatting | bytes 1179648 | tf_op jit(solution)/shard_map/reshape | solution.py:252
  138.9 1.1 copy.15
  140.0 3.5 %reshape.33 = bf16[32,12,2,384]{3,2,1,0:T(2,128)(2,1)} reshape(bf16[32,32,288]{2,1,0:T(8,128)(2,1)} %copy.15) | data formatting | bytes 1179648 | tf_op jit(solution)/shard_map/reshape | solution.py:253
Async XLA Ops:
  0.0 94.1 %copy-start = (bf16[1024,1024]{1,0:T(8,128)(2,1)S(1)}, bf16[1024,1024]{1,0:T(8,128)(2,1)}, u32[]{:S(2)}) copy-start(bf16[1024,1024]{1,0:T(8,128)(2,1)} %param.5) | copy-start | bytes 6291460
  0.0 7.4 %copy-start.3 = (f32[12,2,384]{2,1,0:T(2,128)S(1)}, f32[12,2,384]{2,1,0:T(2,128)}, u32[]{:S(2)}) copy-start(f32[12,2,384]{2,1,0:T(2,128)} %param.4) | copy-start | bytes 110596
  1.7 6.3 %copy-start.1 = (f32[32,12,2,384]{3,0,2,1:T(8,128)}, f32[32,12,2,384]{3,0,2,1:T(8,128)S(1)}, u32[]{:S(2)}) copy-start(f32[32,12,2,384]{3,0,2,1:T(8,128)S(1)} %copy.17) | copy-start | bytes 3538948
  3.0 5.0 %collective-permute-start = (f32[6,2,32,384]{3,2,1,0:T(8,128)}, f32[6,2,32,384]{3,2,1,0:T(8,128)}, u32[]{:S(2)}, u32[]{:S(2)}) collective-permute-start(f32[6,2,32,384]{3,2,1,0:T(8,128)} %get-tuple-element.10), channel_id=1, source_target_pairs={{0,32},{32,0},{64,96},{96,64},{128,160},{160,128},{192,224},{224,1... | collective-permute-start | bytes 1769480 | tf_op jit(solution)/shard_map/ppermute | solution.py:199
  4.9 11.5 %collective-permute-start.2 = (f32[6,2,32,384]{3,2,1,0:T(8,128)}, f32[6,2,32,384]{3,2,1,0:T(8,128)}, u32[]{:S(2)}, u32[]{:S(2)}) collective-permute-start(f32[6,2,32,384]{3,2,1,0:T(8,128)} %get-tuple-element.9), channel_id=1, source_target_pairs={{0,480},{32,64},{64,32},{96,128},{128,96},{160,192},{192,160},{224... | collective-permute-start | bytes 1769480 | tf_op jit(solution)/shard_map/ppermute | solution.py:199
  12.7 15.1 %collective-permute-start.1 = (f32[6,2,32,384]{3,2,1,0:T(8,128)}, f32[6,2,32,384]{3,2,1,0:T(8,128)S(1)}, u32[]{:S(2)}, u32[]{:S(2)}) collective-permute-start(f32[6,2,32,384]{3,2,1,0:T(8,128)} %shard_map.37.a_ref), channel_id=1, source_target_pairs={{0,32},{32,0},{64,96},{96,64},{128,160},{160,128},{192,224},{224,1... | collective-permute-start | bytes 1769480 | tf_op jit(solution)/shard_map/ppermute | solution.py:199
  21.1 15.1 %collective-permute-start.3 = (f32[6,2,32,384]{3,2,1,0:T(8,128)}, f32[6,2,32,384]{3,2,1,0:T(8,128)}, u32[]{:S(2)}, u32[]{:S(2)}) collective-permute-start(f32[6,2,32,384]{3,2,1,0:T(8,128)} %shard_map.38.b_ref), channel_id=1, source_target_pairs={{0,480},{32,64},{64,32},{96,128},{128,96},{160,192},{192,160},{224... | collective-permute-start | bytes 1769480 | tf_op jit(solution)/shard_map/ppermute | solution.py:199
  27.8 0.8 copy-start.2

commit v15 on v14

--- a/solution.py
+++ b/solution.py
@@ -223,8 +223,11 @@
     else:
         even = lax.axis_index("dom") % 2 == 0
         hi = jnp.where(even, 1, 0).astype(jnp.int32)
-        head, tail = psi_t[:reach], psi_t[planes - reach :]
-        rim_in, rim_out = inner_outer(jnp.where(even, tail, head), jnp.where(even, head, tail))
+        in_send = lax.dynamic_slice_in_dim(psi, hi * reach, reach, 1).transpose(1, 2, 0, 3)
+        out_send = lax.dynamic_slice_in_dim(psi, (1 - hi) * reach, reach, 1).transpose(1, 2, 0, 3)
+        psi_b, in_send, out_send = lax.optimization_barrier((psi, in_send, out_send))
+        psi_t = psi_b.transpose(1, 2, 0, 3)
+        rim_in, rim_out = inner_outer(in_send, out_send)
         part_a = run_first_half(hi.reshape(1), rim_in, psi_t, pot_t)
         _, rim_out = lax.optimization_barrier((part_a, rim_out))
         part_b = run_first_half((1 - hi).reshape(1), rim_out, psi_t, pot_t)

time: 144 us -> 145 us (level)
  the two profiles are of different devices: /device:TPU:16 before, /device:TPU:25 now
where the time goes in v15:
time: 145 us; the launch traced here: 144 us
  blocking collectives  86.3 us (60%)
  local copies, waits for them, and re-layouts  20.2 us (14%)
  Pallas kernels  19.4 us (13%)
  starting transfers between devices  12.9 us (9%)
  waiting for transfers between devices  3.3 us (2%)
    all_to_all x1, blocking collectives, per_device(): gathered = lax.all_to_all(blocks, 'band', 0, 0, tiled=True)  47.6 us
    all_to_all x1, blocking collectives, per_device(): back = lax.all_to_all(mixed.reshape(wire), 'band', 0, 0, tiled=True)  38.8 us
    pallas_call x2, Pallas kernels, run_second_half(): pl.pallas_call(second_half_kernel, grid=(1,), in_specs=[smem(), whole(rim...  9.96 us
    pallas_call x2, Pallas kernels, run_first_half(): pl.pallas_call(first_half_kernel, grid=(1,), in_specs=[smem(), whole(rim....  9.42 us
    ppermute x2, starting transfers between devices, inner_outer(): lax.ppermute(send_outer, 'dom', outer)  8.41 us
    ppermute x2, starting transfers between devices, inner_outer(): lax.ppermute(send_inner, 'dom', inner)  4.49 us
    reshape x1, local copies, waits for them, and re-layouts, per_device(): return result.reshape(psi.shape)  3.52 us
    ppermute x2, waiting for transfers between devices, inner_outer(): lax.ppermute(send_outer, 'dom', outer)  3.3 us
  transfers between devices with their start and end apart: 4, of which 2 were waited for; matrix products, arithmetic and copies ran while one was open for 3% of the time, Pallas kernels for 10%

profile of v15, /device:TPU:25, one launch (start us, length us, event | category | flops | bytes accessed | tf_op | source)
XLA Modules:
  0.0 143.8 jit_solution(18343931044140339767)
XLA Ops:
  0.0 0.0 copy-start
  0.0 0.0 copy-start.1
  0.0 1.8 %constant_dynamic-slice_fusion = (f32[32,6,2,384]{3,2,1,0:T(2,128)S(1)}, f32[32,6,2,384]{3,2,1,0:T(2,128)S(1)}) fusion(f32[32,12,2,384]{3,2,1,0:T(2,128)} %param.3, s32[]{:T(128)S(6)} %select_n.29, s32[]{:T(128)S(6)} %select_n.28), kind=kLoop, calls=%fused_computation.8 | loop fusion | bytes 2359304 | tf_op jit(solution)/shard_map/dynamic_slice | solution.py:227
  1.8 0.0 copy-start.4
  1.8 0.1 copy_bitcast_fusion.1
  2.0 2.6 %collective-permute-start = (f32[6,2,32,384]{3,2,1,0:T(8,128)S(1)}, f32[6,2,32,384]{3,2,1,0:T(8,128)S(1)}, u32[]{:S(2)}, u32[]{:S(2)}) collective-permute-start(f32[6,2,32,384]{3,2,1,0:T(8,128)S(1)} %get-tuple-element.10), channel_id=1, source_target_pairs={{0,32},{32,0},{64,96},{96,64},{128,160},{160,128},{192,224},{224,1... | collective-permute-start | bytes 1769480 | tf_op jit(solution)/shard_map/ppermute | solution.py:199
  4.6 4.2 %collective-permute-start.2 = (f32[6,2,32,384]{3,2,1,0:T(8,128)S(1)}, f32[6,2,32,384]{3,2,1,0:T(8,128)}, u32[]{:S(2)}, u32[]{:S(2)}) collective-permute-start(f32[6,2,32,384]{3,2,1,0:T(8,128)S(1)} %get-tuple-element.12), channel_id=1, source_target_pairs={{0,480},{32,64},{64,32},{96,128},{128,96},{160,192},{192,160},{224... | collective-permute-start | bytes 1769480 | tf_op jit(solution)/shard_map/ppermute | solution.py:199
  8.8 0.0 copy-done.1
  8.8 1.2 copy.27
  10.0 0.0 copy-done.4
  10.0 0.6 broadcast_in_dim.3.pot_ref
  10.7 0.0 collective-permute-done.rim_ref
  10.7 0.0 copy-start.3
  10.7 0.8 copy-done.3
  11.5 4.7 %shard_map.37.a_ref = f32[6,2,32,384]{3,2,1,0:T(8,128)} custom-call(s32[1]{0:T(128)} %bitcast.1.side_ref, f32[6,2,32,384]{3,2,1,0:T(8,128)} %copy-done.3, f32[12,2,32,384]{3,2,1,0:T(8,128)} %bitcast.18, f32[12,2,1,384]{3,2,1,0:T(1,128)} %broadcast_in_dim.3.pot_ref), custom_call_target="tpu_custom_call" | custom-call | tf_op jit(solution)/shard_map/pallas_call | solution.py:173
  16.2 1.9 %collective-permute-start.1 = (f32[6,2,32,384]{3,2,1,0:T(8,128)}, f32[6,2,32,384]{3,2,1,0:T(8,128)S(1)}, u32[]{:S(2)}, u32[]{:S(2)}) collective-permute-start(f32[6,2,32,384]{3,2,1,0:T(8,128)} %shard_map.37.a_ref), channel_id=1, source_target_pairs={{0,32},{32,0},{64,96},{96,64},{128,160},{160,128},{192,224},{224,1... | collective-permute-start | bytes 1769480 | tf_op jit(solution)/shard_map/ppermute | solution.py:199
  18.1 1.4 collective-permute-done.2.rim_ref
  19.5 4.7 %shard_map.38.b_ref = f32[6,2,32,384]{3,2,1,0:T(8,128)} custom-call(s32[1]{0:T(128)} %bitcast.side_ref, f32[6,2,32,384]{3,2,1,0:T(8,128)} %collective-permute-done.2.rim_ref, f32[12,2,32,384]{3,2,1,0:T(8,128)} %bitcast.19, f32[12,2,1,384]{3,2,1,0:T(1,128)} %broadcast_in_dim.3.pot_ref), custom_call_target="tpu_custom_call" | custom-call | tf_op jit(solution)/shard_map/pallas_call | solution.py:173
  24.2 4.2 %collective-permute-start.3 = (f32[6,2,32,384]{3,2,1,0:T(8,128)}, f32[6,2,32,384]{3,2,1,0:T(8,128)}, u32[]{:S(2)}, u32[]{:S(2)}) collective-permute-start(f32[6,2,32,384]{3,2,1,0:T(8,128)} %shard_map.38.b_ref), channel_id=1, source_target_pairs={{0,480},{32,64},{64,32},{96,128},{128,96},{160,192},{192,160},{224... | collective-permute-start | bytes 1769480 | tf_op jit(solution)/shard_map/ppermute | solution.py:199
  28.4 0.7 pad_add_fusion
  29.1 0.0 collective-permute-done.1.rim_ref
  29.1 0.0 copy-start.2
  29.1 0.8 copy-done.2
  29.9 5.0 %shard_map.39 = bf16[6,2,32,384]{3,2,1,0:T(8,128)(2,1)} custom-call(s32[2]{0:T(128)} %get-tuple-element.18.side_ref, f32[6,2,32,384]{3,2,1,0:T(8,128)} %copy-done.2, f32[6,2,32,384]{3,2,1,0:T(8,128)} %shard_map.37.a_ref, f32[6,2,32,384]{3,2,1,0:T(8,128)} %shard_map.38.b_ref, f32[12,2,32,384]{3,2,1,0:T(8,128)} %bitcast.20, ...), custom_call_target="tpu_custom_call" | custom-call | tf_op jit(solution)/shard_map/pallas_call | solution.py:185
  34.9 1.2 copy.18
  36.1 0.5 reshape.28
  36.6 0.1 copy.19
  36.7 0.7 reshape.29
  37.4 1.9 %collective-permute-done.3.rim_ref = f32[6,2,32,384]{3,2,1,0:T(8,128)} collective-permute-done((f32[6,2,32,384]{3,2,1,0:T(8,128)}, f32[6,2,32,384]{3,2,1,0:T(8,128)}, u32[]{:S(2)}, u32[]{:S(2)}) %collective-permute-start.3) | collective-permute-done | bytes 589856 | tf_op jit(solution)/shard_map/ppermute | solution.py:199
  39.3 5.0 %shard_map.40 = bf16[6,2,32,384]{3,2,1,0:T(8,128)(2,1)} custom-call(s32[2]{0:T(128)} %get-tuple-element.17.side_ref, f32[6,2,32,384]{3,2,1,0:T(8,128)} %collective-permute-done.3.rim_ref, f32[6,2,32,384]{3,2,1,0:T(8,128)} %shard_map.37.a_ref, f32[6,2,32,384]{3,2,1,0:T(8,128)} %shard_map.38.b_ref, f32[12,2,32,384]{3,2,1,0:T(8,128)} %bitcast.21, ...), custom_call_target="tpu_custom_call" | custom-call | tf_op jit(solution)/shard_map/pallas_call | solution.py:185
  44.3 1.2 copy.16
  45.5 0.5 reshape.26
  46.0 0.1 copy.17
  46.1 0.7 reshape.27
  46.8 0.1 maximum_select_fusion
  46.9 47.6 %all_to_all.10 = bf16[32,24,384]{2,1,0:T(8,128)(2,1)S(1)} all-to-all(bf16[32,24,384]{2,1,0:T(8,128)(2,1)S(1)} %maximum_select_fusion), channel_id=1, replica_groups=mesh['dom'=16,'band'=32] {'band'}, dimensions={0} | all-to-all | bytes 1179648 | tf_op jit(solution)/shard_map/all_to_all | solution.py:247
  94.5 1.1 reshape.30
  95.6 0.0 copy-done
  95.6 0.8 fusion
  96.4 0.4 copy.20
  96.8 1.4 reshape.31
  98.2 38.8 %all_to_all.11 = bf16[32,24,384]{2,1,0:T(8,128)(2,1)} all-to-all(bf16[32,24,384]{2,1,0:T(8,128)(2,1)S(1)} %reshape.31), channel_id=1, replica_groups=mesh['dom'=16,'band'=32] {'band'}, dimensions={0} | all-to-all | bytes 1179648 | tf_op jit(solution)/shard_map/all_to_all | solution.py:254
  136.9 2.2 %reshape.32 = bf16[32,32,288]{2,1,0:T(8,128)(2,1)S(1)} reshape(bf16[32,24,384]{2,1,0:T(8,128)(2,1)} %all_to_all.11) | data formatting | bytes 1179648 | tf_op jit(solution)/shard_map/reshape | solution.py:255
  139.2 1.1 copy.21
  140.3 3.5 %reshape.33 = bf16[32,12,2,384]{3,2,1,0:T(2,128)(2,1)} reshape(bf16[32,32,288]{2,1,0:T(8,128)(2,1)} %copy.21) | data formatting | bytes 1179648 | tf_op jit(solution)/shard_map/reshape | solution.py:256
Async XLA Ops:
  0.0 95.6 %copy-start = (bf16[1024,1024]{1,0:T(8,128)(2,1)S(1)}, bf16[1024,1024]{1,0:T(8,128)(2,1)}, u32[]{:S(2)}) copy-start(bf16[1024,1024]{1,0:T(8,128)(2,1)} %param.5) | copy-start | bytes 6291460
  0.0 8.8 %copy-start.1 = (f32[32,12,2,384]{3,2,1,0:T(2,128)S(1)}, f32[32,12,2,384]{3,2,1,0:T(2,128)}, u32[]{:S(2)}) copy-start(f32[32,12,2,384]{3,2,1,0:T(2,128)} %param.3) | copy-start | bytes 3538948
  1.8 8.2 %copy-start.4 = (f32[12,2,384]{2,1,0:T(2,128)S(1)}, f32[12,2,384]{2,1,0:T(2,128)}, u32[]{:S(2)}) copy-start(f32[12,2,384]{2,1,0:T(2,128)} %param.4) | copy-start | bytes 110596
  2.0 8.7 %collective-permute-start = (f32[6,2,32,384]{3,2,1,0:T(8,128)S(1)}, f32[6,2,32,384]{3,2,1,0:T(8,128)S(1)}, u32[]{:S(2)}, u32[]{:S(2)}) collective-permute-start(f32[6,2,32,384]{3,2,1,0:T(8,128)S(1)} %get-tuple-element.10), channel_id=1, source_target_pairs={{0,32},{32,0},{64,96},{96,64},{128,160},{160,128},{192,224},{224,1... | collective-permute-start | bytes 1769480 | tf_op jit(solution)/shard_map/ppermute | solution.py:199
  4.6 14.9 %collective-permute-start.2 = (f32[6,2,32,384]{3,2,1,0:T(8,128)S(1)}, f32[6,2,32,384]{3,2,1,0:T(8,128)}, u32[]{:S(2)}, u32[]{:S(2)}) collective-permute-start(f32[6,2,32,384]{3,2,1,0:T(8,128)S(1)} %get-tuple-element.12), channel_id=1, source_target_pairs={{0,480},{32,64},{64,32},{96,128},{128,96},{160,192},{192,160},{224... | collective-permute-start | bytes 1769480 | tf_op jit(solution)/shard_map/ppermute | solution.py:199
  10.7 0.8 copy-start.3
  16.2 12.8 %collective-permute-start.1 = (f32[6,2,32,384]{3,2,1,0:T(8,128)}, f32[6,2,32,384]{3,2,1,0:T(8,128)S(1)}, u32[]{:S(2)}, u32[]{:S(2)}) collective-permute-start(f32[6,2,32,384]{3,2,1,0:T(8,128)} %shard_map.37.a_ref), channel_id=1, source_target_pairs={{0,32},{32,0},{64,96},{96,64},{128,160},{160,128},{192,224},{224,1... | collective-permute-start | bytes 1769480 | tf_op jit(solution)/shard_map/ppermute | solution.py:199
  24.2 15.1 %collective-permute-start.3 = (f32[6,2,32,384]{3,2,1,0:T(8,128)}, f32[6,2,32,384]{3,2,1,0:T(8,128)}, u32[]{:S(2)}, u32[]{:S(2)}) collective-permute-start(f32[6,2,32,384]{3,2,1,0:T(8,128)} %shard_map.38.b_ref), channel_id=1, source_target_pairs={{0,480},{32,64},{64,32},{96,128},{128,96},{160,192},{192,160},{224... | collective-permute-start | bytes 1769480 | tf_op jit(solution)/shard_map/ppermute | solution.py:199
  29.1 0.8 copy-start.2

commit v16 on v14

--- a/solution.py
+++ b/solution.py
@@ -139,8 +139,8 @@
 
 
 def second_half_kernel(side_ref, rim_ref, a_ref, b_ref, psi_ref, pot_ref, out_ref, ext_ref):
-    planes = psi_ref.shape[0]
-    half = planes - reach
+    half = a_ref.shape[0]
+    planes = 2 * half
     depth, ny = out_ref.shape[1], out_ref.shape[3]
     h = side_ref[0]
     a_side = side_ref[1]
@@ -152,7 +152,7 @@
     def body(x, carry):
         for z in range(depth):
             hv, mid = ham_planes(ext_ref, pot_ref, base + x, z, ny)
-            second = 2.0 / half_width * (hv - center_shift * mid) - psi_ref[base + x, z]
+            second = 2.0 / half_width * (hv - center_shift * mid) - psi_ref[x, z]
             out_ref[x, z] = second.astype(out_ref.dtype)
         return carry
 
@@ -181,7 +181,8 @@
 
 
 def run_second_half(side, rim, a, b, psi, pot):
-    planes, depth, states, ny = psi.shape
+    depth, states, ny = psi.shape[1:]
+    planes = 2 * a.shape[0]
     return pl.pallas_call(
         second_half_kernel,
         grid=(1,),
@@ -231,9 +232,11 @@
         rim_in, rim_out = inner_outer(part_a, part_b)
         sides_a = jnp.stack([hi, hi])
         sides_b = jnp.stack([1 - hi, hi])
-        second_a = run_second_half(sides_a, rim_in, part_a, part_b, psi_t, pot_t)
+        psi_a = lax.dynamic_slice_in_dim(psi_t, hi * reach, reach, 0)
+        psi_b = lax.dynamic_slice_in_dim(psi_t, (1 - hi) * reach, reach, 0)
+        second_a = run_second_half(sides_a, rim_in, part_a, part_b, psi_a, pot_t)
         _, rim_out = lax.optimization_barrier((second_a, rim_out))
-        second_b = run_second_half(sides_b, rim_out, part_a, part_b, psi_t, pot_t)
+        second_b = run_second_half(sides_b, rim_out, part_a, part_b, psi_b, pot_t)
         wire_a = to_wire(second_a, count // 2)
         wire_b = to_wire(second_b, count // 2)
         blocks = jnp.where(

time: 144 us -> 145 us (level)
  the two profiles are of different devices: /device:TPU:16 before, /device:TPU:2 now
where the time goes in v16:
time: 145 us; the launch traced here: 144 us
  blocking collectives  85.4 us (59%)
  Pallas kernels  19.1 us (13%)
  local copies, waits for them, and re-layouts  18 us (12%)
  starting transfers between devices  17 us (12%)
  waiting for transfers between devices  2.98 us (2%)
    all_to_all x1, blocking collectives, per_device(): gathered = lax.all_to_all(blocks, 'band', 0, 0, tiled=True)  48.3 us
    all_to_all x1, blocking collectives, per_device(): back = lax.all_to_all(mixed.reshape(wire), 'band', 0, 0, tiled=True)  37.1 us
    ppermute x2, starting transfers between devices, inner_outer(): lax.ppermute(send_outer, 'dom', outer)  13.2 us
    pallas_call x2, Pallas kernels, run_second_half(): pl.pallas_call(second_half_kernel, grid=(1,), in_specs=[smem(), whole(rim...  9.6 us
    pallas_call x2, Pallas kernels, run_first_half(): pl.pallas_call(first_half_kernel, grid=(1,), in_specs=[smem(), whole(rim....  9.53 us
    ppermute x2, starting transfers between devices, inner_outer(): lax.ppermute(send_inner, 'dom', inner)  3.82 us
    reshape x1, local copies, waits for them, and re-layouts, per_device(): return result.reshape(psi.shape)  3.52 us
    ppermute x2, waiting for transfers between devices, inner_outer(): lax.ppermute(send_outer, 'dom', outer)  2.97 us
  transfers between devices with their start and end apart: 4, of which 2 were waited for; matrix products, arithmetic and copies ran while one was open for 2% of the time, Pallas kernels for 10%

profile of v16, /device:TPU:2, one launch (start us, length us, event | category | flops | bytes accessed | tf_op | source)
XLA Modules:
  0.0 144.5 jit_solution(6575734743010345194)
XLA Ops:
  0.0 0.0 copy-start
  0.0 1.6 %copy.24 = f32[32,12,2,384]{3,0,2,1:T(8,128)S(1)} copy(f32[32,12,2,384]{3,2,1,0:T(2,128)} %param.3) | data formatting | bytes 2359296 | tf_op args[0]
  1.7 0.0 copy-start.1
  1.7 0.0 copy-start.4
  1.7 0.1 slice_select_fusion
  1.8 0.9 copy-done.1
  2.7 1.9 %collective-permute-start = (f32[6,2,32,384]{3,2,1,0:T(8,128)S(1)}, f32[6,2,32,384]{3,2,1,0:T(8,128)}, u32[]{:S(2)}, u32[]{:S(2)}) collective-permute-start(f32[6,2,32,384]{3,2,1,0:T(8,128)S(1)} %get-tuple-element.14), channel_id=1, source_target_pairs={{0,32},{32,0},{64,96},{96,64},{128,160},{160,128},{192,224},{224,1... | collective-permute-start | bytes 1769480 | tf_op jit(solution)/shard_map/ppermute | solution.py:200
  4.6 6.6 %collective-permute-start.2 = (f32[6,2,32,384]{3,2,1,0:T(8,128)S(1)}, f32[6,2,32,384]{3,2,1,0:T(8,128)}, u32[]{:S(2)}, u32[]{:S(2)}) collective-permute-start(f32[6,2,32,384]{3,2,1,0:T(8,128)S(1)} %get-tuple-element.13), channel_id=1, source_target_pairs={{0,480},{32,64},{64,32},{96,128},{128,96},{160,192},{192,160},{224... | collective-permute-start | bytes 1769480 | tf_op jit(solution)/shard_map/ppermute | solution.py:200
  11.2 0.0 copy-done.4
  11.2 0.6 broadcast_in_dim.3.pot_ref
  11.8 0.0 collective-permute-done.rim_ref
  11.8 4.7 %shard_map.37.a_ref = f32[6,2,32,384]{3,2,1,0:T(8,128)} custom-call(s32[1]{0:T(128)} %bitcast.1.side_ref, f32[6,2,32,384]{3,2,1,0:T(8,128)} %collective-permute-done.rim_ref, f32[12,2,32,384]{3,2,1,0:T(8,128)} %bitcast.18, f32[12,2,1,384]{3,2,1,0:T(1,128)} %broadcast_in_dim.3.pot_ref), custom_call_target="tpu_custom_call" | custom-call | tf_op jit(solution)/shard_map/pallas_call | solution.py:173
  16.5 1.9 %collective-permute-start.1 = (f32[6,2,32,384]{3,2,1,0:T(8,128)}, f32[6,2,32,384]{3,2,1,0:T(8,128)}, u32[]{:S(2)}, u32[]{:S(2)}) collective-permute-start(f32[6,2,32,384]{3,2,1,0:T(8,128)} %shard_map.37.a_ref), channel_id=1, source_target_pairs={{0,32},{32,0},{64,96},{96,64},{128,160},{160,128},{192,224},{224,1... | collective-permute-start | bytes 1769480 | tf_op jit(solution)/shard_map/ppermute | solution.py:200
  18.5 1.0 collective-permute-done.2.rim_ref
  19.5 0.0 copy-start.2
  19.5 4.8 %shard_map.38.b_ref = f32[6,2,32,384]{3,2,1,0:T(8,128)} custom-call(s32[1]{0:T(128)} %bitcast.side_ref, f32[6,2,32,384]{3,2,1,0:T(8,128)} %collective-permute-done.2.rim_ref, f32[12,2,32,384]{3,2,1,0:T(8,128)} %bitcast.19, f32[12,2,1,384]{3,2,1,0:T(1,128)} %broadcast_in_dim.3.pot_ref), custom_call_target="tpu_custom_call" | custom-call | tf_op jit(solution)/shard_map/pallas_call | solution.py:173
  24.3 6.6 %collective-permute-start.3 = (f32[6,2,32,384]{3,2,1,0:T(8,128)}, f32[6,2,32,384]{3,2,1,0:T(8,128)}, u32[]{:S(2)}, u32[]{:S(2)}) collective-permute-start(f32[6,2,32,384]{3,2,1,0:T(8,128)} %shard_map.38.b_ref), channel_id=1, source_target_pairs={{0,480},{32,64},{64,32},{96,128},{128,96},{160,192},{192,160},{224... | collective-permute-start | bytes 1769480 | tf_op jit(solution)/shard_map/ppermute | solution.py:200
  30.9 0.7 pad_add_fusion
  31.6 0.0 copy-done.2
  31.6 1.1 dynamic-slice_bitcast_fusion
  32.7 0.0 collective-permute-done.1.rim_ref
  32.7 4.8 %shard_map.39 = bf16[6,2,32,384]{3,2,1,0:T(8,128)(2,1)} custom-call(s32[2]{0:T(128)} %get-tuple-element.16.side_ref, f32[6,2,32,384]{3,2,1,0:T(8,128)} %collective-permute-done.1.rim_ref, f32[6,2,32,384]{3,2,1,0:T(8,128)} %shard_map.37.a_ref, f32[6,2,32,384]{3,2,1,0:T(8,128)} %shard_map.38.b_ref, f32[6,2,32,384]{3,2,1,0:T(8,128)} %get-tuple-element.10.psi_ref, ...), custom_call_target="tpu_custom_call" | custom-call | tf_op jit(solution)/shard_map/pallas_call | solution.py:186
  37.5 1.9 %collective-permute-done.3.rim_ref = f32[6,2,32,384]{3,2,1,0:T(8,128)} collective-permute-done((f32[6,2,32,384]{3,2,1,0:T(8,128)}, f32[6,2,32,384]{3,2,1,0:T(8,128)}, u32[]{:S(2)}, u32[]{:S(2)}) %collective-permute-start.3) | collective-permute-done | bytes 589856 | tf_op jit(solution)/shard_map/ppermute | solution.py:200
  39.5 4.8 %shard_map.40 = bf16[6,2,32,384]{3,2,1,0:T(8,128)(2,1)} custom-call(s32[2]{0:T(128)} %get-tuple-element.15.side_ref, f32[6,2,32,384]{3,2,1,0:T(8,128)} %collective-permute-done.3.rim_ref, f32[6,2,32,384]{3,2,1,0:T(8,128)} %shard_map.37.a_ref, f32[6,2,32,384]{3,2,1,0:T(8,128)} %shard_map.38.b_ref, f32[6,2,32,384]{3,2,1,0:T(8,128)} %get-tuple-element.9.psi_ref, ...), custom_call_target="tpu_custom_call" | custom-call | tf_op jit(solution)/shard_map/pallas_call | solution.py:186
  44.3 1.2 copy.16
  45.5 0.0 copy-start.3
  45.5 0.5 reshape.26
  46.0 0.1 copy.17
  46.1 0.7 reshape.27
  46.8 0.0 copy-done.3
  46.8 0.2 copy.18
  47.0 0.5 reshape.28
  47.6 0.1 copy.19
  47.6 0.7 reshape.29
  48.3 0.1 maximum_select_fusion
  48.5 48.3 %all_to_all.10 = bf16[32,24,384]{2,1,0:T(8,128)(2,1)S(1)} all-to-all(bf16[32,24,384]{2,1,0:T(8,128)(2,1)S(1)} %maximum_select_fusion), channel_id=1, replica_groups=mesh['dom'=16,'band'=32] {'band'}, dimensions={0} | all-to-all | bytes 1179648 | tf_op jit(solution)/shard_map/all_to_all | solution.py:247
  96.8 1.1 reshape.30
  97.9 0.0 copy-done
  97.9 0.8 fusion
  98.7 0.4 copy.20
  99.0 1.4 reshape.31
  100.4 37.1 %all_to_all.11 = bf16[32,24,384]{2,1,0:T(8,128)(2,1)} all-to-all(bf16[32,24,384]{2,1,0:T(8,128)(2,1)S(1)} %reshape.31), channel_id=1, replica_groups=mesh['dom'=16,'band'=32] {'band'}, dimensions={0} | all-to-all | bytes 1179648 | tf_op jit(solution)/shard_map/all_to_all | solution.py:254
  137.6 2.2 %reshape.32 = bf16[32,32,288]{2,1,0:T(8,128)(2,1)S(1)} reshape(bf16[32,24,384]{2,1,0:T(8,128)(2,1)} %all_to_all.11) | data formatting | bytes 1179648 | tf_op jit(solution)/shard_map/reshape | solution.py:255
  139.8 1.1 copy.21
  141.0 3.5 %reshape.33 = bf16[32,12,2,384]{3,2,1,0:T(2,128)(2,1)} reshape(bf16[32,32,288]{2,1,0:T(8,128)(2,1)} %copy.21) | data formatting | bytes 1179648 | tf_op jit(solution)/shard_map/reshape | solution.py:256
Async XLA Ops:
  0.0 97.9 %copy-start = (bf16[1024,1024]{1,0:T(8,128)(2,1)S(1)}, bf16[1024,1024]{1,0:T(8,128)(2,1)}, u32[]{:S(2)}) copy-start(bf16[1024,1024]{1,0:T(8,128)(2,1)} %param.5) | copy-start | bytes 6291460
  1.7 1.0 copy-start.1
  1.7 9.5 %copy-start.4 = (f32[12,2,384]{2,1,0:T(2,128)S(1)}, f32[12,2,384]{2,1,0:T(2,128)}, u32[]{:S(2)}) copy-start(f32[12,2,384]{2,1,0:T(2,128)} %param.4) | copy-start | bytes 110596
  2.7 9.2 %collective-permute-start = (f32[6,2,32,384]{3,2,1,0:T(8,128)S(1)}, f32[6,2,32,384]{3,2,1,0:T(8,128)}, u32[]{:S(2)}, u32[]{:S(2)}) collective-permute-start(f32[6,2,32,384]{3,2,1,0:T(8,128)S(1)} %get-tuple-element.14), channel_id=1, source_target_pairs={{0,32},{32,0},{64,96},{96,64},{128,160},{160,128},{192,224},{224,1... | collective-permute-start | bytes 1769480 | tf_op jit(solution)/shard_map/ppermute | solution.py:200
  4.6 14.9 %collective-permute-start.2 = (f32[6,2,32,384]{3,2,1,0:T(8,128)S(1)}, f32[6,2,32,384]{3,2,1,0:T(8,128)}, u32[]{:S(2)}, u32[]{:S(2)}) collective-permute-start(f32[6,2,32,384]{3,2,1,0:T(8,128)S(1)} %get-tuple-element.13), channel_id=1, source_target_pairs={{0,480},{32,64},{64,32},{96,128},{128,96},{160,192},{192,160},{224... | collective-permute-start | bytes 1769480 | tf_op jit(solution)/shard_map/ppermute | solution.py:200
  16.5 16.2 %collective-permute-start.1 = (f32[6,2,32,384]{3,2,1,0:T(8,128)}, f32[6,2,32,384]{3,2,1,0:T(8,128)}, u32[]{:S(2)}, u32[]{:S(2)}) collective-permute-start(f32[6,2,32,384]{3,2,1,0:T(8,128)} %shard_map.37.a_ref), channel_id=1, source_target_pairs={{0,32},{32,0},{64,96},{96,64},{128,160},{160,128},{192,224},{224,1... | collective-permute-start | bytes 1769480 | tf_op jit(solution)/shard_map/ppermute | solution.py:200
  19.5 12.1 %copy-start.2 = (f32[32,12,2,384]{3,0,2,1:T(8,128)S(1)}, f32[32,12,2,384]{3,0,2,1:T(8,128)}, u32[]{:S(2)}) copy-start(f32[32,12,2,384]{3,0,2,1:T(8,128)} %copy-done.1) | copy-start | bytes 3538948
  24.3 15.1 %collective-permute-start.3 = (f32[6,2,32,384]{3,2,1,0:T(8,128)}, f32[6,2,32,384]{3,2,1,0:T(8,128)}, u32[]{:S(2)}, u32[]{:S(2)}) collective-permute-start(f32[6,2,32,384]{3,2,1,0:T(8,128)} %shard_map.38.b_ref), channel_id=1, source_target_pairs={{0,480},{32,64},{64,32},{96,128},{128,96},{160,192},{192,160},{224... | collective-permute-start | bytes 1769480 | tf_op jit(solution)/shard_map/ppermute | solution.py:200
  45.5 1.3 copy-start.3
